TPU v7x, 512 devices: a whole 4x4x16 slice. The times are simulated.
512 devices in a mesh: lat: 16 (over y, x), lon: 32 (over z, core).
Axes of the slice: x: 4, y: 4, z: 16, core: 2. Of those that a mesh axis runs over, the one named last changes fastest.
Arguments:
- cotangent: bfloat16 [144, 32, 4096], P(None, 'lat', 'lon'), may hold values from -4.5 to 6.5
- cell_area: float32 [32, 4096], P('lat', 'lon'), may hold values from 0.01 to 4
- reach_count: int32 [16, 32], P('lat', 'lon'), may hold values from 1 to 8, as said below
- weights: bfloat16 [16, 32, 8, 256, 768], P('lat', 'lon'), may hold values from -0.0625 to 0.0625
Outputs:
- tracer_adjoint: float32 [144, 32, 4096], P(None, 'lat', 'lon')
Inputs may be any that keep to these rules, and one draw needn't show every extreme that they name: reach_count[l, n] counts the tiles (l, n), (l, n - 1), ... (column index modulo 32) that the departure regions of tile (l, n) touch; in every draw one whole latitude row of tiles has 8.
All inputs are finite; a program needn't handle non-finite values.
Results may differ from a plain program's by a relative error of at most 0.0027.
Values may be sent and summed in bfloat16 or wider, within the bound.
No kernel may reach another device: no remote copies, remote signals or barrier semaphores. Data moves between devices by JAX's collectives and lax.ppermute only.
A program may use at most 64 MiB of HBM per device.

v0:
```python
import jax
import jax.numpy as jnp
from jax import lax
from jax.sharding import PartitionSpec as P


def shifted(value, axis, by):
    length = lax.axis_size(axis)
    return lax.ppermute(value, axis, [(i, (i + by) % length) for i in range(length)])


def padded_2(block, sides, width):
    for axis, dim in sides:
        count = lax.axis_size(axis)
        forward = [(i, i + 1) for i in range(count - 1)]
        forward.append((count - 1, 0))
        backward = [(target, source) for source, target in forward]
        low = lax.ppermute(
            lax.slice_in_dim(block, block.shape[dim] - width, None, axis=dim), axis, forward
        )
        high = lax.ppermute(lax.slice_in_dim(block, 0, width, axis=dim), axis, backward)
        block = jnp.concatenate([low, block, high], axis=dim)
    return block


def slot_term(flux_flat, count_here, slot_index, weight_panel):
    is_live = count_here[0, 0] > slot_index
    product = jnp.dot(flux_flat, weight_panel, preferred_element_type=jnp.float32)
    return jnp.where(is_live, product, 0.0)


def on_device(cotangent, cell_area, reach_count, weights):
    fields, tile_rows, tile_cols = cotangent.shape
    cell_count = tile_rows * tile_cols
    slot_count = weights.shape[2]
    cot_full = cotangent.astype(jnp.float32)
    weighted = jnp.sum(cot_full * cell_area[None], axis=(1, 2))
    squares = jnp.sum(cell_area * cell_area)
    totals, norm_sq = lax.psum((weighted, squares), ("lat", "lon"))
    factor = totals / norm_sq
    correction = cell_area[None] * factor[:, None, None]
    adjoint_flux = (cot_full - correction).astype(jnp.bfloat16)
    moments = slot_term(adjoint_flux.reshape(fields, cell_count), reach_count, 0, weights[0, 0, 0])
    for slot_index in range(1, slot_count):
        received, received_count = shifted((adjoint_flux, reach_count), "lon", -slot_index)
        moments = moments + slot_term(
            received.reshape(fields, cell_count),
            received_count,
            slot_index,
            weights[0, 0, slot_index],
        )
    moments = moments.reshape(fields, 3, tile_rows, tile_cols)
    mean_adj = moments[:, 0]
    curv_adj = moments[:, 2]
    signs = jnp.array([-3.0, 3.0], jnp.float32)[None, :, None, None]
    edge_pair = moments[:, 1:2] + signs * moments[:, 2:3]
    padded = padded_2(edge_pair, (("lon", 3),), 2)
    left_pad = padded[:, 0]
    right_pad = padded[:, 1]
    near = (
        left_pad[..., 2 : tile_cols + 2]
        + left_pad[..., 1 : tile_cols + 1]
        - right_pad[..., 2 : tile_cols + 2]
        - right_pad[..., 3 : tile_cols + 3]
    )
    far = (
        left_pad[..., 3 : tile_cols + 3]
        + left_pad[..., 0:tile_cols]
        - right_pad[..., 4 : tile_cols + 4]
        - right_pad[..., 1 : tile_cols + 1]
    )
    return mean_adj + 6.0 * curv_adj + 7.0 / 12.0 * near - 1.0 / 12.0 * far + correction


def solution(mesh):
    in_specs = (
        P(None, "lat", "lon"),
        P("lat", "lon"),
        P("lat", "lon"),
        P("lat", "lon", None, None, None),
    )
    out_specs = P(None, "lat", "lon")
    return jax.shard_map(
        on_device, mesh=mesh, in_specs=in_specs, out_specs=out_specs, check_vma=False
    )
```

profile of v0, /device:TPU:1, one launch (start us, length us, event | category | flops | bytes accessed | tf_op | source)
XLA Modules:
  0.0 191.6 jit_solution(6734571853574604118)
XLA Ops:
  0.0 0.0 copy-start
  0.0 13.2 %collective-permute-start.8 = (s32[1,1]{1,0:T(1,128)}, s32[1,1]{1,0:T(1,128)}, u32[]{:S(2)}, u32[]{:S(2)}) collective-permute-start(s32[1,1]{1,0:T(1,128)} %param.7), channel_id=1, source_target_pairs={{0,27},{1,28},{2,29},{3,30},{4,31},{5,0},{6,1},{7,2},{8,3},{9,4},{... | collective-permute-start | bytes 20 | tf_op jit(solution)/shard_map/ppermute | solution.py:9
  13.2 3.1 %collective-permute-start.6 = (s32[1,1]{1,0:T(1,128)}, s32[1,1]{1,0:T(1,128)}, u32[]{:S(2)}, u32[]{:S(2)}) collective-permute-start(s32[1,1]{1,0:T(1,128)} %param.7), channel_id=1, source_target_pairs={{0,28},{1,29},{2,30},{3,31},{4,0},{5,1},{6,2},{7,3},{8,4},{9,5},{1... | collective-permute-start | bytes 20 | tf_op jit(solution)/shard_map/ppermute | solution.py:9
  16.3 4.3 %collective-permute-start.4 = (s32[1,1]{1,0:T(1,128)}, s32[1,1]{1,0:T(1,128)}, u32[]{:S(2)}, u32[]{:S(2)}) collective-permute-start(s32[1,1]{1,0:T(1,128)} %param.7), channel_id=1, source_target_pairs={{0,29},{1,30},{2,31},{3,0},{4,1},{5,2},{6,3},{7,4},{8,5},{9,6},{10... | collective-permute-start | bytes 20 | tf_op jit(solution)/shard_map/ppermute | solution.py:9
  20.6 2.6 %collective-permute-start.2 = (s32[1,1]{1,0:T(1,128)}, s32[1,1]{1,0:T(1,128)}, u32[]{:S(2)}, u32[]{:S(2)}) collective-permute-start(s32[1,1]{1,0:T(1,128)} %param.7), channel_id=1, source_target_pairs={{0,30},{1,31},{2,0},{3,1},{4,2},{5,3},{6,4},{7,5},{8,6},{9,7},{10,... | collective-permute-start | bytes 20 | tf_op jit(solution)/shard_map/ppermute | solution.py:9
  23.2 1.3 multiply_reduce_fusion
  24.5 1.9 fusion.23
  26.5 101.9 %all-reduce = (f32[144]{0:T(256)S(1)}, f32[]{:T(128)}) all-reduce(f32[144]{0:T(256)S(1)} %fusion.23, f32[]{:T(128)} %multiply_reduce_fusion), channel_id=1, replica_groups=mesh['lat'=16,'lon'=32] {'lat','lon'}, use_global_device_ids=true, to_apply=%region_1.0 | all-reduce | flops 145 | bytes 1160 | tf_op jit(solution)/shard_map/psum | solution.py:39
  128.4 0.6 broadcast_divide_fusion
  129.0 1.1 fusion.24
  130.1 0.8 collective-permute-start.1
  131.6 1.2 convolution_select_fusion
  132.9 0.0 collective-permute-done.8
  132.9 1.3 collective-permute-start
  134.8 0.0 collective-permute-done.6
  134.9 2.1 %collective-permute-start.12 = (s32[1,1]{1,0:T(1,128)}, s32[1,1]{1,0:T(1,128)}, u32[]{:S(2)}, u32[]{:S(2)}) collective-permute-start(s32[1,1]{1,0:T(1,128)} %param.7), channel_id=1, source_target_pairs={{0,25},{1,26},{2,27},{3,28},{4,29},{5,30},{6,31},{7,0},{8,1},{9,2}... | collective-permute-start | bytes 20 | tf_op jit(solution)/shard_map/ppermute | solution.py:9
  137.6 0.0 collective-permute-done.4
  137.6 5.8 %collective-permute-start.10 = (s32[1,1]{1,0:T(1,128)}, s32[1,1]{1,0:T(1,128)}, u32[]{:S(2)}, u32[]{:S(2)}) collective-permute-start(s32[1,1]{1,0:T(1,128)} %param.7), channel_id=1, source_target_pairs={{0,26},{1,27},{2,28},{3,29},{4,30},{5,31},{6,0},{7,1},{8,2},{9,3},... | collective-permute-start | bytes 20 | tf_op jit(solution)/shard_map/ppermute | solution.py:9
  144.0 0.0 collective-permute-done.2
  144.0 5.0 %collective-permute-start.13 = (bf16[144,2,128]{2,1,0:T(2,128)(2,1)S(1)}, bf16[144,2,128]{2,1,0:T(2,128)(2,1)S(1)}, u32[]{:S(2)}, u32[]{:S(2)}) collective-permute-start(bf16[144,2,128]{2,1,0:T(2,128)(2,1)S(1)} %fusion.24), channel_id=1, source_target_pairs={{0,25},{1,26},{2,27},{3,28},{4,29},{5,30},{6,31},{7,0},{8,1},{9,2}... | collective-permute-start | bytes 221192 | tf_op jit(solution)/shard_map/ppermute | solution.py:9
  149.6 0.0 collective-permute-done
  149.6 3.3 %collective-permute-start.11 = (bf16[144,2,128]{2,1,0:T(2,128)(2,1)S(1)}, bf16[144,2,128]{2,1,0:T(2,128)(2,1)S(1)}, u32[]{:S(2)}, u32[]{:S(2)}) collective-permute-start(bf16[144,2,128]{2,1,0:T(2,128)(2,1)S(1)} %fusion.24), channel_id=1, source_target_pairs={{0,26},{1,27},{2,28},{3,29},{4,30},{5,31},{6,0},{7,1},{8,2},{9,3},... | collective-permute-start | bytes 221192 | tf_op jit(solution)/shard_map/ppermute | solution.py:9
  153.5 0.0 collective-permute-done.12
  153.5 4.2 %collective-permute-start.9 = (bf16[144,2,128]{2,1,0:T(2,128)(2,1)S(1)}, bf16[144,2,128]{2,1,0:T(2,128)(2,1)S(1)}, u32[]{:S(2)}, u32[]{:S(2)}) collective-permute-start(bf16[144,2,128]{2,1,0:T(2,128)(2,1)S(1)} %fusion.24), channel_id=1, source_target_pairs={{0,27},{1,28},{2,29},{3,30},{4,31},{5,0},{6,1},{7,2},{8,3},{9,4},{... | collective-permute-start | bytes 221192 | tf_op jit(solution)/shard_map/ppermute | solution.py:9
  158.4 0.0 collective-permute-done.10
  158.4 3.0 %collective-permute-start.7 = (bf16[144,2,128]{2,1,0:T(2,128)(2,1)S(1)}, bf16[144,2,128]{2,1,0:T(2,128)(2,1)S(1)}, u32[]{:S(2)}, u32[]{:S(2)}) collective-permute-start(bf16[144,2,128]{2,1,0:T(2,128)(2,1)S(1)} %fusion.24), channel_id=1, source_target_pairs={{0,28},{1,29},{2,30},{3,31},{4,0},{5,1},{6,2},{7,3},{8,4},{9,5},{1... | collective-permute-start | bytes 221192 | tf_op jit(solution)/shard_map/ppermute | solution.py:9
  162.2 0.0 collective-permute-done.1
  162.2 2.6 %collective-permute-start.3 = (bf16[144,2,128]{2,1,0:T(2,128)(2,1)S(1)}, bf16[144,2,128]{2,1,0:T(2,128)(2,1)S(1)}, u32[]{:S(2)}, u32[]{:S(2)}) collective-permute-start(bf16[144,2,128]{2,1,0:T(2,128)(2,1)S(1)} %fusion.24), channel_id=1, source_target_pairs={{0,30},{1,31},{2,0},{3,1},{4,2},{5,3},{6,4},{7,5},{8,6},{9,7},{10,... | collective-permute-start | bytes 221192 | tf_op jit(solution)/shard_map/ppermute | solution.py:9
  164.8 1.2 fusion.12
  166.0 3.2 %collective-permute-done.3 = bf16[144,2,128]{2,1,0:T(2,128)(2,1)S(1)} collective-permute-done((bf16[144,2,128]{2,1,0:T(2,128)(2,1)S(1)}, bf16[144,2,128]{2,1,0:T(2,128)(2,1)S(1)}, u32[]{:S(2)}, u32[]{:S(2)}) %collective-permute-start.3) | collective-permute-done | bytes 73760 | tf_op jit(solution)/shard_map/ppermute | solution.py:9
  169.2 4.5 %collective-permute-start.5 = (bf16[144,2,128]{2,1,0:T(2,128)(2,1)S(1)}, bf16[144,2,128]{2,1,0:T(2,128)(2,1)S(1)}, u32[]{:S(2)}, u32[]{:S(2)}) collective-permute-start(bf16[144,2,128]{2,1,0:T(2,128)(2,1)S(1)} %fusion.24), channel_id=1, source_target_pairs={{0,29},{1,30},{2,31},{3,0},{4,1},{5,2},{6,3},{7,4},{8,5},{9,6},{10... | collective-permute-start | bytes 221192 | tf_op jit(solution)/shard_map/ppermute | solution.py:9
  173.7 1.2 fusion.10
  174.9 2.0 %collective-permute-done.5 = bf16[144,2,128]{2,1,0:T(2,128)(2,1)S(1)} collective-permute-done((bf16[144,2,128]{2,1,0:T(2,128)(2,1)S(1)}, bf16[144,2,128]{2,1,0:T(2,128)(2,1)S(1)}, u32[]{:S(2)}, u32[]{:S(2)}) %collective-permute-start.5) | collective-permute-done | bytes 73760 | tf_op jit(solution)/shard_map/ppermute | solution.py:9
  177.0 1.2 fusion.8
  178.2 0.0 collective-permute-done.7
  178.2 0.0 copy-done
  178.2 0.2 fusion.6
  178.4 0.0 collective-permute-done.9
  178.5 0.2 fusion.4
  178.7 0.0 collective-permute-done.11
  178.7 0.0 copy-start.2
  178.7 0.2 fusion.2
  178.9 0.0 collective-permute-done.13
  178.9 1.1 select_add_fusion
  180.0 0.0 copy-start.1
  180.0 1.2 reshape.54
  181.3 0.1 slice_bitcast_fusion.2
  181.4 0.0 copy-done.2
  181.4 0.2 multiply_add_fusion
  181.6 0.4 fusion.50
  181.9 0.0 collective-permute-start.14
  182.0 0.5 collective-permute-start.15
  182.5 3.2 %collective-permute-done.14 = f32[144,2,2,2]{3,2,0,1:T(2,128)S(1)} collective-permute-done((f32[144,2,2,2]{3,2,0,1:T(2,128)S(1)}, f32[144,2,2,2]{3,2,0,1:T(2,128)S(1)}, u32[]{:S(2)}, u32[]{:S(2)}) %collective-permute-start.14) | collective-permute-done | bytes 4640 | tf_op jit(solution)/shard_map/ppermute | solution.py:18
  185.6 2.8 %collective-permute-done.15 = f32[144,2,2,2]{3,2,0,1:T(2,128)S(1)} collective-permute-done((f32[144,2,2,2]{3,2,0,1:T(2,128)S(1)}, f32[144,2,2,2]{3,2,0,1:T(2,128)S(1)}, u32[]{:S(2)}, u32[]{:S(2)}) %collective-permute-start.15) | collective-permute-done | bytes 4640 | tf_op jit(solution)/shard_map/ppermute | solution.py:21
  188.4 1.0 pad_maximum_fusion
  189.4 0.2 slice_bitcast_fusion.1
  189.6 0.0 copy-done.1
  189.6 1.9 %multiply_add_fusion.1 = f32[144,2,128]{2,1,0:T(2,128)} fusion(f32[144,2,132]{2,1,0:T(2,128)S(1)} %get-tuple-element.8, f32[144,2,132]{2,1,0:T(2,128)S(1)} %get-tuple-element.7, f32[144,3,2,128]{3,2,1,0:T(2,128)S(1)} %reshape.54, f32[2,128]{1,0:T(2,128)S(1)} %copy-done.1, f32[144]{0:T(256)S(1)} %broadcast_divide_fusion), kind=kLoop, calls=%fused_computation.29 | loop fusion | flops 516096 | bytes 1623616 | tf_op jit(solution)/shard_map/add | solution.py:72
Async XLA Ops:
  0.0 178.2 %copy-start = (bf16[1,1,8,256,768]{4,3,2,1,0:T(8,128)(2,1)S(1)}, bf16[1,1,8,256,768]{4,3,2,1,0:T(8,128)(2,1)}, u32[]{:S(2)}) copy-start(bf16[1,1,8,256,768]{4,3,2,1,0:T(8,128)(2,1)} %param.8) | copy-start | bytes 9437188
  0.0 132.9 %collective-permute-start.8 = (s32[1,1]{1,0:T(1,128)}, s32[1,1]{1,0:T(1,128)}, u32[]{:S(2)}, u32[]{:S(2)}) collective-permute-start(s32[1,1]{1,0:T(1,128)} %param.7), channel_id=1, source_target_pairs={{0,27},{1,28},{2,29},{3,30},{4,31},{5,0},{6,1},{7,2},{8,3},{9,4},{... | collective-permute-start | bytes 20 | tf_op jit(solution)/shard_map/ppermute | solution.py:9
  13.2 121.6 %collective-permute-start.6 = (s32[1,1]{1,0:T(1,128)}, s32[1,1]{1,0:T(1,128)}, u32[]{:S(2)}, u32[]{:S(2)}) collective-permute-start(s32[1,1]{1,0:T(1,128)} %param.7), channel_id=1, source_target_pairs={{0,28},{1,29},{2,30},{3,31},{4,0},{5,1},{6,2},{7,3},{8,4},{9,5},{1... | collective-permute-start | bytes 20 | tf_op jit(solution)/shard_map/ppermute | solution.py:9
  16.3 121.3 %collective-permute-start.4 = (s32[1,1]{1,0:T(1,128)}, s32[1,1]{1,0:T(1,128)}, u32[]{:S(2)}, u32[]{:S(2)}) collective-permute-start(s32[1,1]{1,0:T(1,128)} %param.7), channel_id=1, source_target_pairs={{0,29},{1,30},{2,31},{3,0},{4,1},{5,2},{6,3},{7,4},{8,5},{9,6},{10... | collective-permute-start | bytes 20 | tf_op jit(solution)/shard_map/ppermute | solution.py:9
  20.6 123.4 %collective-permute-start.2 = (s32[1,1]{1,0:T(1,128)}, s32[1,1]{1,0:T(1,128)}, u32[]{:S(2)}, u32[]{:S(2)}) collective-permute-start(s32[1,1]{1,0:T(1,128)} %param.7), channel_id=1, source_target_pairs={{0,30},{1,31},{2,0},{3,1},{4,2},{5,3},{6,4},{7,5},{8,6},{9,7},{10,... | collective-permute-start | bytes 20 | tf_op jit(solution)/shard_map/ppermute | solution.py:9
  130.1 32.0 %collective-permute-start.1 = (bf16[144,2,128]{2,1,0:T(2,128)(2,1)S(1)}, bf16[144,2,128]{2,1,0:T(2,128)(2,1)S(1)}, u32[]{:S(2)}, u32[]{:S(2)}) collective-permute-start(bf16[144,2,128]{2,1,0:T(2,128)(2,1)S(1)} %fusion.24), channel_id=1, source_target_pairs={{0,31},{1,0},{2,1},{3,2},{4,3},{5,4},{6,5},{7,6},{8,7},{9,8},{10,9... | collective-permute-start | bytes 221192 | tf_op jit(solution)/shard_map/ppermute | solution.py:9
  132.9 16.8 %collective-permute-start = (s32[1,1]{1,0:T(1,128)}, s32[1,1]{1,0:T(1,128)}, u32[]{:S(2)}, u32[]{:S(2)}) collective-permute-start(s32[1,1]{1,0:T(1,128)} %param.7), channel_id=1, source_target_pairs={{0,31},{1,0},{2,1},{3,2},{4,3},{5,4},{6,5},{7,6},{8,7},{9,8},{10,9... | collective-permute-start | bytes 20 | tf_op jit(solution)/shard_map/ppermute | solution.py:9
  134.9 18.7 %collective-permute-start.12 = (s32[1,1]{1,0:T(1,128)}, s32[1,1]{1,0:T(1,128)}, u32[]{:S(2)}, u32[]{:S(2)}) collective-permute-start(s32[1,1]{1,0:T(1,128)} %param.7), channel_id=1, source_target_pairs={{0,25},{1,26},{2,27},{3,28},{4,29},{5,30},{6,31},{7,0},{8,1},{9,2}... | collective-permute-start | bytes 20 | tf_op jit(solution)/shard_map/ppermute | solution.py:9
  137.6 20.8 %collective-permute-start.10 = (s32[1,1]{1,0:T(1,128)}, s32[1,1]{1,0:T(1,128)}, u32[]{:S(2)}, u32[]{:S(2)}) collective-permute-start(s32[1,1]{1,0:T(1,128)} %param.7), channel_id=1, source_target_pairs={{0,26},{1,27},{2,28},{3,29},{4,30},{5,31},{6,0},{7,1},{8,2},{9,3},... | collective-permute-start | bytes 20 | tf_op jit(solution)/shard_map/ppermute | solution.py:9
  144.0 35.0 %collective-permute-start.13 = (bf16[144,2,128]{2,1,0:T(2,128)(2,1)S(1)}, bf16[144,2,128]{2,1,0:T(2,128)(2,1)S(1)}, u32[]{:S(2)}, u32[]{:S(2)}) collective-permute-start(bf16[144,2,128]{2,1,0:T(2,128)(2,1)S(1)} %fusion.24), channel_id=1, source_target_pairs={{0,25},{1,26},{2,27},{3,28},{4,29},{5,30},{6,31},{7,0},{8,1},{9,2}... | collective-permute-start | bytes 221192 | tf_op jit(solution)/shard_map/ppermute | solution.py:9
  149.6 29.1 %collective-permute-start.11 = (bf16[144,2,128]{2,1,0:T(2,128)(2,1)S(1)}, bf16[144,2,128]{2,1,0:T(2,128)(2,1)S(1)}, u32[]{:S(2)}, u32[]{:S(2)}) collective-permute-start(bf16[144,2,128]{2,1,0:T(2,128)(2,1)S(1)} %fusion.24), channel_id=1, source_target_pairs={{0,26},{1,27},{2,28},{3,29},{4,30},{5,31},{6,0},{7,1},{8,2},{9,3},... | collective-permute-start | bytes 221192 | tf_op jit(solution)/shard_map/ppermute | solution.py:9
  153.5 24.9 %collective-permute-start.9 = (bf16[144,2,128]{2,1,0:T(2,128)(2,1)S(1)}, bf16[144,2,128]{2,1,0:T(2,128)(2,1)S(1)}, u32[]{:S(2)}, u32[]{:S(2)}) collective-permute-start(bf16[144,2,128]{2,1,0:T(2,128)(2,1)S(1)} %fusion.24), channel_id=1, source_target_pairs={{0,27},{1,28},{2,29},{3,30},{4,31},{5,0},{6,1},{7,2},{8,3},{9,4},{... | collective-permute-start | bytes 221192 | tf_op jit(solution)/shard_map/ppermute | solution.py:9
  158.4 19.8 %collective-permute-start.7 = (bf16[144,2,128]{2,1,0:T(2,128)(2,1)S(1)}, bf16[144,2,128]{2,1,0:T(2,128)(2,1)S(1)}, u32[]{:S(2)}, u32[]{:S(2)}) collective-permute-start(bf16[144,2,128]{2,1,0:T(2,128)(2,1)S(1)} %fusion.24), channel_id=1, source_target_pairs={{0,28},{1,29},{2,30},{3,31},{4,0},{5,1},{6,2},{7,3},{8,4},{9,5},{1... | collective-permute-start | bytes 221192 | tf_op jit(solution)/shard_map/ppermute | solution.py:9
  162.2 7.1 %collective-permute-start.3 = (bf16[144,2,128]{2,1,0:T(2,128)(2,1)S(1)}, bf16[144,2,128]{2,1,0:T(2,128)(2,1)S(1)}, u32[]{:S(2)}, u32[]{:S(2)}) collective-permute-start(bf16[144,2,128]{2,1,0:T(2,128)(2,1)S(1)} %fusion.24), channel_id=1, source_target_pairs={{0,30},{1,31},{2,0},{3,1},{4,2},{5,3},{6,4},{7,5},{8,6},{9,7},{10,... | collective-permute-start | bytes 221192 | tf_op jit(solution)/shard_map/ppermute | solution.py:9
  169.2 7.7 %collective-permute-start.5 = (bf16[144,2,128]{2,1,0:T(2,128)(2,1)S(1)}, bf16[144,2,128]{2,1,0:T(2,128)(2,1)S(1)}, u32[]{:S(2)}, u32[]{:S(2)}) collective-permute-start(bf16[144,2,128]{2,1,0:T(2,128)(2,1)S(1)} %fusion.24), channel_id=1, source_target_pairs={{0,29},{1,30},{2,31},{3,0},{4,1},{5,2},{6,3},{7,4},{8,5},{9,6},{10... | collective-permute-start | bytes 221192 | tf_op jit(solution)/shard_map/ppermute | solution.py:9
  178.7 2.7 %copy-start.2 = (f32[2]{0:T(128)S(1)}, f32[2]{0:T(128)}, u32[]{:S(2)}) copy-start(f32[2]{0:T(128)} %constant.34.clone) | copy-start | bytes 28
  180.0 9.6 %copy-start.1 = (f32[2,128]{1,0:T(2,128)S(1)}, f32[2,128]{1,0:T(2,128)}, u32[]{:S(2)}) copy-start(f32[2,128]{1,0:T(2,128)} %param.6) | copy-start | bytes 3076
  181.9 3.7 %collective-permute-start.14 = (f32[144,2,2,2]{3,2,0,1:T(2,128)S(1)}, f32[144,2,2,2]{3,2,0,1:T(2,128)S(1)}, u32[]{:S(2)}, u32[]{:S(2)}) collective-permute-start(f32[144,2,2,2]{3,2,0,1:T(2,128)S(1)} %get-tuple-element.11), channel_id=1, source_target_pairs={{0,1},{1,2},{2,3},{3,4},{4,5},{5,6},{6,7},{7,8},{8,9},{9,10},{10,1... | collective-permute-start | bytes 13832 | tf_op jit(solution)/shard_map/ppermute | solution.py:18
  182.0 6.5 %collective-permute-start.15 = (f32[144,2,2,2]{3,2,0,1:T(2,128)S(1)}, f32[144,2,2,2]{3,2,0,1:T(2,128)S(1)}, u32[]{:S(2)}, u32[]{:S(2)}) collective-permute-start(f32[144,2,2,2]{3,2,0,1:T(2,128)S(1)} %get-tuple-element.12), channel_id=1, source_target_pairs={{1,0},{2,1},{3,2},{4,3},{5,4},{6,5},{7,6},{8,7},{9,8},{10,9},{11,1... | collective-permute-start | bytes 13832 | tf_op jit(solution)/shard_map/ppermute | solution.py:21
where the time goes:
time: 192 us
  blocking collectives  102 us (53%)
  starting transfers between devices  56.4 us (29%)
  waiting for transfers between devices  11.3 us (6%)
  other arithmetic  8.05 us (4%)
  matrix products  6.64 us (3%)
  between operations  5.42 us (3%)
  local copies, waits for them, and re-layouts  1.94 us (1%)
    psum x1, blocking collectives, on_device(): totals, norm_sq = lax.psum((weighted, squares), ('lat', 'lon'))  102 us
    ppermute x14, starting transfers between devices, shifted(): lax.ppermute(value, axis, [(i, (i + by) % length) for i in range(length)])  55.8 us
    dot_general x8, matrix products, slot_term(): jnp.dot(flux_flat, weight_panel, preferred_element_type=jnp.float32)  6.64 us
    ppermute x14, waiting for transfers between devices, shifted(): lax.ppermute(value, axis, [(i, (i + by) % length) for i in range(length)])  5.31 us
  transfers between devices with their start and end apart: 16, of which 4 were waited for; matrix products, arithmetic and copies ran while one was open for 5% of the time, Pallas kernels for 0%

commit v1 on v0

--- a/solution.py
+++ b/solution.py
@@ -7,6 +7,16 @@
 def shifted(value, axis, by):
     length = lax.axis_size(axis)
     return lax.ppermute(value, axis, [(i, (i + by) % length) for i in range(length)])
+
+
+def butterfly_sum(value, axes):
+    for axis in axes:
+        length = lax.axis_size(axis)
+        step = 1
+        while step < length:
+            value = value + lax.ppermute(value, axis, [(i, i ^ step) for i in range(length)])
+            step *= 2
+    return value
 
 
 def padded_2(block, sides, width):
@@ -23,10 +33,12 @@
     return block
 
 
-def slot_term(flux_flat, count_here, slot_index, weight_panel):
-    is_live = count_here[0, 0] > slot_index
-    product = jnp.dot(flux_flat, weight_panel, preferred_element_type=jnp.float32)
-    return jnp.where(is_live, product, 0.0)
+def split_bf16(value):
+    high = lax.reduce_precision(value, exponent_bits=8, mantissa_bits=7)
+    rest = value - high
+    middle = lax.reduce_precision(rest, exponent_bits=8, mantissa_bits=7)
+    low = rest - middle
+    return [part.astype(jnp.bfloat16) for part in (high, middle, low)]
 
 
 def on_device(cotangent, cell_area, reach_count, weights):
@@ -36,20 +48,23 @@
     cot_full = cotangent.astype(jnp.float32)
     weighted = jnp.sum(cot_full * cell_area[None], axis=(1, 2))
     squares = jnp.sum(cell_area * cell_area)
-    totals, norm_sq = lax.psum((weighted, squares), ("lat", "lon"))
-    factor = totals / norm_sq
-    correction = cell_area[None] * factor[:, None, None]
-    adjoint_flux = (cot_full - correction).astype(jnp.bfloat16)
-    moments = slot_term(adjoint_flux.reshape(fields, cell_count), reach_count, 0, weights[0, 0, 0])
-    for slot_index in range(1, slot_count):
-        received, received_count = shifted((adjoint_flux, reach_count), "lon", -slot_index)
-        moments = moments + slot_term(
-            received.reshape(fields, cell_count),
-            received_count,
-            slot_index,
-            weights[0, 0, slot_index],
-        )
-    moments = moments.reshape(fields, 3, tile_rows, tile_cols)
+    stats = butterfly_sum(jnp.concatenate([weighted, squares[None]]), ("lat", "lon"))
+    factor = stats[:fields] / stats[fields]
+
+    area_parts = split_bf16(cell_area.reshape(1, cell_count))
+    payload = jnp.concatenate([cotangent.reshape(fields, cell_count)] + area_parts, axis=0)
+    count_here = reach_count[0, 0]
+    tiles = []
+    for slot_index in range(slot_count):
+        live = jnp.where(count_here > slot_index, payload, jnp.zeros_like(payload))
+        tiles.append(live if slot_index == 0 else shifted(live, "lon", -slot_index))
+    stacked = jnp.stack(tiles)
+    moments = lax.dot_general(
+        stacked, weights[0, 0], (((0, 2), (0, 1)), ((), ())), preferred_element_type=jnp.float32
+    )
+    area_moments = moments[fields] + moments[fields + 1] + moments[fields + 2]
+    moments = jnp.concatenate([moments[:fields], area_moments[None]], axis=0)
+    moments = moments.reshape(fields + 1, 3, tile_rows, tile_cols)
     mean_adj = moments[:, 0]
     curv_adj = moments[:, 2]
     signs = jnp.array([-3.0, 3.0], jnp.float32)[None, :, None, None]
@@ -69,7 +84,8 @@
         - right_pad[..., 4 : tile_cols + 4]
         - right_pad[..., 1 : tile_cols + 1]
     )
-    return mean_adj + 6.0 * curv_adj + 7.0 / 12.0 * near - 1.0 / 12.0 * far + correction
+    stencil = mean_adj + 6.0 * curv_adj + 7.0 / 12.0 * near - 1.0 / 12.0 * far
+    return stencil[:fields] + factor[:, None, None] * (cell_area[None] - stencil[fields][None])
 
 
 def solution(mesh):

time: 192 us -> 122 us (0.64)
  blocking collectives: 102 us -> 0 us
  starting transfers between devices: 56.4 us -> 73 us
  waiting for transfers between devices: 11.3 us -> 25.8 us
  local copies, waits for them, and re-layouts: 1.94 us -> 8.59 us
  matrix products: 6.64 us -> 0.66 us
  between operations: 5.42 us -> 1.04 us
  other arithmetic: 8.05 us -> 12 us
    psum x1 -> x0, blocking collectives: 102 us -> none  [on_device(): totals, norm_sq = lax.psum((weighted, squares), ('lat', 'lon'))]
    ppermute x0 -> x9, starting transfers between devices: none -> 42.9 us  [butterfly_sum(): lax.ppermute(value, axis, [(i, i ^ step) for i in range(length)])]
    ppermute x14 -> x7, starting transfers between devices: 55.8 us -> 28.3 us  [shifted(): lax.ppermute(value, axis, [(i, (i + by) % length) for i in range(length)])]
    ppermute x0 -> x9, waiting for transfers between devices: none -> 13.3 us  [butterfly_sum(): lax.ppermute(value, axis, [(i, i ^ step) for i in range(length)])]
    dot_general x8 -> x1, matrix products: 6.64 us -> 0.66 us  [on_device(): lax.dot_general(stacked, weights[0, 0], (((0, 2), (0, 1)), ((), ())), pre...]
    unnamed x6 -> x15, local copies, waits for them, and re-layouts: 0.01 us -> 3.62 us
    ppermute x14 -> x7, waiting for transfers between devices: 5.31 us -> 8.72 us  [shifted(): lax.ppermute(value, axis, [(i, (i + by) % length) for i in range(length)])]
    ppermute x1, waiting for transfers between devices: 3.16 us -> 0.01 us  [padded_2(): lax.ppermute(lax.slice_in_dim(block, block.shape[dim] - width, None, axis...]
  transfers between devices with their start and end apart: 16 -> 18, of which waited for: 4 -> 8; matrix products, arithmetic and copies ran while one was open for 5% -> 7% of each run, Pallas kernels for 0% -> 0%
where the time goes in v1:
time: 122 us; the launch traced here: 121 us
  starting transfers between devices  73 us (60%)
  waiting for transfers between devices  25.8 us (21%)
  other arithmetic  12 us (10%)
  local copies, waits for them, and re-layouts  8.59 us (7%)
    ppermute x9, starting transfers between devices, butterfly_sum(): lax.ppermute(value, axis, [(i, i ^ step) for i in range(length)])  42.9 us
    ppermute x7, starting transfers between devices, shifted(): lax.ppermute(value, axis, [(i, (i + by) % length) for i in range(length)])  28.3 us
    ppermute x9, waiting for transfers between devices, butterfly_sum(): lax.ppermute(value, axis, [(i, i ^ step) for i in range(length)])  13.3 us
    ppermute x7, waiting for transfers between devices, shifted(): lax.ppermute(value, axis, [(i, (i + by) % length) for i in range(length)])  8.72 us
    ppermute x1, waiting for transfers between devices, padded_2(): lax.ppermute(lax.slice_in_dim(block, 0, width, axis=dim), axis, backward)  3.73 us
    unnamed x15, local copies, waits for them, and re-layouts  3.62 us
  transfers between devices with their start and end apart: 18, of which 8 were waited for; matrix products, arithmetic and copies ran while one was open for 7% of the time, Pallas kernels for 0%

profile of v1, /device:TPU:1, one launch (start us, length us, event | category | flops | bytes accessed | tf_op | source)
XLA Modules:
  0.0 121.1 jit_solution(15888788261839393324)
XLA Ops:
  0.0 1.4 %multiply_reduce_fusion.1 = f32[]{:T(128)} fusion(f32[2,128]{1,0:T(2,128)} %param.6), kind=kLoop, calls=%fused_computation.58 | loop fusion | flops 511 | bytes 1028 | tf_op jit(solution)/shard_map/reduce_sum | solution.py:50
  1.4 1.9 %multiply_reduce_fusion = f32[144]{0:T(256)S(1)} fusion(bf16[144,2,128]{2,1,0:T(2,128)(2,1)} %param.5, f32[2,128]{1,0:T(2,128)} %param.6), kind=kLoop, calls=%fused_computation.28 | loop fusion | flops 110448 | bytes 75328 | tf_op jit(solution)/shard_map/reduce_sum | solution.py:49
  3.4 0.7 pad_maximum_fusion.3
  4.1 3.9 %collective-permute-start.9 = (f32[145]{0:T(256)S(1)}, f32[145]{0:T(256)S(1)}, u32[]{:S(2)}, u32[]{:S(2)}) collective-permute-start(f32[145]{0:T(256)S(1)} %pad_maximum_fusion.3), channel_id=1, source_target_pairs={{0,32},{32,0},{64,96},{96,64},{128,160},{160,128},{192,224},{224,1... | collective-permute-start | bytes 1748 | tf_op jit(solution)/shard_map/ppermute | solution.py:17
  8.0 0.9 collective-permute-done.9
  9.0 0.7 fusion.19
  9.7 4.9 %collective-permute-start.10 = (f32[145]{0:T(256)S(1)}, f32[145]{0:T(256)S(1)}, u32[]{:S(2)}, u32[]{:S(2)}) collective-permute-start(f32[145]{0:T(256)S(1)} %fusion.19), channel_id=1, source_target_pairs={{0,64},{32,96},{64,0},{96,32},{128,192},{160,224},{192,128},{224,1... | collective-permute-start | bytes 1748 | tf_op jit(solution)/shard_map/ppermute | solution.py:17
  14.6 0.9 collective-permute-done.10
  15.5 3.4 %collective-permute-start.11 = (f32[145]{0:T(256)S(1)}, f32[145]{0:T(256)S(1)}, u32[]{:S(2)}, u32[]{:S(2)}) collective-permute-start(f32[145]{0:T(256)S(1)} %add.70), channel_id=1, source_target_pairs={{0,128},{32,160},{64,192},{96,224},{128,0},{160,32},{192,64},{224,... | collective-permute-start | bytes 1748 | tf_op jit(solution)/shard_map/ppermute | solution.py:17
  18.9 0.9 collective-permute-done.11
  19.9 5.0 %collective-permute-start.12 = (f32[145]{0:T(256)S(1)}, f32[145]{0:T(256)S(1)}, u32[]{:S(2)}, u32[]{:S(2)}) collective-permute-start(f32[145]{0:T(256)S(1)} %add.71), channel_id=1, source_target_pairs={{0,256},{32,288},{64,320},{96,352},{128,384},{160,416},{192,448},{... | collective-permute-start | bytes 1748 | tf_op jit(solution)/shard_map/ppermute | solution.py:17
  24.9 0.9 collective-permute-done.12
  25.8 12.6 %collective-permute-start.13 = (f32[145]{0:T(256)S(1)}, f32[145]{0:T(256)S(1)}, u32[]{:S(2)}, u32[]{:S(2)}) collective-permute-start(f32[145]{0:T(256)S(1)} %add.72), channel_id=1, source_target_pairs={{0,1},{1,0},{2,3},{3,2},{4,5},{5,4},{6,7},{7,6},{8,9},{9,8},{10,11... | collective-permute-start | bytes 1748 | tf_op jit(solution)/shard_map/ppermute | solution.py:17
  38.4 0.7 reduce-precision_convert_fusion.1
  39.7 0.9 copy.14
  40.6 0.0 collective-permute-done.13
  40.7 1.9 %collective-permute-start.14 = (f32[145]{0:T(256)S(1)}, f32[145]{0:T(256)S(1)}, u32[]{:S(2)}, u32[]{:S(2)}) collective-permute-start(f32[145]{0:T(256)S(1)} %add.73), channel_id=1, source_target_pairs={{0,2},{1,3},{2,0},{3,1},{4,6},{5,7},{6,4},{7,5},{8,10},{9,11},{10,... | collective-permute-start | bytes 1748 | tf_op jit(solution)/shard_map/ppermute | solution.py:17
  42.6 0.0 collective-permute-start
  42.6 2.3 %collective-permute-done.14 = f32[145]{0:T(256)S(1)} collective-permute-done((f32[145]{0:T(256)S(1)}, f32[145]{0:T(256)S(1)}, u32[]{:S(2)}, u32[]{:S(2)}) %collective-permute-start.14) | collective-permute-done | bytes 612 | tf_op jit(solution)/shard_map/ppermute | solution.py:17
  45.0 1.9 %collective-permute-start.15 = (f32[145]{0:T(256)S(1)}, f32[145]{0:T(256)S(1)}, u32[]{:S(2)}, u32[]{:S(2)}) collective-permute-start(f32[145]{0:T(256)S(1)} %add.74), channel_id=1, source_target_pairs={{0,4},{1,5},{2,6},{3,7},{4,0},{5,1},{6,2},{7,3},{8,12},{9,13},{10,... | collective-permute-start | bytes 1748 | tf_op jit(solution)/shard_map/ppermute | solution.py:17
  46.9 0.7 broadcast_select_fusion
  47.6 6.9 %collective-permute-start.1 = (bf16[147,256]{1,0:T(8,128)(2,1)}, bf16[147,256]{1,0:T(8,128)(2,1)}, u32[]{:S(2)}, u32[]{:S(2)}) collective-permute-start(bf16[147,256]{1,0:T(8,128)(2,1)} %get-tuple-element.12), channel_id=1, source_target_pairs={{0,30},{1,31},{2,0},{3,1},{4,2},{5,3},{6,4},{7,5},{8,6},{9,7},{10,... | collective-permute-start | bytes 225800 | tf_op jit(solution)/shard_map/ppermute | solution.py:9
  54.5 4.2 %collective-permute-start.2 = (bf16[147,256]{1,0:T(8,128)(2,1)S(1)}, bf16[147,256]{1,0:T(8,128)(2,1)}, u32[]{:S(2)}, u32[]{:S(2)}) collective-permute-start(bf16[147,256]{1,0:T(8,128)(2,1)S(1)} %get-tuple-element.13), channel_id=1, source_target_pairs={{0,29},{1,30},{2,31},{3,0},{4,1},{5,2},{6,3},{7,4},{8,5},{9,6},{10... | collective-permute-start | bytes 225800 | tf_op jit(solution)/shard_map/ppermute | solution.py:9
  58.8 0.0 collective-permute-done.15
  58.8 3.6 %collective-permute-start.16 = (f32[145]{0:T(256)S(1)}, f32[145]{0:T(256)S(1)}, u32[]{:S(2)}, u32[]{:S(2)}) collective-permute-start(f32[145]{0:T(256)S(1)} %add.75), channel_id=1, source_target_pairs={{0,8},{1,9},{2,10},{3,11},{4,12},{5,13},{6,14},{7,15},{8,0},{9,1},... | collective-permute-start | bytes 1748 | tf_op jit(solution)/shard_map/ppermute | solution.py:17
  62.3 0.7 broadcast_select_fusion.1
  63.1 4.7 %collective-permute-start.3 = (bf16[147,256]{1,0:T(8,128)(2,1)}, bf16[147,256]{1,0:T(8,128)(2,1)}, u32[]{:S(2)}, u32[]{:S(2)}) collective-permute-start(bf16[147,256]{1,0:T(8,128)(2,1)} %get-tuple-element.15), channel_id=1, source_target_pairs={{0,28},{1,29},{2,30},{3,31},{4,0},{5,1},{6,2},{7,3},{8,4},{9,5},{1... | collective-permute-start | bytes 225800 | tf_op jit(solution)/shard_map/ppermute | solution.py:9
  67.8 0.9 concatenate.34
  68.7 0.0 collective-permute-done.16
  68.8 5.8 %collective-permute-start.17 = (f32[145]{0:T(256)S(1)}, f32[145]{0:T(256)S(1)}, u32[]{:S(2)}, u32[]{:S(2)}) collective-permute-start(f32[145]{0:T(256)S(1)} %add.76), channel_id=1, source_target_pairs={{0,16},{1,17},{2,18},{3,19},{4,20},{5,21},{6,22},{7,23},{8,24},{9,... | collective-permute-start | bytes 1748 | tf_op jit(solution)/shard_map/ppermute | solution.py:17
  74.6 7.2 %collective-permute-done.17 = f32[145]{0:T(256)S(1)} collective-permute-done((f32[145]{0:T(256)S(1)}, f32[145]{0:T(256)S(1)}, u32[]{:S(2)}, u32[]{:S(2)}) %collective-permute-start.17) | collective-permute-done | bytes 612 | tf_op jit(solution)/shard_map/ppermute | solution.py:17
  81.8 3.9 %collective-permute-start.4 = (bf16[147,256]{1,0:T(8,128)(2,1)}, bf16[147,256]{1,0:T(8,128)(2,1)S(1)}, u32[]{:S(2)}, u32[]{:S(2)}) collective-permute-start(bf16[147,256]{1,0:T(8,128)(2,1)} %get-tuple-element.16), channel_id=1, source_target_pairs={{0,27},{1,28},{2,29},{3,30},{4,31},{5,0},{6,1},{7,2},{8,3},{9,4},{... | collective-permute-start | bytes 225800 | tf_op jit(solution)/shard_map/ppermute | solution.py:9
  85.8 0.7 slice.91
  86.4 0.0 collective-permute-done
  86.4 4.7 %collective-permute-start.5 = (bf16[147,256]{1,0:T(8,128)(2,1)}, bf16[147,256]{1,0:T(8,128)(2,1)S(1)}, u32[]{:S(2)}, u32[]{:S(2)}) collective-permute-start(bf16[147,256]{1,0:T(8,128)(2,1)} %get-tuple-element.14), channel_id=1, source_target_pairs={{0,26},{1,27},{2,28},{3,29},{4,30},{5,31},{6,0},{7,1},{8,2},{9,3},... | collective-permute-start | bytes 225800 | tf_op jit(solution)/shard_map/ppermute | solution.py:9
  91.1 0.0 collective-permute-done.1
  91.1 3.7 %collective-permute-start.6 = (bf16[147,256]{1,0:T(8,128)(2,1)S(1)}, bf16[147,256]{1,0:T(8,128)(2,1)S(1)}, u32[]{:S(2)}, u32[]{:S(2)}) collective-permute-start(bf16[147,256]{1,0:T(8,128)(2,1)S(1)} %get-tuple-element.11), channel_id=1, source_target_pairs={{0,25},{1,26},{2,27},{3,28},{4,29},{5,30},{6,31},{7,0},{8,1},{9,2}... | collective-permute-start | bytes 225800 | tf_op jit(solution)/shard_map/ppermute | solution.py:9
  94.9 0.9 bitcast_dynamic-update-slice_fusion.5
  95.8 0.0 collective-permute-done.2
  95.8 0.9 bitcast_dynamic-update-slice_fusion.4
  96.7 0.0 collective-permute-done.3
  96.7 0.9 bitcast_dynamic-update-slice_fusion.3
  97.6 0.0 collective-permute-done.4
  97.6 0.0 collective-permute-done.5
  97.6 8.7 %collective-permute-done.6 = bf16[147,256]{1,0:T(8,128)(2,1)S(1)} collective-permute-done((bf16[147,256]{1,0:T(8,128)(2,1)S(1)}, bf16[147,256]{1,0:T(8,128)(2,1)S(1)}, u32[]{:S(2)}, u32[]{:S(2)}) %collective-permute-start.6) | collective-permute-done | bytes 75296 | tf_op jit(solution)/shard_map/ppermute | solution.py:9
  106.4 0.0 copy-done
  106.4 0.0 copy-start.3
  106.4 0.7 fusion.2
  107.1 0.8 slice.93
  107.9 2.0 %concatenate.40 = f32[144,3,2,128]{3,2,1,0:T(2,128)} reshape(f32[144,768]{1,0:T(8,128)} %slice.93) | data formatting | bytes 884736 | tf_op jit(solution)/shard_map/concatenate | solution.py:66
  109.8 1.2 fusion.11
  111.0 0.0 copy-start.2
  111.1 0.2 multiply_add_fusion
  111.2 0.4 fusion.17
  111.6 0.0 collective-permute-start.8
  111.6 1.7 %collective-permute-start.7 = (f32[145,2,2,2]{3,2,0,1:T(2,128)S(1)}, f32[145,2,2,2]{3,2,0,1:T(2,128)S(1)}, u32[]{:S(2)}, u32[]{:S(2)}) collective-permute-start(f32[145,2,2,2]{3,2,0,1:T(2,128)S(1)} %get-tuple-element.9), channel_id=1, source_target_pairs={{0,1},{1,2},{2,3},{3,4},{4,5},{5,6},{6,7},{7,8},{8,9},{9,10},{10,1... | collective-permute-start | bytes 13928 | tf_op jit(solution)/shard_map/ppermute | solution.py:28
  113.4 0.7 slice_divide_fusion
  114.1 3.7 %collective-permute-done.8 = f32[145,2,2,2]{3,2,0,1:T(2,128)S(1)} collective-permute-done((f32[145,2,2,2]{3,2,0,1:T(2,128)S(1)}, f32[145,2,2,2]{3,2,0,1:T(2,128)S(1)}, u32[]{:S(2)}, u32[]{:S(2)}) %collective-permute-start.8) | collective-permute-done | bytes 4672 | tf_op jit(solution)/shard_map/ppermute | solution.py:31
  117.8 0.0 collective-permute-done.7
  117.8 1.0 pad_maximum_fusion
  118.8 0.2 slice_bitcast_fusion.1
  119.0 0.0 copy-done.1
  119.0 1.1 fusion.8
  120.2 0.9 slice_add_fusion.2
  (20 shorter events, 0.1 us)
Async XLA Ops:
  0.0 106.4 %copy-start = (bf16[1,1,8,256,768]{4,3,2,1,0:T(8,128)(2,1)S(1)}, bf16[1,1,8,256,768]{4,3,2,1,0:T(8,128)(2,1)}, u32[]{:S(2)}) copy-start(bf16[1,1,8,256,768]{4,3,2,1,0:T(8,128)(2,1)} %param.8) | copy-start | bytes 9437188
  4.1 4.9 %collective-permute-start.9 = (f32[145]{0:T(256)S(1)}, f32[145]{0:T(256)S(1)}, u32[]{:S(2)}, u32[]{:S(2)}) collective-permute-start(f32[145]{0:T(256)S(1)} %pad_maximum_fusion.3), channel_id=1, source_target_pairs={{0,32},{32,0},{64,96},{96,64},{128,160},{160,128},{192,224},{224,1... | collective-permute-start | bytes 1748 | tf_op jit(solution)/shard_map/ppermute | solution.py:17
  9.7 5.8 %collective-permute-start.10 = (f32[145]{0:T(256)S(1)}, f32[145]{0:T(256)S(1)}, u32[]{:S(2)}, u32[]{:S(2)}) collective-permute-start(f32[145]{0:T(256)S(1)} %fusion.19), channel_id=1, source_target_pairs={{0,64},{32,96},{64,0},{96,32},{128,192},{160,224},{192,128},{224,1... | collective-permute-start | bytes 1748 | tf_op jit(solution)/shard_map/ppermute | solution.py:17
  15.5 4.4 %collective-permute-start.11 = (f32[145]{0:T(256)S(1)}, f32[145]{0:T(256)S(1)}, u32[]{:S(2)}, u32[]{:S(2)}) collective-permute-start(f32[145]{0:T(256)S(1)} %add.70), channel_id=1, source_target_pairs={{0,128},{32,160},{64,192},{96,224},{128,0},{160,32},{192,64},{224,... | collective-permute-start | bytes 1748 | tf_op jit(solution)/shard_map/ppermute | solution.py:17
  19.9 5.9 %collective-permute-start.12 = (f32[145]{0:T(256)S(1)}, f32[145]{0:T(256)S(1)}, u32[]{:S(2)}, u32[]{:S(2)}) collective-permute-start(f32[145]{0:T(256)S(1)} %add.71), channel_id=1, source_target_pairs={{0,256},{32,288},{64,320},{96,352},{128,384},{160,416},{192,448},{... | collective-permute-start | bytes 1748 | tf_op jit(solution)/shard_map/ppermute | solution.py:17
  25.8 14.8 %collective-permute-start.13 = (f32[145]{0:T(256)S(1)}, f32[145]{0:T(256)S(1)}, u32[]{:S(2)}, u32[]{:S(2)}) collective-permute-start(f32[145]{0:T(256)S(1)} %add.72), channel_id=1, source_target_pairs={{0,1},{1,0},{2,3},{3,2},{4,5},{5,4},{6,7},{7,6},{8,9},{9,8},{10,11... | collective-permute-start | bytes 1748 | tf_op jit(solution)/shard_map/ppermute | solution.py:17
  40.7 4.3 %collective-permute-start.14 = (f32[145]{0:T(256)S(1)}, f32[145]{0:T(256)S(1)}, u32[]{:S(2)}, u32[]{:S(2)}) collective-permute-start(f32[145]{0:T(256)S(1)} %add.73), channel_id=1, source_target_pairs={{0,2},{1,3},{2,0},{3,1},{4,6},{5,7},{6,4},{7,5},{8,10},{9,11},{10,... | collective-permute-start | bytes 1748 | tf_op jit(solution)/shard_map/ppermute | solution.py:17
  42.6 43.8 %collective-permute-start = (bf16[147,256]{1,0:T(8,128)(2,1)S(1)}, bf16[147,256]{1,0:T(8,128)(2,1)S(1)}, u32[]{:S(2)}, u32[]{:S(2)}) collective-permute-start(bf16[147,256]{1,0:T(8,128)(2,1)S(1)} %broadcast_select_fusion.6), channel_id=1, source_target_pairs={{0,31},{1,0},{2,1},{3,2},{4,3},{5,4},{6,5},{7,6},{8,7},{9,8},{10,9... | collective-permute-start | bytes 225800 | tf_op jit(solution)/shard_map/ppermute | solution.py:9
  45.0 13.8 %collective-permute-start.15 = (f32[145]{0:T(256)S(1)}, f32[145]{0:T(256)S(1)}, u32[]{:S(2)}, u32[]{:S(2)}) collective-permute-start(f32[145]{0:T(256)S(1)} %add.74), channel_id=1, source_target_pairs={{0,4},{1,5},{2,6},{3,7},{4,0},{5,1},{6,2},{7,3},{8,12},{9,13},{10,... | collective-permute-start | bytes 1748 | tf_op jit(solution)/shard_map/ppermute | solution.py:17
  47.6 43.6 %collective-permute-start.1 = (bf16[147,256]{1,0:T(8,128)(2,1)}, bf16[147,256]{1,0:T(8,128)(2,1)}, u32[]{:S(2)}, u32[]{:S(2)}) collective-permute-start(bf16[147,256]{1,0:T(8,128)(2,1)} %get-tuple-element.12), channel_id=1, source_target_pairs={{0,30},{1,31},{2,0},{3,1},{4,2},{5,3},{6,4},{7,5},{8,6},{9,7},{10,... | collective-permute-start | bytes 225800 | tf_op jit(solution)/shard_map/ppermute | solution.py:9
  54.5 41.3 %collective-permute-start.2 = (bf16[147,256]{1,0:T(8,128)(2,1)S(1)}, bf16[147,256]{1,0:T(8,128)(2,1)}, u32[]{:S(2)}, u32[]{:S(2)}) collective-permute-start(bf16[147,256]{1,0:T(8,128)(2,1)S(1)} %get-tuple-element.13), channel_id=1, source_target_pairs={{0,29},{1,30},{2,31},{3,0},{4,1},{5,2},{6,3},{7,4},{8,5},{9,6},{10... | collective-permute-start | bytes 225800 | tf_op jit(solution)/shard_map/ppermute | solution.py:9
  58.8 10.0 %collective-permute-start.16 = (f32[145]{0:T(256)S(1)}, f32[145]{0:T(256)S(1)}, u32[]{:S(2)}, u32[]{:S(2)}) collective-permute-start(f32[145]{0:T(256)S(1)} %add.75), channel_id=1, source_target_pairs={{0,8},{1,9},{2,10},{3,11},{4,12},{5,13},{6,14},{7,15},{8,0},{9,1},... | collective-permute-start | bytes 1748 | tf_op jit(solution)/shard_map/ppermute | solution.py:17
  63.1 33.6 %collective-permute-start.3 = (bf16[147,256]{1,0:T(8,128)(2,1)}, bf16[147,256]{1,0:T(8,128)(2,1)}, u32[]{:S(2)}, u32[]{:S(2)}) collective-permute-start(bf16[147,256]{1,0:T(8,128)(2,1)} %get-tuple-element.15), channel_id=1, source_target_pairs={{0,28},{1,29},{2,30},{3,31},{4,0},{5,1},{6,2},{7,3},{8,4},{9,5},{1... | collective-permute-start | bytes 225800 | tf_op jit(solution)/shard_map/ppermute | solution.py:9
  68.8 13.0 %collective-permute-start.17 = (f32[145]{0:T(256)S(1)}, f32[145]{0:T(256)S(1)}, u32[]{:S(2)}, u32[]{:S(2)}) collective-permute-start(f32[145]{0:T(256)S(1)} %add.76), channel_id=1, source_target_pairs={{0,16},{1,17},{2,18},{3,19},{4,20},{5,21},{6,22},{7,23},{8,24},{9,... | collective-permute-start | bytes 1748 | tf_op jit(solution)/shard_map/ppermute | solution.py:17
  81.8 15.8 %collective-permute-start.4 = (bf16[147,256]{1,0:T(8,128)(2,1)}, bf16[147,256]{1,0:T(8,128)(2,1)S(1)}, u32[]{:S(2)}, u32[]{:S(2)}) collective-permute-start(bf16[147,256]{1,0:T(8,128)(2,1)} %get-tuple-element.16), channel_id=1, source_target_pairs={{0,27},{1,28},{2,29},{3,30},{4,31},{5,0},{6,1},{7,2},{8,3},{9,4},{... | collective-permute-start | bytes 225800 | tf_op jit(solution)/shard_map/ppermute | solution.py:9
  86.4 11.2 %collective-permute-start.5 = (bf16[147,256]{1,0:T(8,128)(2,1)}, bf16[147,256]{1,0:T(8,128)(2,1)S(1)}, u32[]{:S(2)}, u32[]{:S(2)}) collective-permute-start(bf16[147,256]{1,0:T(8,128)(2,1)} %get-tuple-element.14), channel_id=1, source_target_pairs={{0,26},{1,27},{2,28},{3,29},{4,30},{5,31},{6,0},{7,1},{8,2},{9,3},... | collective-permute-start | bytes 225800 | tf_op jit(solution)/shard_map/ppermute | solution.py:9
  91.1 15.2 %collective-permute-start.6 = (bf16[147,256]{1,0:T(8,128)(2,1)S(1)}, bf16[147,256]{1,0:T(8,128)(2,1)S(1)}, u32[]{:S(2)}, u32[]{:S(2)}) collective-permute-start(bf16[147,256]{1,0:T(8,128)(2,1)S(1)} %get-tuple-element.11), channel_id=1, source_target_pairs={{0,25},{1,26},{2,27},{3,28},{4,29},{5,30},{6,31},{7,0},{8,1},{9,2}... | collective-permute-start | bytes 225800 | tf_op jit(solution)/shard_map/ppermute | solution.py:9
  106.4 4.7 %copy-start.3 = (f32[2]{0:T(128)S(1)}, f32[2]{0:T(128)}, u32[]{:S(2)}) copy-start(f32[2]{0:T(128)} %constant.36.clone) | copy-start | bytes 28
  109.8 9.1 %copy-start.1 = (f32[144,3,2,128]{3,2,1,0:T(2,128)S(1)}, f32[144,3,2,128]{3,2,1,0:T(2,128)}, u32[]{:S(2)}) copy-start(f32[144,3,2,128]{3,2,1,0:T(2,128)} %concatenate.40) | copy-start | bytes 1327108
  111.0 9.1 %copy-start.2 = (f32[2,128]{1,0:T(2,128)S(1)}, f32[2,128]{1,0:T(2,128)}, u32[]{:S(2)}) copy-start(f32[2,128]{1,0:T(2,128)} %param.6) | copy-start | bytes 3076
  111.6 6.2 %collective-permute-start.8 = (f32[145,2,2,2]{3,2,0,1:T(2,128)S(1)}, f32[145,2,2,2]{3,2,0,1:T(2,128)S(1)}, u32[]{:S(2)}, u32[]{:S(2)}) collective-permute-start(f32[145,2,2,2]{3,2,0,1:T(2,128)S(1)} %get-tuple-element.10), channel_id=1, source_target_pairs={{1,0},{2,1},{3,2},{4,3},{5,4},{6,5},{7,6},{8,7},{9,8},{10,9},{11,1... | collective-permute-start | bytes 13928 | tf_op jit(solution)/shard_map/ppermute | solution.py:31
  111.6 6.2 %collective-permute-start.7 = (f32[145,2,2,2]{3,2,0,1:T(2,128)S(1)}, f32[145,2,2,2]{3,2,0,1:T(2,128)S(1)}, u32[]{:S(2)}, u32[]{:S(2)}) collective-permute-start(f32[145,2,2,2]{3,2,0,1:T(2,128)S(1)} %get-tuple-element.9), channel_id=1, source_target_pairs={{0,1},{1,2},{2,3},{3,4},{4,5},{5,6},{6,7},{7,8},{8,9},{9,10},{10,1... | collective-permute-start | bytes 13928 | tf_op jit(solution)/shard_map/ppermute | solution.py:28

commit v2 on v1

--- a/solution.py
+++ b/solution.py
@@ -52,12 +52,20 @@
     factor = stats[:fields] / stats[fields]
 
     area_parts = split_bf16(cell_area.reshape(1, cell_count))
-    payload = jnp.concatenate([cotangent.reshape(fields, cell_count)] + area_parts, axis=0)
-    count_here = reach_count[0, 0]
+    count_row = jnp.full((1, cell_count), reach_count[0, 0], jnp.float32).astype(jnp.bfloat16)
+    payload = jnp.concatenate([cotangent.reshape(fields, cell_count)] + area_parts + [count_row], axis=0)
+    ring = [payload]
+    for _ in range(slot_count // 2):
+        ring.append(shifted(ring[-1], "lon", -2))
+    odd = lax.axis_index("lon") % 2 == 1
+    half = slot_count // 2
+    offer = jnp.where(odd, jnp.stack(ring[:half]), jnp.stack(ring[1 : half + 1]))
+    swapped = lax.ppermute(offer, "lon", [(i, i ^ 1) for i in range(lax.axis_size("lon"))])
     tiles = []
     for slot_index in range(slot_count):
-        live = jnp.where(count_here > slot_index, payload, jnp.zeros_like(payload))
-        tiles.append(live if slot_index == 0 else shifted(live, "lon", -slot_index))
+        tile = ring[slot_index // 2] if slot_index % 2 == 0 else swapped[slot_index // 2]
+        live = tile[fields + 3, 0].astype(jnp.float32) > slot_index
+        tiles.append(jnp.where(live, tile[: fields + 3], jnp.zeros_like(tile[: fields + 3])))
     stacked = jnp.stack(tiles)
     moments = lax.dot_general(
         stacked, weights[0, 0], (((0, 2), (0, 1)), ((), ())), preferred_element_type=jnp.float32

time: 122 us -> 132 us (1.082); the launches traced: 121 us -> 129 us
  between operations: 1.04 us -> 5.48 us
  other arithmetic: 12 us -> 15.1 us
  local copies, waits for them, and re-layouts: 8.59 us -> 11.6 us
  starting transfers between devices: 73 us -> 70.1 us
    ppermute x9, starting transfers between devices: 42.9 us -> 32.6 us  [butterfly_sum(): lax.ppermute(value, axis, [(i, i ^ step) for i in range(length)])]
    ppermute x9, waiting for transfers between devices: 13.3 us -> 20.9 us  [butterfly_sum(): lax.ppermute(value, axis, [(i, i ^ step) for i in range(length)])]
    ppermute x7 -> x4, waiting for transfers between devices: 8.72 us -> 1.6 us  [shifted(): lax.ppermute(value, axis, [(i, (i + by) % length) for i in range(length)])]
    ppermute x0 -> x1, starting transfers between devices: none -> 6.58 us  [on_device(): lax.ppermute(offer, 'lon', [(i, i ^ 1) for i in range(lax.axis_size('lon'...]
    slice x0 -> x7, local copies, waits for them, and re-layouts: none -> 5.14 us  [on_device(): live = tile[fields + 3, 0].astype(jnp.float32) > slot_index]
    ppermute x1, starting transfers between devices: 0.02 us -> 4.79 us  [padded_2(): lax.ppermute(lax.slice_in_dim(block, 0, width, axis=dim), axis, backward)]
    unnamed x1 -> x7, other arithmetic: 0.02 us -> 2.81 us
    unnamed x15 -> x13, local copies, waits for them, and re-layouts: 3.62 us -> 0.93 us
  transfers between devices with their start and end apart: 18 -> 16, of which waited for: 8 -> 11; matrix products, arithmetic and copies ran while one was open for 7% -> 10% of each run, Pallas kernels for 0% -> 0%
where the time goes in v2:
time: 132 us; the launch traced here: 129 us
  starting transfers between devices  70.1 us (53%)
  waiting for transfers between devices  26.3 us (20%)
  other arithmetic  15.1 us (11%)
  local copies, waits for them, and re-layouts  11.6 us (9%)
  between operations  5.48 us (4%)
    ppermute x9, starting transfers between devices, butterfly_sum(): lax.ppermute(value, axis, [(i, i ^ step) for i in range(length)])  32.6 us
    ppermute x4, starting transfers between devices, shifted(): lax.ppermute(value, axis, [(i, (i + by) % length) for i in range(length)])  26.2 us
    ppermute x9, waiting for transfers between devices, butterfly_sum(): lax.ppermute(value, axis, [(i, i ^ step) for i in range(length)])  20.9 us
    ppermute x1, starting transfers between devices, on_device(): lax.ppermute(offer, 'lon', [(i, i ^ 1) for i in range(lax.axis_size('lon'...  6.58 us
    slice x7, local copies, waits for them, and re-layouts, on_device(): live = tile[fields + 3, 0].astype(jnp.float32) > slot_index  5.14 us
    ppermute x1, starting transfers between devices, padded_2(): lax.ppermute(lax.slice_in_dim(block, 0, width, axis=dim), axis, backward)  4.79 us
    ppermute x1, waiting for transfers between devices, padded_2(): lax.ppermute(lax.slice_in_dim(block, 0, width, axis=dim), axis, backward)  3.78 us
    unnamed x7, other arithmetic  2.81 us
  transfers between devices with their start and end apart: 16, of which 11 were waited for; matrix products, arithmetic and copies ran while one was open for 10% of the time, Pallas kernels for 0%

profile of v2, /device:TPU:1, one launch (start us, length us, event | category | flops | bytes accessed | tf_op | source)
XLA Modules:
  0.0 129.3 jit_solution(6554122880587886437)
XLA Ops:
  0.0 0.8 reduce-precision_convert_fusion.1
  1.6 0.9 copy.14
  2.6 11.9 %collective-permute-start = (bf16[148,256]{1,0:T(8,128)(2,1)S(1)}, bf16[148,256]{1,0:T(8,128)(2,1)S(1)}, u32[]{:S(2)}, u32[]{:S(2)}) collective-permute-start(bf16[148,256]{1,0:T(8,128)(2,1)S(1)} %concatenate.38), channel_id=1, source_target_pairs={{0,30},{1,31},{2,0},{3,1},{4,2},{5,3},{6,4},{7,5},{8,6},{9,7},{10,... | collective-permute-start | bytes 227336 | tf_op jit(solution)/shard_map/ppermute | solution.py:9
  14.5 1.4 %collective-permute-done = bf16[148,256]{1,0:T(8,128)(2,1)S(1)} collective-permute-done((bf16[148,256]{1,0:T(8,128)(2,1)S(1)}, bf16[148,256]{1,0:T(8,128)(2,1)S(1)}, u32[]{:S(2)}, u32[]{:S(2)}) %collective-permute-start) | collective-permute-done | bytes 75808 | tf_op jit(solution)/shard_map/ppermute | solution.py:9
  15.9 4.9 %collective-permute-start.1 = (bf16[148,256]{1,0:T(8,128)(2,1)S(1)}, bf16[148,256]{1,0:T(8,128)(2,1)S(1)}, u32[]{:S(2)}, u32[]{:S(2)}) collective-permute-start(bf16[148,256]{1,0:T(8,128)(2,1)S(1)} %collective-permute-done), channel_id=1, source_target_pairs={{0,30},{1,31},{2,0},{3,1},{4,2},{5,3},{6,4},{7,5},{8,6},{9,7},{10,... | collective-permute-start | bytes 227336 | tf_op jit(solution)/shard_map/ppermute | solution.py:9
  20.9 1.9 %multiply_reduce_fusion = f32[144]{0:T(256)S(1)} fusion(bf16[144,2,128]{2,1,0:T(2,128)(2,1)} %param.5, f32[2,128]{1,0:T(2,128)} %param.6), kind=kLoop, calls=%fused_computation.29 | loop fusion | flops 110448 | bytes 75328 | tf_op jit(solution)/shard_map/reduce_sum | solution.py:49
  22.8 0.0 collective-permute-done.1
  22.8 4.4 %collective-permute-start.2 = (bf16[148,256]{1,0:T(8,128)(2,1)S(1)}, bf16[148,256]{1,0:T(8,128)(2,1)S(1)}, u32[]{:S(2)}, u32[]{:S(2)}) collective-permute-start(bf16[148,256]{1,0:T(8,128)(2,1)S(1)} %collective-permute-done.1), channel_id=1, source_target_pairs={{0,30},{1,31},{2,0},{3,1},{4,2},{5,3},{6,4},{7,5},{8,6},{9,7},{10,... | collective-permute-start | bytes 227336 | tf_op jit(solution)/shard_map/ppermute | solution.py:9
  27.2 1.3 multiply_reduce_fusion.1
  28.5 0.2 collective-permute-done.2
  28.6 4.9 %collective-permute-start.3 = (bf16[148,256]{1,0:T(8,128)(2,1)S(1)}, bf16[148,256]{1,0:T(8,128)(2,1)S(1)}, u32[]{:S(2)}, u32[]{:S(2)}) collective-permute-start(bf16[148,256]{1,0:T(8,128)(2,1)S(1)} %collective-permute-done.2), channel_id=1, source_target_pairs={{0,30},{1,31},{2,0},{3,1},{4,2},{5,3},{6,4},{7,5},{8,6},{9,7},{10,... | collective-permute-start | bytes 227336 | tf_op jit(solution)/shard_map/ppermute | solution.py:9
  33.5 1.2 pad_maximum_fusion.2
  34.7 3.1 %collective-permute-start.7 = (f32[145]{0:T(256)}, f32[145]{0:T(256)S(1)}, u32[]{:S(2)}, u32[]{:S(2)}) collective-permute-start(f32[145]{0:T(256)} %pad_maximum_fusion.2), channel_id=1, source_target_pairs={{0,32},{32,0},{64,96},{96,64},{128,160},{160,128},{192,224},{224,1... | collective-permute-start | bytes 1748 | tf_op jit(solution)/shard_map/ppermute | solution.py:17
  37.9 0.0 collective-permute-done.3
  37.9 0.8 maximum_select_fusion
  38.7 6.6 %collective-permute-start.4 = (bf16[4,148,256]{2,1,0:T(8,128)(2,1)}, bf16[4,148,256]{2,1,0:T(8,128)(2,1)S(1)}, u32[]{:S(2)}, u32[]{:S(2)}) collective-permute-start(bf16[4,148,256]{2,1,0:T(8,128)(2,1)} %maximum_select_fusion), channel_id=1, source_target_pairs={{0,1},{1,0},{2,3},{3,2},{4,5},{5,4},{6,7},{7,6},{8,9},{9,8},{10,11... | collective-permute-start | bytes 909320 | tf_op jit(solution)/shard_map/ppermute | solution.py:63
  45.3 0.0 collective-permute-done.7
  45.3 0.6 fusion.29
  45.9 4.3 %collective-permute-start.8 = (f32[145]{0:T(256)S(1)}, f32[145]{0:T(256)S(1)}, u32[]{:S(2)}, u32[]{:S(2)}) collective-permute-start(f32[145]{0:T(256)S(1)} %fusion.29), channel_id=1, source_target_pairs={{0,64},{32,96},{64,0},{96,32},{128,192},{160,224},{192,128},{224,1... | collective-permute-start | bytes 1748 | tf_op jit(solution)/shard_map/ppermute | solution.py:17
  50.3 1.5 %collective-permute-done.8 = f32[145]{0:T(256)S(1)} collective-permute-done((f32[145]{0:T(256)S(1)}, f32[145]{0:T(256)S(1)}, u32[]{:S(2)}, u32[]{:S(2)}) %collective-permute-start.8) | collective-permute-done | bytes 612 | tf_op jit(solution)/shard_map/ppermute | solution.py:17
  51.7 3.2 %collective-permute-start.9 = (f32[145]{0:T(256)S(1)}, f32[145]{0:T(256)S(1)}, u32[]{:S(2)}, u32[]{:S(2)}) collective-permute-start(f32[145]{0:T(256)S(1)} %add.75), channel_id=1, source_target_pairs={{0,128},{32,160},{64,192},{96,224},{128,0},{160,32},{192,64},{224,... | collective-permute-start | bytes 1748 | tf_op jit(solution)/shard_map/ppermute | solution.py:17
  54.9 1.1 collective-permute-done.9
  56.0 4.8 %collective-permute-start.10 = (f32[145]{0:T(256)S(1)}, f32[145]{0:T(256)S(1)}, u32[]{:S(2)}, u32[]{:S(2)}) collective-permute-start(f32[145]{0:T(256)S(1)} %add.76), channel_id=1, source_target_pairs={{0,256},{32,288},{64,320},{96,352},{128,384},{160,416},{192,448},{... | collective-permute-start | bytes 1748 | tf_op jit(solution)/shard_map/ppermute | solution.py:17
  60.9 1.0 collective-permute-done.10
  61.8 5.4 %collective-permute-start.11 = (f32[145]{0:T(256)S(1)}, f32[145]{0:T(256)S(1)}, u32[]{:S(2)}, u32[]{:S(2)}) collective-permute-start(f32[145]{0:T(256)S(1)} %add.77), channel_id=1, source_target_pairs={{0,1},{1,0},{2,3},{3,2},{4,5},{5,4},{6,7},{7,6},{8,9},{9,8},{10,11... | collective-permute-start | bytes 1748 | tf_op jit(solution)/shard_map/ppermute | solution.py:17
  67.2 0.8 collective-permute-done.11
  68.0 1.9 %collective-permute-start.12 = (f32[145]{0:T(256)S(1)}, f32[145]{0:T(256)S(1)}, u32[]{:S(2)}, u32[]{:S(2)}) collective-permute-start(f32[145]{0:T(256)S(1)} %add.78), channel_id=1, source_target_pairs={{0,2},{1,3},{2,0},{3,1},{4,6},{5,7},{6,4},{7,5},{8,10},{9,11},{10,... | collective-permute-start | bytes 1748 | tf_op jit(solution)/shard_map/ppermute | solution.py:17
  69.9 2.4 %collective-permute-done.12 = f32[145]{0:T(256)S(1)} collective-permute-done((f32[145]{0:T(256)S(1)}, f32[145]{0:T(256)S(1)}, u32[]{:S(2)}, u32[]{:S(2)}) %collective-permute-start.12) | collective-permute-done | bytes 612 | tf_op jit(solution)/shard_map/ppermute | solution.py:17
  72.3 1.9 %collective-permute-start.13 = (f32[145]{0:T(256)S(1)}, f32[145]{0:T(256)S(1)}, u32[]{:S(2)}, u32[]{:S(2)}) collective-permute-start(f32[145]{0:T(256)S(1)} %add.79), channel_id=1, source_target_pairs={{0,4},{1,5},{2,6},{3,7},{4,0},{5,1},{6,2},{7,3},{8,12},{9,13},{10,... | collective-permute-start | bytes 1748 | tf_op jit(solution)/shard_map/ppermute | solution.py:17
  74.2 3.3 %collective-permute-done.13 = f32[145]{0:T(256)S(1)} collective-permute-done((f32[145]{0:T(256)S(1)}, f32[145]{0:T(256)S(1)}, u32[]{:S(2)}, u32[]{:S(2)}) %collective-permute-start.13) | collective-permute-done | bytes 612 | tf_op jit(solution)/shard_map/ppermute | solution.py:17
  77.5 1.9 %collective-permute-start.14 = (f32[145]{0:T(256)S(1)}, f32[145]{0:T(256)}, u32[]{:S(2)}, u32[]{:S(2)}) collective-permute-start(f32[145]{0:T(256)S(1)} %add.80), channel_id=1, source_target_pairs={{0,8},{1,9},{2,10},{3,11},{4,12},{5,13},{6,14},{7,15},{8,0},{9,1},... | collective-permute-start | bytes 1748 | tf_op jit(solution)/shard_map/ppermute | solution.py:17
  79.5 1.6 %concatenate.33 = bf16[1,144,256]{2,1,0:T(8,128)(2,1)} reshape(bf16[144,2,128]{2,1,0:T(2,128)(2,1)} %param.5) | data formatting | bytes 147456 | tf_op jit(solution)/shard_map/concatenate | solution.py:56
  81.0 4.8 %collective-permute-done.14 = f32[145]{0:T(256)} collective-permute-done((f32[145]{0:T(256)S(1)}, f32[145]{0:T(256)}, u32[]{:S(2)}, u32[]{:S(2)}) %collective-permute-start.14) | collective-permute-done | bytes 612 | tf_op jit(solution)/shard_map/ppermute | solution.py:17
  85.9 0.7 add.81
  86.5 6.0 %collective-permute-start.15 = (f32[145]{0:T(256)S(1)}, f32[145]{0:T(256)S(1)}, u32[]{:S(2)}, u32[]{:S(2)}) collective-permute-start(f32[145]{0:T(256)S(1)} %add.81), channel_id=1, source_target_pairs={{0,16},{1,17},{2,18},{3,19},{4,20},{5,21},{6,22},{7,23},{8,24},{9,... | collective-permute-start | bytes 1748 | tf_op jit(solution)/shard_map/ppermute | solution.py:17
  92.6 0.9 fusion.23
  93.5 6.1 %collective-permute-done.15 = f32[145]{0:T(256)S(1)} collective-permute-done((f32[145]{0:T(256)S(1)}, f32[145]{0:T(256)S(1)}, u32[]{:S(2)}, u32[]{:S(2)}) %collective-permute-start.15) | collective-permute-done | bytes 612 | tf_op jit(solution)/shard_map/ppermute | solution.py:17
  99.6 0.6 slice.174
  100.1 0.5 slice.179
  101.2 1.3 slice.184
  103.1 1.2 slice.189
  104.8 0.0 collective-permute-done.4
  104.8 0.6 slice.177
  105.4 0.5 slice.182
  105.9 0.5 slice.187
  106.5 0.6 slice.192
  109.7 0.9 fusion.18
  110.7 0.9 fusion.15
  111.6 0.0 copy-start.5
  111.6 0.7 fusion.2
  112.3 0.8 slice.194
  113.1 2.0 %concatenate.39 = f32[144,3,2,128]{3,2,1,0:T(2,128)} reshape(f32[144,768]{1,0:T(8,128)} %slice.194) | data formatting | bytes 884736 | tf_op jit(solution)/shard_map/concatenate | solution.py:74
  115.1 1.2 fusion.11
  116.3 0.0 copy-start.4
  116.3 0.2 multiply_add_fusion
  116.5 0.4 fusion.27
  116.9 4.8 %collective-permute-start.6 = (f32[145,2,2,2]{3,2,0,1:T(2,128)S(1)}, f32[145,2,2,2]{3,2,0,1:T(2,128)S(1)}, u32[]{:S(2)}, u32[]{:S(2)}) collective-permute-start(f32[145,2,2,2]{3,2,0,1:T(2,128)S(1)} %get-tuple-element.14), channel_id=1, source_target_pairs={{1,0},{2,1},{3,2},{4,3},{5,4},{6,5},{7,6},{8,7},{9,8},{10,9},{11,1... | collective-permute-start | bytes 13928 | tf_op jit(solution)/shard_map/ppermute | solution.py:31
  121.7 0.0 collective-permute-start.5
  121.7 0.6 slice_divide_fusion
  122.3 3.8 %collective-permute-done.6 = f32[145,2,2,2]{3,2,0,1:T(2,128)S(1)} collective-permute-done((f32[145,2,2,2]{3,2,0,1:T(2,128)S(1)}, f32[145,2,2,2]{3,2,0,1:T(2,128)S(1)}, u32[]{:S(2)}, u32[]{:S(2)}) %collective-permute-start.6) | collective-permute-done | bytes 4672 | tf_op jit(solution)/shard_map/ppermute | solution.py:31
  126.0 1.0 pad_maximum_fusion
  127.0 0.2 slice_bitcast_fusion.1
  127.3 1.1 fusion.8
  128.4 0.9 slice_add_fusion.2
  (28 shorter events, 0.2 us)
Async XLA Ops:
  0.0 111.6 %copy-start = (bf16[1,1,8,256,768]{4,3,2,1,0:T(8,128)(2,1)S(1)}, bf16[1,1,8,256,768]{4,3,2,1,0:T(8,128)(2,1)}, u32[]{:S(2)}) copy-start(bf16[1,1,8,256,768]{4,3,2,1,0:T(8,128)(2,1)} %param.8) | copy-start | bytes 9437188
  2.6 13.4 %collective-permute-start = (bf16[148,256]{1,0:T(8,128)(2,1)S(1)}, bf16[148,256]{1,0:T(8,128)(2,1)S(1)}, u32[]{:S(2)}, u32[]{:S(2)}) collective-permute-start(bf16[148,256]{1,0:T(8,128)(2,1)S(1)} %concatenate.38), channel_id=1, source_target_pairs={{0,30},{1,31},{2,0},{3,1},{4,2},{5,3},{6,4},{7,5},{8,6},{9,7},{10,... | collective-permute-start | bytes 227336 | tf_op jit(solution)/shard_map/ppermute | solution.py:9
  15.9 6.8 %collective-permute-start.1 = (bf16[148,256]{1,0:T(8,128)(2,1)S(1)}, bf16[148,256]{1,0:T(8,128)(2,1)S(1)}, u32[]{:S(2)}, u32[]{:S(2)}) collective-permute-start(bf16[148,256]{1,0:T(8,128)(2,1)S(1)} %collective-permute-done), channel_id=1, source_target_pairs={{0,30},{1,31},{2,0},{3,1},{4,2},{5,3},{6,4},{7,5},{8,6},{9,7},{10,... | collective-permute-start | bytes 227336 | tf_op jit(solution)/shard_map/ppermute | solution.py:9
  22.8 15.1 %copy-start.2 = (bf16[148,256]{1,0:T(8,128)(2,1)}, bf16[148,256]{1,0:T(8,128)(2,1)S(1)}, u32[]{:S(2)}) copy-start(bf16[148,256]{1,0:T(8,128)(2,1)S(1)} %collective-permute-done.1) | copy-start | bytes 227332
  22.8 5.8 %collective-permute-start.2 = (bf16[148,256]{1,0:T(8,128)(2,1)S(1)}, bf16[148,256]{1,0:T(8,128)(2,1)S(1)}, u32[]{:S(2)}, u32[]{:S(2)}) collective-permute-start(bf16[148,256]{1,0:T(8,128)(2,1)S(1)} %collective-permute-done.1), channel_id=1, source_target_pairs={{0,30},{1,31},{2,0},{3,1},{4,2},{5,3},{6,4},{7,5},{8,6},{9,7},{10,... | collective-permute-start | bytes 227336 | tf_op jit(solution)/shard_map/ppermute | solution.py:9
  28.6 9.3 %copy-start.3 = (bf16[148,256]{1,0:T(8,128)(2,1)}, bf16[148,256]{1,0:T(8,128)(2,1)S(1)}, u32[]{:S(2)}) copy-start(bf16[148,256]{1,0:T(8,128)(2,1)S(1)} %collective-permute-done.2) | copy-start | bytes 227332
  28.6 9.2 %collective-permute-start.3 = (bf16[148,256]{1,0:T(8,128)(2,1)S(1)}, bf16[148,256]{1,0:T(8,128)(2,1)S(1)}, u32[]{:S(2)}, u32[]{:S(2)}) collective-permute-start(bf16[148,256]{1,0:T(8,128)(2,1)S(1)} %collective-permute-done.2), channel_id=1, source_target_pairs={{0,30},{1,31},{2,0},{3,1},{4,2},{5,3},{6,4},{7,5},{8,6},{9,7},{10,... | collective-permute-start | bytes 227336 | tf_op jit(solution)/shard_map/ppermute | solution.py:9
  34.7 10.5 %collective-permute-start.7 = (f32[145]{0:T(256)}, f32[145]{0:T(256)S(1)}, u32[]{:S(2)}, u32[]{:S(2)}) collective-permute-start(f32[145]{0:T(256)} %pad_maximum_fusion.2), channel_id=1, source_target_pairs={{0,32},{32,0},{64,96},{96,64},{128,160},{160,128},{192,224},{224,1... | collective-permute-start | bytes 1748 | tf_op jit(solution)/shard_map/ppermute | solution.py:17
  38.7 66.1 %collective-permute-start.4 = (bf16[4,148,256]{2,1,0:T(8,128)(2,1)}, bf16[4,148,256]{2,1,0:T(8,128)(2,1)S(1)}, u32[]{:S(2)}, u32[]{:S(2)}) collective-permute-start(bf16[4,148,256]{2,1,0:T(8,128)(2,1)} %maximum_select_fusion), channel_id=1, source_target_pairs={{0,1},{1,0},{2,3},{3,2},{4,5},{5,4},{6,7},{7,6},{8,9},{9,8},{10,11... | collective-permute-start | bytes 909320 | tf_op jit(solution)/shard_map/ppermute | solution.py:63
  45.9 5.8 %collective-permute-start.8 = (f32[145]{0:T(256)S(1)}, f32[145]{0:T(256)S(1)}, u32[]{:S(2)}, u32[]{:S(2)}) collective-permute-start(f32[145]{0:T(256)S(1)} %fusion.29), channel_id=1, source_target_pairs={{0,64},{32,96},{64,0},{96,32},{128,192},{160,224},{192,128},{224,1... | collective-permute-start | bytes 1748 | tf_op jit(solution)/shard_map/ppermute | solution.py:17
  51.7 4.3 %collective-permute-start.9 = (f32[145]{0:T(256)S(1)}, f32[145]{0:T(256)S(1)}, u32[]{:S(2)}, u32[]{:S(2)}) collective-permute-start(f32[145]{0:T(256)S(1)} %add.75), channel_id=1, source_target_pairs={{0,128},{32,160},{64,192},{96,224},{128,0},{160,32},{192,64},{224,... | collective-permute-start | bytes 1748 | tf_op jit(solution)/shard_map/ppermute | solution.py:17
  56.0 5.8 %collective-permute-start.10 = (f32[145]{0:T(256)S(1)}, f32[145]{0:T(256)S(1)}, u32[]{:S(2)}, u32[]{:S(2)}) collective-permute-start(f32[145]{0:T(256)S(1)} %add.76), channel_id=1, source_target_pairs={{0,256},{32,288},{64,320},{96,352},{128,384},{160,416},{192,448},{... | collective-permute-start | bytes 1748 | tf_op jit(solution)/shard_map/ppermute | solution.py:17
  61.8 6.2 %collective-permute-start.11 = (f32[145]{0:T(256)S(1)}, f32[145]{0:T(256)S(1)}, u32[]{:S(2)}, u32[]{:S(2)}) collective-permute-start(f32[145]{0:T(256)S(1)} %add.77), channel_id=1, source_target_pairs={{0,1},{1,0},{2,3},{3,2},{4,5},{5,4},{6,7},{7,6},{8,9},{9,8},{10,11... | collective-permute-start | bytes 1748 | tf_op jit(solution)/shard_map/ppermute | solution.py:17
  68.0 4.3 %collective-permute-start.12 = (f32[145]{0:T(256)S(1)}, f32[145]{0:T(256)S(1)}, u32[]{:S(2)}, u32[]{:S(2)}) collective-permute-start(f32[145]{0:T(256)S(1)} %add.78), channel_id=1, source_target_pairs={{0,2},{1,3},{2,0},{3,1},{4,6},{5,7},{6,4},{7,5},{8,10},{9,11},{10,... | collective-permute-start | bytes 1748 | tf_op jit(solution)/shard_map/ppermute | solution.py:17
  72.3 5.2 %collective-permute-start.13 = (f32[145]{0:T(256)S(1)}, f32[145]{0:T(256)S(1)}, u32[]{:S(2)}, u32[]{:S(2)}) collective-permute-start(f32[145]{0:T(256)S(1)} %add.79), channel_id=1, source_target_pairs={{0,4},{1,5},{2,6},{3,7},{4,0},{5,1},{6,2},{7,3},{8,12},{9,13},{10,... | collective-permute-start | bytes 1748 | tf_op jit(solution)/shard_map/ppermute | solution.py:17
  77.5 8.3 %collective-permute-start.14 = (f32[145]{0:T(256)S(1)}, f32[145]{0:T(256)}, u32[]{:S(2)}, u32[]{:S(2)}) collective-permute-start(f32[145]{0:T(256)S(1)} %add.80), channel_id=1, source_target_pairs={{0,8},{1,9},{2,10},{3,11},{4,12},{5,13},{6,14},{7,15},{8,0},{9,1},... | collective-permute-start | bytes 1748 | tf_op jit(solution)/shard_map/ppermute | solution.py:17
  86.5 13.0 %collective-permute-start.15 = (f32[145]{0:T(256)S(1)}, f32[145]{0:T(256)S(1)}, u32[]{:S(2)}, u32[]{:S(2)}) collective-permute-start(f32[145]{0:T(256)S(1)} %add.81), channel_id=1, source_target_pairs={{0,16},{1,17},{2,18},{3,19},{4,20},{5,21},{6,22},{7,23},{8,24},{9,... | collective-permute-start | bytes 1748 | tf_op jit(solution)/shard_map/ppermute | solution.py:17
  111.6 4.7 %copy-start.5 = (f32[2]{0:T(128)S(1)}, f32[2]{0:T(128)}, u32[]{:S(2)}) copy-start(f32[2]{0:T(128)} %constant.51.clone) | copy-start | bytes 28
  115.1 12.1 %copy-start.1 = (f32[144,3,2,128]{3,2,1,0:T(2,128)S(1)}, f32[144,3,2,128]{3,2,1,0:T(2,128)}, u32[]{:S(2)}) copy-start(f32[144,3,2,128]{3,2,1,0:T(2,128)} %concatenate.39) | copy-start | bytes 1327108
  116.3 12.1 %copy-start.4 = (f32[2,128]{1,0:T(2,128)S(1)}, f32[2,128]{1,0:T(2,128)}, u32[]{:S(2)}) copy-start(f32[2,128]{1,0:T(2,128)} %param.6) | copy-start | bytes 3076
  116.9 9.2 %collective-permute-start.6 = (f32[145,2,2,2]{3,2,0,1:T(2,128)S(1)}, f32[145,2,2,2]{3,2,0,1:T(2,128)S(1)}, u32[]{:S(2)}, u32[]{:S(2)}) collective-permute-start(f32[145,2,2,2]{3,2,0,1:T(2,128)S(1)} %get-tuple-element.14), channel_id=1, source_target_pairs={{1,0},{2,1},{3,2},{4,3},{5,4},{6,5},{7,6},{8,7},{9,8},{10,9},{11,1... | collective-permute-start | bytes 13928 | tf_op jit(solution)/shard_map/ppermute | solution.py:31
  121.7 4.4 %collective-permute-start.5 = (f32[145,2,2,2]{3,2,0,1:T(2,128)S(1)}, f32[145,2,2,2]{3,2,0,1:T(2,128)S(1)}, u32[]{:S(2)}, u32[]{:S(2)}) collective-permute-start(f32[145,2,2,2]{3,2,0,1:T(2,128)S(1)} %get-tuple-element.13), channel_id=1, source_target_pairs={{0,1},{1,2},{2,3},{3,4},{4,5},{5,6},{6,7},{7,8},{8,9},{9,10},{10,1... | collective-permute-start | bytes 13928 | tf_op jit(solution)/shard_map/ppermute | solution.py:28

commit v3 on v2

--- a/solution.py
+++ b/solution.py
@@ -14,7 +14,8 @@
         length = lax.axis_size(axis)
         step = 1
         while step < length:
-            value = value + lax.ppermute(value, axis, [(i, i ^ step) for i in range(length)])
+            partner = lax.ppermute(value, axis, [(i, i ^ step) for i in range(length)])
+            value = value + partner
             step *= 2
     return value
 
@@ -41,7 +42,7 @@
     return [part.astype(jnp.bfloat16) for part in (high, middle, low)]
 
 
-def on_device(cotangent, cell_area, reach_count, weights):
+def on_device_body(cotangent, cell_area, reach_count, weights):
     fields, tile_rows, tile_cols = cotangent.shape
     cell_count = tile_rows * tile_cols
     slot_count = weights.shape[2]
@@ -105,5 +106,5 @@
     )
     out_specs = P(None, "lat", "lon")
     return jax.shard_map(
-        on_device, mesh=mesh, in_specs=in_specs, out_specs=out_specs, check_vma=False
+        on_device_body, mesh=mesh, in_specs=in_specs, out_specs=out_specs, check_vma=False
     )

time: 132 us -> 132 us (level)
  no operation moved by 1% of the time
where the time goes in v3:
time: 132 us; the launch traced here: 129 us
  starting transfers between devices  70.1 us (53%)
  waiting for transfers between devices  26.3 us (20%)
  other arithmetic  15.1 us (11%)
  local copies, waits for them, and re-layouts  11.6 us (9%)
  between operations  5.48 us (4%)
    ppermute x9, starting transfers between devices, butterfly_sum(): partner = lax.ppermute(value, axis, [(i, i ^ step) for i in range(length)])  32.6 us
    ppermute x4, starting transfers between devices, shifted(): lax.ppermute(value, axis, [(i, (i + by) % length) for i in range(length)])  26.2 us
    ppermute x9, waiting for transfers between devices, butterfly_sum(): partner = lax.ppermute(value, axis, [(i, i ^ step) for i in range(length)])  20.9 us
    ppermute x1, starting transfers between devices, on_device_body(): lax.ppermute(offer, 'lon', [(i, i ^ 1) for i in range(lax.axis_size('lon'...  6.58 us
    slice x7, local copies, waits for them, and re-layouts, on_device_body(): live = tile[fields + 3, 0].astype(jnp.float32) > slot_index  5.14 us
    ppermute x1, starting transfers between devices, padded_2(): lax.ppermute(lax.slice_in_dim(block, 0, width, axis=dim), axis, backward)  4.79 us
    ppermute x1, waiting for transfers between devices, padded_2(): lax.ppermute(lax.slice_in_dim(block, 0, width, axis=dim), axis, backward)  3.78 us
    unnamed x7, other arithmetic  2.81 us
  transfers between devices with their start and end apart: 16, of which 11 were waited for; matrix products, arithmetic and copies ran while one was open for 10% of the time, Pallas kernels for 0%

profile of v3, /device:TPU:1, one launch (start us, length us, event | category | flops | bytes accessed | tf_op | source)
XLA Modules:
  0.0 129.3 jit_solution(6554122880587886437)
XLA Ops:
  0.0 0.8 reduce-precision_convert_fusion.1
  1.6 0.9 copy.14
  2.6 11.9 %collective-permute-start = (bf16[148,256]{1,0:T(8,128)(2,1)S(1)}, bf16[148,256]{1,0:T(8,128)(2,1)S(1)}, u32[]{:S(2)}, u32[]{:S(2)}) collective-permute-start(bf16[148,256]{1,0:T(8,128)(2,1)S(1)} %concatenate.38), channel_id=1, source_target_pairs={{0,30},{1,31},{2,0},{3,1},{4,2},{5,3},{6,4},{7,5},{8,6},{9,7},{10,... | collective-permute-start | bytes 227336 | tf_op jit(solution)/shard_map/ppermute | solution.py:9
  14.5 1.4 %collective-permute-done = bf16[148,256]{1,0:T(8,128)(2,1)S(1)} collective-permute-done((bf16[148,256]{1,0:T(8,128)(2,1)S(1)}, bf16[148,256]{1,0:T(8,128)(2,1)S(1)}, u32[]{:S(2)}, u32[]{:S(2)}) %collective-permute-start) | collective-permute-done | bytes 75808 | tf_op jit(solution)/shard_map/ppermute | solution.py:9
  15.9 4.9 %collective-permute-start.1 = (bf16[148,256]{1,0:T(8,128)(2,1)S(1)}, bf16[148,256]{1,0:T(8,128)(2,1)S(1)}, u32[]{:S(2)}, u32[]{:S(2)}) collective-permute-start(bf16[148,256]{1,0:T(8,128)(2,1)S(1)} %collective-permute-done), channel_id=1, source_target_pairs={{0,30},{1,31},{2,0},{3,1},{4,2},{5,3},{6,4},{7,5},{8,6},{9,7},{10,... | collective-permute-start | bytes 227336 | tf_op jit(solution)/shard_map/ppermute | solution.py:9
  20.9 1.9 %multiply_reduce_fusion = f32[144]{0:T(256)S(1)} fusion(bf16[144,2,128]{2,1,0:T(2,128)(2,1)} %param.5, f32[2,128]{1,0:T(2,128)} %param.6), kind=kLoop, calls=%fused_computation.29 | loop fusion | flops 110448 | bytes 75328 | tf_op jit(solution)/shard_map/reduce_sum | solution.py:50
  22.8 0.0 collective-permute-done.1
  22.8 4.4 %collective-permute-start.2 = (bf16[148,256]{1,0:T(8,128)(2,1)S(1)}, bf16[148,256]{1,0:T(8,128)(2,1)S(1)}, u32[]{:S(2)}, u32[]{:S(2)}) collective-permute-start(bf16[148,256]{1,0:T(8,128)(2,1)S(1)} %collective-permute-done.1), channel_id=1, source_target_pairs={{0,30},{1,31},{2,0},{3,1},{4,2},{5,3},{6,4},{7,5},{8,6},{9,7},{10,... | collective-permute-start | bytes 227336 | tf_op jit(solution)/shard_map/ppermute | solution.py:9
  27.2 1.3 multiply_reduce_fusion.1
  28.5 0.2 collective-permute-done.2
  28.6 4.9 %collective-permute-start.3 = (bf16[148,256]{1,0:T(8,128)(2,1)S(1)}, bf16[148,256]{1,0:T(8,128)(2,1)S(1)}, u32[]{:S(2)}, u32[]{:S(2)}) collective-permute-start(bf16[148,256]{1,0:T(8,128)(2,1)S(1)} %collective-permute-done.2), channel_id=1, source_target_pairs={{0,30},{1,31},{2,0},{3,1},{4,2},{5,3},{6,4},{7,5},{8,6},{9,7},{10,... | collective-permute-start | bytes 227336 | tf_op jit(solution)/shard_map/ppermute | solution.py:9
  33.5 1.2 pad_maximum_fusion.2
  34.7 3.1 %collective-permute-start.7 = (f32[145]{0:T(256)}, f32[145]{0:T(256)S(1)}, u32[]{:S(2)}, u32[]{:S(2)}) collective-permute-start(f32[145]{0:T(256)} %pad_maximum_fusion.2), channel_id=1, source_target_pairs={{0,32},{32,0},{64,96},{96,64},{128,160},{160,128},{192,224},{224,1... | collective-permute-start | bytes 1748 | tf_op jit(solution)/shard_map/ppermute | solution.py:17
  37.9 0.0 collective-permute-done.3
  37.9 0.8 maximum_select_fusion
  38.7 6.6 %collective-permute-start.4 = (bf16[4,148,256]{2,1,0:T(8,128)(2,1)}, bf16[4,148,256]{2,1,0:T(8,128)(2,1)S(1)}, u32[]{:S(2)}, u32[]{:S(2)}) collective-permute-start(bf16[4,148,256]{2,1,0:T(8,128)(2,1)} %maximum_select_fusion), channel_id=1, source_target_pairs={{0,1},{1,0},{2,3},{3,2},{4,5},{5,4},{6,7},{7,6},{8,9},{9,8},{10,11... | collective-permute-start | bytes 909320 | tf_op jit(solution)/shard_map/ppermute | solution.py:64
  45.3 0.0 collective-permute-done.7
  45.3 0.6 fusion.29
  45.9 4.3 %collective-permute-start.8 = (f32[145]{0:T(256)S(1)}, f32[145]{0:T(256)S(1)}, u32[]{:S(2)}, u32[]{:S(2)}) collective-permute-start(f32[145]{0:T(256)S(1)} %fusion.29), channel_id=1, source_target_pairs={{0,64},{32,96},{64,0},{96,32},{128,192},{160,224},{192,128},{224,1... | collective-permute-start | bytes 1748 | tf_op jit(solution)/shard_map/ppermute | solution.py:17
  50.3 1.5 %collective-permute-done.8 = f32[145]{0:T(256)S(1)} collective-permute-done((f32[145]{0:T(256)S(1)}, f32[145]{0:T(256)S(1)}, u32[]{:S(2)}, u32[]{:S(2)}) %collective-permute-start.8) | collective-permute-done | bytes 612 | tf_op jit(solution)/shard_map/ppermute | solution.py:17
  51.7 3.2 %collective-permute-start.9 = (f32[145]{0:T(256)S(1)}, f32[145]{0:T(256)S(1)}, u32[]{:S(2)}, u32[]{:S(2)}) collective-permute-start(f32[145]{0:T(256)S(1)} %add.75), channel_id=1, source_target_pairs={{0,128},{32,160},{64,192},{96,224},{128,0},{160,32},{192,64},{224,... | collective-permute-start | bytes 1748 | tf_op jit(solution)/shard_map/ppermute | solution.py:17
  54.9 1.1 collective-permute-done.9
  56.0 4.8 %collective-permute-start.10 = (f32[145]{0:T(256)S(1)}, f32[145]{0:T(256)S(1)}, u32[]{:S(2)}, u32[]{:S(2)}) collective-permute-start(f32[145]{0:T(256)S(1)} %add.76), channel_id=1, source_target_pairs={{0,256},{32,288},{64,320},{96,352},{128,384},{160,416},{192,448},{... | collective-permute-start | bytes 1748 | tf_op jit(solution)/shard_map/ppermute | solution.py:17
  60.9 1.0 collective-permute-done.10
  61.8 5.4 %collective-permute-start.11 = (f32[145]{0:T(256)S(1)}, f32[145]{0:T(256)S(1)}, u32[]{:S(2)}, u32[]{:S(2)}) collective-permute-start(f32[145]{0:T(256)S(1)} %add.77), channel_id=1, source_target_pairs={{0,1},{1,0},{2,3},{3,2},{4,5},{5,4},{6,7},{7,6},{8,9},{9,8},{10,11... | collective-permute-start | bytes 1748 | tf_op jit(solution)/shard_map/ppermute | solution.py:17
  67.2 0.8 collective-permute-done.11
  68.0 1.9 %collective-permute-start.12 = (f32[145]{0:T(256)S(1)}, f32[145]{0:T(256)S(1)}, u32[]{:S(2)}, u32[]{:S(2)}) collective-permute-start(f32[145]{0:T(256)S(1)} %add.78), channel_id=1, source_target_pairs={{0,2},{1,3},{2,0},{3,1},{4,6},{5,7},{6,4},{7,5},{8,10},{9,11},{10,... | collective-permute-start | bytes 1748 | tf_op jit(solution)/shard_map/ppermute | solution.py:17
  69.9 2.4 %collective-permute-done.12 = f32[145]{0:T(256)S(1)} collective-permute-done((f32[145]{0:T(256)S(1)}, f32[145]{0:T(256)S(1)}, u32[]{:S(2)}, u32[]{:S(2)}) %collective-permute-start.12) | collective-permute-done | bytes 612 | tf_op jit(solution)/shard_map/ppermute | solution.py:17
  72.3 1.9 %collective-permute-start.13 = (f32[145]{0:T(256)S(1)}, f32[145]{0:T(256)S(1)}, u32[]{:S(2)}, u32[]{:S(2)}) collective-permute-start(f32[145]{0:T(256)S(1)} %add.79), channel_id=1, source_target_pairs={{0,4},{1,5},{2,6},{3,7},{4,0},{5,1},{6,2},{7,3},{8,12},{9,13},{10,... | collective-permute-start | bytes 1748 | tf_op jit(solution)/shard_map/ppermute | solution.py:17
  74.2 3.3 %collective-permute-done.13 = f32[145]{0:T(256)S(1)} collective-permute-done((f32[145]{0:T(256)S(1)}, f32[145]{0:T(256)S(1)}, u32[]{:S(2)}, u32[]{:S(2)}) %collective-permute-start.13) | collective-permute-done | bytes 612 | tf_op jit(solution)/shard_map/ppermute | solution.py:17
  77.5 1.9 %collective-permute-start.14 = (f32[145]{0:T(256)S(1)}, f32[145]{0:T(256)}, u32[]{:S(2)}, u32[]{:S(2)}) collective-permute-start(f32[145]{0:T(256)S(1)} %add.80), channel_id=1, source_target_pairs={{0,8},{1,9},{2,10},{3,11},{4,12},{5,13},{6,14},{7,15},{8,0},{9,1},... | collective-permute-start | bytes 1748 | tf_op jit(solution)/shard_map/ppermute | solution.py:17
  79.5 1.6 %concatenate.33 = bf16[1,144,256]{2,1,0:T(8,128)(2,1)} reshape(bf16[144,2,128]{2,1,0:T(2,128)(2,1)} %param.5) | data formatting | bytes 147456 | tf_op jit(solution)/shard_map/concatenate | solution.py:57
  81.0 4.8 %collective-permute-done.14 = f32[145]{0:T(256)} collective-permute-done((f32[145]{0:T(256)S(1)}, f32[145]{0:T(256)}, u32[]{:S(2)}, u32[]{:S(2)}) %collective-permute-start.14) | collective-permute-done | bytes 612 | tf_op jit(solution)/shard_map/ppermute | solution.py:17
  85.9 0.7 add.81
  86.5 6.0 %collective-permute-start.15 = (f32[145]{0:T(256)S(1)}, f32[145]{0:T(256)S(1)}, u32[]{:S(2)}, u32[]{:S(2)}) collective-permute-start(f32[145]{0:T(256)S(1)} %add.81), channel_id=1, source_target_pairs={{0,16},{1,17},{2,18},{3,19},{4,20},{5,21},{6,22},{7,23},{8,24},{9,... | collective-permute-start | bytes 1748 | tf_op jit(solution)/shard_map/ppermute | solution.py:17
  92.6 0.9 fusion.23
  93.5 6.1 %collective-permute-done.15 = f32[145]{0:T(256)S(1)} collective-permute-done((f32[145]{0:T(256)S(1)}, f32[145]{0:T(256)S(1)}, u32[]{:S(2)}, u32[]{:S(2)}) %collective-permute-start.15) | collective-permute-done | bytes 612 | tf_op jit(solution)/shard_map/ppermute | solution.py:17
  99.6 0.6 slice.174
  100.1 0.5 slice.179
  101.2 1.3 slice.184
  103.1 1.2 slice.189
  104.8 0.0 collective-permute-done.4
  104.8 0.6 slice.177
  105.4 0.5 slice.182
  105.9 0.5 slice.187
  106.5 0.6 slice.192
  109.7 0.9 fusion.18
  110.7 0.9 fusion.15
  111.6 0.0 copy-start.5
  111.6 0.7 fusion.2
  112.3 0.8 slice.194
  113.1 2.0 %concatenate.39 = f32[144,3,2,128]{3,2,1,0:T(2,128)} reshape(f32[144,768]{1,0:T(8,128)} %slice.194) | data formatting | bytes 884736 | tf_op jit(solution)/shard_map/concatenate | solution.py:75
  115.1 1.2 fusion.11
  116.3 0.0 copy-start.4
  116.3 0.2 multiply_add_fusion
  116.5 0.4 fusion.27
  116.9 4.8 %collective-permute-start.6 = (f32[145,2,2,2]{3,2,0,1:T(2,128)S(1)}, f32[145,2,2,2]{3,2,0,1:T(2,128)S(1)}, u32[]{:S(2)}, u32[]{:S(2)}) collective-permute-start(f32[145,2,2,2]{3,2,0,1:T(2,128)S(1)} %get-tuple-element.14), channel_id=1, source_target_pairs={{1,0},{2,1},{3,2},{4,3},{5,4},{6,5},{7,6},{8,7},{9,8},{10,9},{11,1... | collective-permute-start | bytes 13928 | tf_op jit(solution)/shard_map/ppermute | solution.py:32
  121.7 0.0 collective-permute-start.5
  121.7 0.6 slice_divide_fusion
  122.3 3.8 %collective-permute-done.6 = f32[145,2,2,2]{3,2,0,1:T(2,128)S(1)} collective-permute-done((f32[145,2,2,2]{3,2,0,1:T(2,128)S(1)}, f32[145,2,2,2]{3,2,0,1:T(2,128)S(1)}, u32[]{:S(2)}, u32[]{:S(2)}) %collective-permute-start.6) | collective-permute-done | bytes 4672 | tf_op jit(solution)/shard_map/ppermute | solution.py:32
  126.0 1.0 pad_maximum_fusion
  127.0 0.2 slice_bitcast_fusion.1
  127.3 1.1 fusion.8
  128.4 0.9 slice_add_fusion.2
  (28 shorter events, 0.2 us)
Async XLA Ops:
  0.0 111.6 %copy-start = (bf16[1,1,8,256,768]{4,3,2,1,0:T(8,128)(2,1)S(1)}, bf16[1,1,8,256,768]{4,3,2,1,0:T(8,128)(2,1)}, u32[]{:S(2)}) copy-start(bf16[1,1,8,256,768]{4,3,2,1,0:T(8,128)(2,1)} %param.8) | copy-start | bytes 9437188
  2.6 13.4 %collective-permute-start = (bf16[148,256]{1,0:T(8,128)(2,1)S(1)}, bf16[148,256]{1,0:T(8,128)(2,1)S(1)}, u32[]{:S(2)}, u32[]{:S(2)}) collective-permute-start(bf16[148,256]{1,0:T(8,128)(2,1)S(1)} %concatenate.38), channel_id=1, source_target_pairs={{0,30},{1,31},{2,0},{3,1},{4,2},{5,3},{6,4},{7,5},{8,6},{9,7},{10,... | collective-permute-start | bytes 227336 | tf_op jit(solution)/shard_map/ppermute | solution.py:9
  15.9 6.8 %collective-permute-start.1 = (bf16[148,256]{1,0:T(8,128)(2,1)S(1)}, bf16[148,256]{1,0:T(8,128)(2,1)S(1)}, u32[]{:S(2)}, u32[]{:S(2)}) collective-permute-start(bf16[148,256]{1,0:T(8,128)(2,1)S(1)} %collective-permute-done), channel_id=1, source_target_pairs={{0,30},{1,31},{2,0},{3,1},{4,2},{5,3},{6,4},{7,5},{8,6},{9,7},{10,... | collective-permute-start | bytes 227336 | tf_op jit(solution)/shard_map/ppermute | solution.py:9
  22.8 15.1 %copy-start.2 = (bf16[148,256]{1,0:T(8,128)(2,1)}, bf16[148,256]{1,0:T(8,128)(2,1)S(1)}, u32[]{:S(2)}) copy-start(bf16[148,256]{1,0:T(8,128)(2,1)S(1)} %collective-permute-done.1) | copy-start | bytes 227332
  22.8 5.8 %collective-permute-start.2 = (bf16[148,256]{1,0:T(8,128)(2,1)S(1)}, bf16[148,256]{1,0:T(8,128)(2,1)S(1)}, u32[]{:S(2)}, u32[]{:S(2)}) collective-permute-start(bf16[148,256]{1,0:T(8,128)(2,1)S(1)} %collective-permute-done.1), channel_id=1, source_target_pairs={{0,30},{1,31},{2,0},{3,1},{4,2},{5,3},{6,4},{7,5},{8,6},{9,7},{10,... | collective-permute-start | bytes 227336 | tf_op jit(solution)/shard_map/ppermute | solution.py:9
  28.6 9.3 %copy-start.3 = (bf16[148,256]{1,0:T(8,128)(2,1)}, bf16[148,256]{1,0:T(8,128)(2,1)S(1)}, u32[]{:S(2)}) copy-start(bf16[148,256]{1,0:T(8,128)(2,1)S(1)} %collective-permute-done.2) | copy-start | bytes 227332
  28.6 9.2 %collective-permute-start.3 = (bf16[148,256]{1,0:T(8,128)(2,1)S(1)}, bf16[148,256]{1,0:T(8,128)(2,1)S(1)}, u32[]{:S(2)}, u32[]{:S(2)}) collective-permute-start(bf16[148,256]{1,0:T(8,128)(2,1)S(1)} %collective-permute-done.2), channel_id=1, source_target_pairs={{0,30},{1,31},{2,0},{3,1},{4,2},{5,3},{6,4},{7,5},{8,6},{9,7},{10,... | collective-permute-start | bytes 227336 | tf_op jit(solution)/shard_map/ppermute | solution.py:9
  34.7 10.5 %collective-permute-start.7 = (f32[145]{0:T(256)}, f32[145]{0:T(256)S(1)}, u32[]{:S(2)}, u32[]{:S(2)}) collective-permute-start(f32[145]{0:T(256)} %pad_maximum_fusion.2), channel_id=1, source_target_pairs={{0,32},{32,0},{64,96},{96,64},{128,160},{160,128},{192,224},{224,1... | collective-permute-start | bytes 1748 | tf_op jit(solution)/shard_map/ppermute | solution.py:17
  38.7 66.1 %collective-permute-start.4 = (bf16[4,148,256]{2,1,0:T(8,128)(2,1)}, bf16[4,148,256]{2,1,0:T(8,128)(2,1)S(1)}, u32[]{:S(2)}, u32[]{:S(2)}) collective-permute-start(bf16[4,148,256]{2,1,0:T(8,128)(2,1)} %maximum_select_fusion), channel_id=1, source_target_pairs={{0,1},{1,0},{2,3},{3,2},{4,5},{5,4},{6,7},{7,6},{8,9},{9,8},{10,11... | collective-permute-start | bytes 909320 | tf_op jit(solution)/shard_map/ppermute | solution.py:64
  45.9 5.8 %collective-permute-start.8 = (f32[145]{0:T(256)S(1)}, f32[145]{0:T(256)S(1)}, u32[]{:S(2)}, u32[]{:S(2)}) collective-permute-start(f32[145]{0:T(256)S(1)} %fusion.29), channel_id=1, source_target_pairs={{0,64},{32,96},{64,0},{96,32},{128,192},{160,224},{192,128},{224,1... | collective-permute-start | bytes 1748 | tf_op jit(solution)/shard_map/ppermute | solution.py:17
  51.7 4.3 %collective-permute-start.9 = (f32[145]{0:T(256)S(1)}, f32[145]{0:T(256)S(1)}, u32[]{:S(2)}, u32[]{:S(2)}) collective-permute-start(f32[145]{0:T(256)S(1)} %add.75), channel_id=1, source_target_pairs={{0,128},{32,160},{64,192},{96,224},{128,0},{160,32},{192,64},{224,... | collective-permute-start | bytes 1748 | tf_op jit(solution)/shard_map/ppermute | solution.py:17
  56.0 5.8 %collective-permute-start.10 = (f32[145]{0:T(256)S(1)}, f32[145]{0:T(256)S(1)}, u32[]{:S(2)}, u32[]{:S(2)}) collective-permute-start(f32[145]{0:T(256)S(1)} %add.76), channel_id=1, source_target_pairs={{0,256},{32,288},{64,320},{96,352},{128,384},{160,416},{192,448},{... | collective-permute-start | bytes 1748 | tf_op jit(solution)/shard_map/ppermute | solution.py:17
  61.8 6.2 %collective-permute-start.11 = (f32[145]{0:T(256)S(1)}, f32[145]{0:T(256)S(1)}, u32[]{:S(2)}, u32[]{:S(2)}) collective-permute-start(f32[145]{0:T(256)S(1)} %add.77), channel_id=1, source_target_pairs={{0,1},{1,0},{2,3},{3,2},{4,5},{5,4},{6,7},{7,6},{8,9},{9,8},{10,11... | collective-permute-start | bytes 1748 | tf_op jit(solution)/shard_map/ppermute | solution.py:17
  68.0 4.3 %collective-permute-start.12 = (f32[145]{0:T(256)S(1)}, f32[145]{0:T(256)S(1)}, u32[]{:S(2)}, u32[]{:S(2)}) collective-permute-start(f32[145]{0:T(256)S(1)} %add.78), channel_id=1, source_target_pairs={{0,2},{1,3},{2,0},{3,1},{4,6},{5,7},{6,4},{7,5},{8,10},{9,11},{10,... | collective-permute-start | bytes 1748 | tf_op jit(solution)/shard_map/ppermute | solution.py:17
  72.3 5.2 %collective-permute-start.13 = (f32[145]{0:T(256)S(1)}, f32[145]{0:T(256)S(1)}, u32[]{:S(2)}, u32[]{:S(2)}) collective-permute-start(f32[145]{0:T(256)S(1)} %add.79), channel_id=1, source_target_pairs={{0,4},{1,5},{2,6},{3,7},{4,0},{5,1},{6,2},{7,3},{8,12},{9,13},{10,... | collective-permute-start | bytes 1748 | tf_op jit(solution)/shard_map/ppermute | solution.py:17
  77.5 8.3 %collective-permute-start.14 = (f32[145]{0:T(256)S(1)}, f32[145]{0:T(256)}, u32[]{:S(2)}, u32[]{:S(2)}) collective-permute-start(f32[145]{0:T(256)S(1)} %add.80), channel_id=1, source_target_pairs={{0,8},{1,9},{2,10},{3,11},{4,12},{5,13},{6,14},{7,15},{8,0},{9,1},... | collective-permute-start | bytes 1748 | tf_op jit(solution)/shard_map/ppermute | solution.py:17
  86.5 13.0 %collective-permute-start.15 = (f32[145]{0:T(256)S(1)}, f32[145]{0:T(256)S(1)}, u32[]{:S(2)}, u32[]{:S(2)}) collective-permute-start(f32[145]{0:T(256)S(1)} %add.81), channel_id=1, source_target_pairs={{0,16},{1,17},{2,18},{3,19},{4,20},{5,21},{6,22},{7,23},{8,24},{9,... | collective-permute-start | bytes 1748 | tf_op jit(solution)/shard_map/ppermute | solution.py:17
  111.6 4.7 %copy-start.5 = (f32[2]{0:T(128)S(1)}, f32[2]{0:T(128)}, u32[]{:S(2)}) copy-start(f32[2]{0:T(128)} %constant.51.clone) | copy-start | bytes 28
  115.1 12.1 %copy-start.1 = (f32[144,3,2,128]{3,2,1,0:T(2,128)S(1)}, f32[144,3,2,128]{3,2,1,0:T(2,128)}, u32[]{:S(2)}) copy-start(f32[144,3,2,128]{3,2,1,0:T(2,128)} %concatenate.39) | copy-start | bytes 1327108
  116.3 12.1 %copy-start.4 = (f32[2,128]{1,0:T(2,128)S(1)}, f32[2,128]{1,0:T(2,128)}, u32[]{:S(2)}) copy-start(f32[2,128]{1,0:T(2,128)} %param.6) | copy-start | bytes 3076
  116.9 9.2 %collective-permute-start.6 = (f32[145,2,2,2]{3,2,0,1:T(2,128)S(1)}, f32[145,2,2,2]{3,2,0,1:T(2,128)S(1)}, u32[]{:S(2)}, u32[]{:S(2)}) collective-permute-start(f32[145,2,2,2]{3,2,0,1:T(2,128)S(1)} %get-tuple-element.14), channel_id=1, source_target_pairs={{1,0},{2,1},{3,2},{4,3},{5,4},{6,5},{7,6},{8,7},{9,8},{10,9},{11,1... | collective-permute-start | bytes 13928 | tf_op jit(solution)/shard_map/ppermute | solution.py:32
  121.7 4.4 %collective-permute-start.5 = (f32[145,2,2,2]{3,2,0,1:T(2,128)S(1)}, f32[145,2,2,2]{3,2,0,1:T(2,128)S(1)}, u32[]{:S(2)}, u32[]{:S(2)}) collective-permute-start(f32[145,2,2,2]{3,2,0,1:T(2,128)S(1)} %get-tuple-element.13), channel_id=1, source_target_pairs={{0,1},{1,2},{2,3},{3,4},{4,5},{5,6},{6,7},{7,8},{8,9},{9,10},{10,1... | collective-permute-start | bytes 13928 | tf_op jit(solution)/shard_map/ppermute | solution.py:29

commit v4 on v3

--- a/solution.py
+++ b/solution.py
@@ -49,31 +49,31 @@
     cot_full = cotangent.astype(jnp.float32)
     weighted = jnp.sum(cot_full * cell_area[None], axis=(1, 2))
     squares = jnp.sum(cell_area * cell_area)
-    stats = butterfly_sum(jnp.concatenate([weighted, squares[None]]), ("lat", "lon"))
+    stats, area_late = lax.optimization_barrier((jnp.concatenate([weighted, squares[None]]), cell_area))
+    stats = butterfly_sum(stats, ("lat", "lon"))
     factor = stats[:fields] / stats[fields]
 
     area_parts = split_bf16(cell_area.reshape(1, cell_count))
     count_row = jnp.full((1, cell_count), reach_count[0, 0], jnp.float32).astype(jnp.bfloat16)
     payload = jnp.concatenate([cotangent.reshape(fields, cell_count)] + area_parts + [count_row], axis=0)
+    payload = lax.optimization_barrier(payload)
     ring = [payload]
     for _ in range(slot_count // 2):
         ring.append(shifted(ring[-1], "lon", -2))
     odd = lax.axis_index("lon") % 2 == 1
     half = slot_count // 2
-    offer = jnp.where(odd, jnp.stack(ring[:half]), jnp.stack(ring[1 : half + 1]))
+    offer = jnp.stack([jnp.where(odd, ring[k], ring[k + 1]) for k in range(half)])
+    offer = lax.optimization_barrier(offer)
     swapped = lax.ppermute(offer, "lon", [(i, i ^ 1) for i in range(lax.axis_size("lon"))])
-    tiles = []
-    for slot_index in range(slot_count):
-        tile = ring[slot_index // 2] if slot_index % 2 == 0 else swapped[slot_index // 2]
-        live = tile[fields + 3, 0].astype(jnp.float32) > slot_index
-        tiles.append(jnp.where(live, tile[: fields + 3], jnp.zeros_like(tile[: fields + 3])))
-    stacked = jnp.stack(tiles)
+    pairs = jnp.stack([jnp.stack(ring[:half]), swapped], axis=1)
+    stacked = pairs.reshape(slot_count, fields + 4, cell_count)
+    counts = stacked[:, fields + 3, 0].astype(jnp.float32)
+    live = counts > jnp.arange(slot_count, dtype=jnp.float32)
+    stacked = jnp.where(live[:, None, None], stacked, jnp.zeros_like(stacked))
     moments = lax.dot_general(
         stacked, weights[0, 0], (((0, 2), (0, 1)), ((), ())), preferred_element_type=jnp.float32
     )
-    area_moments = moments[fields] + moments[fields + 1] + moments[fields + 2]
-    moments = jnp.concatenate([moments[:fields], area_moments[None]], axis=0)
-    moments = moments.reshape(fields + 1, 3, tile_rows, tile_cols)
+    moments = moments.reshape(fields + 4, 3, tile_rows, tile_cols)
     mean_adj = moments[:, 0]
     curv_adj = moments[:, 2]
     signs = jnp.array([-3.0, 3.0], jnp.float32)[None, :, None, None]
@@ -94,7 +94,8 @@
         - right_pad[..., 1 : tile_cols + 1]
     )
     stencil = mean_adj + 6.0 * curv_adj + 7.0 / 12.0 * near - 1.0 / 12.0 * far
-    return stencil[:fields] + factor[:, None, None] * (cell_area[None] - stencil[fields][None])
+    area_stencil = stencil[fields] + stencil[fields + 1] + stencil[fields + 2]
+    return stencil[:fields] + factor[:, None, None] * (area_late[None] - area_stencil[None])
 
 
 def solution(mesh):

time: 132 us -> 122 us (0.924)
  starting transfers between devices: 70.1 us -> 75.7 us
  other arithmetic: 15.1 us -> 10.3 us
  between operations: 5.48 us -> 0.96 us
  local copies, waits for them, and re-layouts: 11.6 us -> 8.33 us
  waiting for transfers between devices: 26.3 us -> 23.9 us
    slice x8 -> x0, local copies, waits for them, and re-layouts: 5.92 us -> none  [the longest x7 5.14 us: on_device_body(): live = tile[fields + 3, 0].astype(jnp.float32) > slot_index]
    dot_general x0 -> x1, local copies, waits for them, and re-layouts: none -> 5.72 us  [on_device_body(): lax.dot_general(stacked, weights[0, 0], (((0, 2), (0, 1)), ((), ())), pre...]
    ppermute x9, waiting for transfers between devices: 20.9 us -> 15.4 us  [butterfly_sum(): partner = lax.ppermute(value, axis, [(i, i ^ step) for i in range(length)])]
    ppermute x9, starting transfers between devices: 32.6 us -> 37.4 us  [butterfly_sum(): partner = lax.ppermute(value, axis, [(i, i ^ step) for i in range(length)])]
    unnamed x7 -> x0, other arithmetic: 2.81 us -> none
    another operation x1 -> x4, other arithmetic: 0.02 us -> 2.82 us  [the longest x2 2.03 us: on_device_body(): pairs = jnp.stack([jnp.stack(ring[:half]), swapped], axis=1)]
    ppermute x4, waiting for transfers between devices: 1.6 us -> 4.27 us  [shifted(): lax.ppermute(value, axis, [(i, (i + by) % length) for i in range(length)])]
    concatenate x1 -> x0, local copies, waits for them, and re-layouts: 2 us -> none  [on_device_body(): moments = jnp.concatenate([moments[:fields], area_moments[None]], axis=0)]
  transfers between devices with their start and end apart: 16 -> 16, of which waited for: 11 -> 12; matrix products, arithmetic and copies ran while one was open for 10% -> 10% of each run, Pallas kernels for 0% -> 0%
where the time goes in v4:
time: 122 us; the launch traced here: 120 us
  starting transfers between devices  75.7 us (62%)
  waiting for transfers between devices  23.9 us (20%)
  other arithmetic  10.3 us (8%)
  local copies, waits for them, and re-layouts  8.33 us (7%)
    ppermute x9, starting transfers between devices, butterfly_sum(): partner = lax.ppermute(value, axis, [(i, i ^ step) for i in range(length)])  37.4 us
    ppermute x4, starting transfers between devices, shifted(): lax.ppermute(value, axis, [(i, (i + by) % length) for i in range(length)])  26.7 us
    ppermute x9, waiting for transfers between devices, butterfly_sum(): partner = lax.ppermute(value, axis, [(i, i ^ step) for i in range(length)])  15.4 us
    ppermute x1, starting transfers between devices, on_device_body(): lax.ppermute(offer, 'lon', [(i, i ^ 1) for i in range(lax.axis_size('lon'...  6.38 us
    dot_general x1, local copies, waits for them, and re-layouts, on_device_body(): lax.dot_general(stacked, weights[0, 0], (((0, 2), (0, 1)), ((), ())), pre...  5.72 us
    ppermute x1, starting transfers between devices, padded_2(): lax.ppermute(lax.slice_in_dim(block, 0, width, axis=dim), axis, backward)  4.56 us
    ppermute x4, waiting for transfers between devices, shifted(): lax.ppermute(value, axis, [(i, (i + by) % length) for i in range(length)])  4.27 us
    ppermute x1, waiting for transfers between devices, padded_2(): lax.ppermute(lax.slice_in_dim(block, 0, width, axis=dim), axis, backward)  4.21 us
  transfers between devices with their start and end apart: 16, of which 12 were waited for; matrix products, arithmetic and copies ran while one was open for 10% of the time, Pallas kernels for 0%

profile of v4, /device:TPU:1, one launch (start us, length us, event | category | flops | bytes accessed | tf_op | source)
XLA Modules:
  0.0 119.8 jit_solution(9520301784901167349)
XLA Ops:
  0.0 0.9 copy.25
  0.9 0.7 fusion.10
  2.3 11.9 %collective-permute-start = (bf16[148,256]{1,0:T(8,128)(2,1)S(1)}, bf16[148,256]{1,0:T(8,128)(2,1)S(1)}, u32[]{:S(2)}, u32[]{:S(2)}) collective-permute-start(bf16[148,256]{1,0:T(8,128)(2,1)S(1)} %concatenate.9), channel_id=1, source_target_pairs={{0,30},{1,31},{2,0},{3,1},{4,2},{5,3},{6,4},{7,5},{8,6},{9,7},{10,... | collective-permute-start | bytes 227336 | tf_op jit(solution)/shard_map/ppermute | solution.py:9
  14.2 1.4 %collective-permute-done = bf16[148,256]{1,0:T(8,128)(2,1)S(1)} collective-permute-done((bf16[148,256]{1,0:T(8,128)(2,1)S(1)}, bf16[148,256]{1,0:T(8,128)(2,1)S(1)}, u32[]{:S(2)}, u32[]{:S(2)}) %collective-permute-start) | collective-permute-done | bytes 75808 | tf_op jit(solution)/shard_map/ppermute | solution.py:9
  15.7 0.0 copy-start
  15.7 4.9 %collective-permute-start.1 = (bf16[148,256]{1,0:T(8,128)(2,1)S(1)}, bf16[148,256]{1,0:T(8,128)(2,1)S(1)}, u32[]{:S(2)}, u32[]{:S(2)}) collective-permute-start(bf16[148,256]{1,0:T(8,128)(2,1)S(1)} %collective-permute-done), channel_id=1, source_target_pairs={{0,30},{1,31},{2,0},{3,1},{4,2},{5,3},{6,4},{7,5},{8,6},{9,7},{10,... | collective-permute-start | bytes 227336 | tf_op jit(solution)/shard_map/ppermute | solution.py:9
  20.6 1.4 %collective-permute-done.1 = bf16[148,256]{1,0:T(8,128)(2,1)S(1)} collective-permute-done((bf16[148,256]{1,0:T(8,128)(2,1)S(1)}, bf16[148,256]{1,0:T(8,128)(2,1)S(1)}, u32[]{:S(2)}, u32[]{:S(2)}) %collective-permute-start.1) | collective-permute-done | bytes 75808 | tf_op jit(solution)/shard_map/ppermute | solution.py:9
  22.0 0.0 copy-start.1
  22.0 4.9 %collective-permute-start.2 = (bf16[148,256]{1,0:T(8,128)(2,1)S(1)}, bf16[148,256]{1,0:T(8,128)(2,1)S(1)}, u32[]{:S(2)}, u32[]{:S(2)}) collective-permute-start(bf16[148,256]{1,0:T(8,128)(2,1)S(1)} %collective-permute-done.1), channel_id=1, source_target_pairs={{0,30},{1,31},{2,0},{3,1},{4,2},{5,3},{6,4},{7,5},{8,6},{9,7},{10,... | collective-permute-start | bytes 227336 | tf_op jit(solution)/shard_map/ppermute | solution.py:9
  26.9 1.4 %collective-permute-done.2 = bf16[148,256]{1,0:T(8,128)(2,1)S(1)} collective-permute-done((bf16[148,256]{1,0:T(8,128)(2,1)S(1)}, bf16[148,256]{1,0:T(8,128)(2,1)S(1)}, u32[]{:S(2)}, u32[]{:S(2)}) %collective-permute-start.2) | collective-permute-done | bytes 75808 | tf_op jit(solution)/shard_map/ppermute | solution.py:9
  28.3 0.0 copy-start.2
  28.3 4.9 %collective-permute-start.3 = (bf16[148,256]{1,0:T(8,128)(2,1)S(1)}, bf16[148,256]{1,0:T(8,128)(2,1)S(1)}, u32[]{:S(2)}, u32[]{:S(2)}) collective-permute-start(bf16[148,256]{1,0:T(8,128)(2,1)S(1)} %collective-permute-done.2), channel_id=1, source_target_pairs={{0,30},{1,31},{2,0},{3,1},{4,2},{5,3},{6,4},{7,5},{8,6},{9,7},{10,... | collective-permute-start | bytes 227336 | tf_op jit(solution)/shard_map/ppermute | solution.py:9
  33.3 1.9 %multiply_reduce_fusion = f32[144]{0:T(256)S(1)} fusion(bf16[144,2,128]{2,1,0:T(2,128)(2,1)} %param.5, f32[2,128]{1,0:T(2,128)} %param.6), kind=kLoop, calls=%fused_computation.26 | loop fusion | flops 110448 | bytes 75328 | tf_op jit(solution)/shard_map/reduce_sum | solution.py:50
  35.2 0.0 collective-permute-done.3
  35.2 0.8 pad_maximum_fusion.2
  36.0 6.4 %collective-permute-start.4 = (bf16[4,148,256]{2,1,0:T(8,128)(2,1)}, bf16[4,148,256]{2,1,0:T(8,128)(2,1)}, u32[]{:S(2)}, u32[]{:S(2)}) collective-permute-start(bf16[4,148,256]{2,1,0:T(8,128)(2,1)} %pad_maximum_fusion.2), channel_id=1, source_target_pairs={{0,1},{1,0},{2,3},{3,2},{4,5},{5,4},{6,7},{7,6},{8,9},{9,8},{10,11... | collective-permute-start | bytes 909320 | tf_op jit(solution)/shard_map/ppermute | solution.py:67
  42.4 1.3 %multiply_reduce_fusion.1 = f32[]{:T(128)} fusion(f32[2,128]{1,0:T(2,128)} %param.6), kind=kLoop, calls=%fused_computation.43 | loop fusion | flops 511 | bytes 1028 | tf_op jit(solution)/shard_map/reduce_sum | solution.py:51
  43.7 0.7 pad_maximum_fusion.3
  44.4 3.1 %collective-permute-start.7 = (f32[145]{0:T(256)S(1)}, f32[145]{0:T(256)S(1)}, u32[]{:S(2)}, u32[]{:S(2)}) collective-permute-start(f32[145]{0:T(256)S(1)} %pad_maximum_fusion.3), channel_id=1, source_target_pairs={{0,32},{32,0},{64,96},{96,64},{128,160},{160,128},{192,224},{224,1... | collective-permute-start | bytes 1748 | tf_op jit(solution)/shard_map/ppermute | solution.py:17
  47.5 1.2 collective-permute-done.7
  48.7 4.6 %collective-permute-start.8 = (f32[145]{0:T(256)S(1)}, f32[145]{0:T(256)S(1)}, u32[]{:S(2)}, u32[]{:S(2)}) collective-permute-start(f32[145]{0:T(256)S(1)} %add.74), channel_id=1, source_target_pairs={{0,64},{32,96},{64,0},{96,32},{128,192},{160,224},{192,128},{224,1... | collective-permute-start | bytes 1748 | tf_op jit(solution)/shard_map/ppermute | solution.py:17
  53.3 1.2 collective-permute-done.8
  54.5 3.2 %collective-permute-start.9 = (f32[145]{0:T(256)S(1)}, f32[145]{0:T(256)S(1)}, u32[]{:S(2)}, u32[]{:S(2)}) collective-permute-start(f32[145]{0:T(256)S(1)} %add.75), channel_id=1, source_target_pairs={{0,128},{32,160},{64,192},{96,224},{128,0},{160,32},{192,64},{224,... | collective-permute-start | bytes 1748 | tf_op jit(solution)/shard_map/ppermute | solution.py:17
  57.7 1.1 collective-permute-done.9
  58.8 4.8 %collective-permute-start.10 = (f32[145]{0:T(256)S(1)}, f32[145]{0:T(256)S(1)}, u32[]{:S(2)}, u32[]{:S(2)}) collective-permute-start(f32[145]{0:T(256)S(1)} %add.76), channel_id=1, source_target_pairs={{0,256},{32,288},{64,320},{96,352},{128,384},{160,416},{192,448},{... | collective-permute-start | bytes 1748 | tf_op jit(solution)/shard_map/ppermute | solution.py:17
  63.6 1.0 collective-permute-done.10
  64.6 6.5 %collective-permute-start.11 = (f32[145]{0:T(256)S(1)}, f32[145]{0:T(256)S(1)}, u32[]{:S(2)}, u32[]{:S(2)}) collective-permute-start(f32[145]{0:T(256)S(1)} %add.77), channel_id=1, source_target_pairs={{0,1},{1,0},{2,3},{3,2},{4,5},{5,4},{6,7},{7,6},{8,9},{9,8},{10,11... | collective-permute-start | bytes 1748 | tf_op jit(solution)/shard_map/ppermute | solution.py:17
  71.1 0.8 collective-permute-done.11
  71.9 1.9 %collective-permute-start.12 = (f32[145]{0:T(256)S(1)}, f32[145]{0:T(256)S(1)}, u32[]{:S(2)}, u32[]{:S(2)}) collective-permute-start(f32[145]{0:T(256)S(1)} %add.78), channel_id=1, source_target_pairs={{0,2},{1,3},{2,0},{3,1},{4,6},{5,7},{6,4},{7,5},{8,10},{9,11},{10,... | collective-permute-start | bytes 1748 | tf_op jit(solution)/shard_map/ppermute | solution.py:17
  73.9 2.4 %collective-permute-done.12 = f32[145]{0:T(256)S(1)} collective-permute-done((f32[145]{0:T(256)S(1)}, f32[145]{0:T(256)S(1)}, u32[]{:S(2)}, u32[]{:S(2)}) %collective-permute-start.12) | collective-permute-done | bytes 612 | tf_op jit(solution)/shard_map/ppermute | solution.py:17
  76.3 1.9 %collective-permute-start.13 = (f32[145]{0:T(256)S(1)}, f32[145]{0:T(256)S(1)}, u32[]{:S(2)}, u32[]{:S(2)}) collective-permute-start(f32[145]{0:T(256)S(1)} %add.79), channel_id=1, source_target_pairs={{0,4},{1,5},{2,6},{3,7},{4,0},{5,1},{6,2},{7,3},{8,12},{9,13},{10,... | collective-permute-start | bytes 1748 | tf_op jit(solution)/shard_map/ppermute | solution.py:17
  78.2 3.3 %collective-permute-done.13 = f32[145]{0:T(256)S(1)} collective-permute-done((f32[145]{0:T(256)S(1)}, f32[145]{0:T(256)S(1)}, u32[]{:S(2)}, u32[]{:S(2)}) %collective-permute-start.13) | collective-permute-done | bytes 612 | tf_op jit(solution)/shard_map/ppermute | solution.py:17
  81.5 3.7 %collective-permute-start.14 = (f32[145]{0:T(256)S(1)}, f32[145]{0:T(256)S(1)}, u32[]{:S(2)}, u32[]{:S(2)}) collective-permute-start(f32[145]{0:T(256)S(1)} %add.80), channel_id=1, source_target_pairs={{0,8},{1,9},{2,10},{3,11},{4,12},{5,13},{6,14},{7,15},{8,0},{9,1},... | collective-permute-start | bytes 1748 | tf_op jit(solution)/shard_map/ppermute | solution.py:17
  85.2 4.5 %collective-permute-done.14 = f32[145]{0:T(256)S(1)} collective-permute-done((f32[145]{0:T(256)S(1)}, f32[145]{0:T(256)S(1)}, u32[]{:S(2)}, u32[]{:S(2)}) %collective-permute-start.14) | collective-permute-done | bytes 612 | tf_op jit(solution)/shard_map/ppermute | solution.py:17
  89.7 7.6 %collective-permute-start.15 = (f32[145]{0:T(256)S(1)}, f32[145]{0:T(256)S(1)}, u32[]{:S(2)}, u32[]{:S(2)}) collective-permute-start(f32[145]{0:T(256)S(1)} %add.81), channel_id=1, source_target_pairs={{0,16},{1,17},{2,18},{3,19},{4,20},{5,21},{6,22},{7,23},{8,24},{9,... | collective-permute-start | bytes 1748 | tf_op jit(solution)/shard_map/ppermute | solution.py:17
  97.3 5.7 %dot_general.8 = bf16[3,2,128,8,256]{2,1,0,4,3:T(2,128)(2,1)S(1)} reshape(bf16[768,8,256]{0,2,1:T(8,128)(2,1)} %bitcast.57) | data formatting | bytes 6291456 | tf_op jit(solution)/shard_map/dot_general | solution.py:73
  103.1 0.0 copy-done
  103.1 0.0 collective-permute-done.15
  103.1 0.6 slice.85
  103.7 0.0 copy-done.1
  103.7 0.0 copy-done.2
  103.7 1.0 maximum_bitcast_fusion
  104.7 0.0 collective-permute-done.4
  104.7 1.0 pad_maximum_fusion
  105.8 0.2 compare_reduce_fusion
  106.0 0.1 broadcast_in_dim.26
  106.1 1.1 broadcast_select_fusion
  107.2 0.0 copy-start.4
  107.2 0.7 fusion.2
  107.9 0.0 copy-done.4
  107.9 0.0 copy-start.3
  108.0 0.1 multiply_add_fusion
  108.1 0.2 fusion.11
  108.2 4.6 %collective-permute-start.6 = (f32[148,2,2,2]{3,0,2,1:T(8,128)S(1)}, f32[148,2,2,2]{3,0,2,1:T(8,128)S(1)}, u32[]{:S(2)}, u32[]{:S(2)}) collective-permute-start(f32[148,2,2,2]{3,0,2,1:T(8,128)S(1)} %get-tuple-element.14), channel_id=1, source_target_pairs={{1,0},{2,1},{3,2},{4,3},{5,4},{6,5},{7,6},{8,7},{9,8},{10,9},{11,1... | collective-permute-start | bytes 14216 | tf_op jit(solution)/shard_map/ppermute | solution.py:32
  112.8 0.6 collective-permute-start.5
  113.4 0.6 slice_divide_fusion
  114.0 4.2 %collective-permute-done.6 = f32[148,2,2,2]{3,0,2,1:T(8,128)S(1)} collective-permute-done((f32[148,2,2,2]{3,0,2,1:T(8,128)S(1)}, f32[148,2,2,2]{3,0,2,1:T(8,128)S(1)}, u32[]{:S(2)}, u32[]{:S(2)}) %collective-permute-start.6) | collective-permute-done | bytes 4768 | tf_op jit(solution)/shard_map/ppermute | solution.py:32
  118.2 0.0 collective-permute-done.5
  118.2 0.3 pad_maximum_fusion.1
  118.6 0.3 fusion.6
  119.0 0.0 copy-done.3
  119.0 0.1 slice_add_fusion.2
  119.1 0.7 copy.16
  (16 shorter events, 0.2 us)
Async XLA Ops:
  2.3 13.4 %collective-permute-start = (bf16[148,256]{1,0:T(8,128)(2,1)S(1)}, bf16[148,256]{1,0:T(8,128)(2,1)S(1)}, u32[]{:S(2)}, u32[]{:S(2)}) collective-permute-start(bf16[148,256]{1,0:T(8,128)(2,1)S(1)} %concatenate.9), channel_id=1, source_target_pairs={{0,30},{1,31},{2,0},{3,1},{4,2},{5,3},{6,4},{7,5},{8,6},{9,7},{10,... | collective-permute-start | bytes 227336 | tf_op jit(solution)/shard_map/ppermute | solution.py:9
  15.7 87.4 %copy-start = (bf16[148,256]{1,0:T(8,128)(2,1)}, bf16[148,256]{1,0:T(8,128)(2,1)S(1)}, u32[]{:S(2)}) copy-start(bf16[148,256]{1,0:T(8,128)(2,1)S(1)} %collective-permute-done) | copy-start | bytes 227332
  15.7 6.3 %collective-permute-start.1 = (bf16[148,256]{1,0:T(8,128)(2,1)S(1)}, bf16[148,256]{1,0:T(8,128)(2,1)S(1)}, u32[]{:S(2)}, u32[]{:S(2)}) collective-permute-start(bf16[148,256]{1,0:T(8,128)(2,1)S(1)} %collective-permute-done), channel_id=1, source_target_pairs={{0,30},{1,31},{2,0},{3,1},{4,2},{5,3},{6,4},{7,5},{8,6},{9,7},{10,... | collective-permute-start | bytes 227336 | tf_op jit(solution)/shard_map/ppermute | solution.py:9
  22.0 81.7 %copy-start.1 = (bf16[148,256]{1,0:T(8,128)(2,1)}, bf16[148,256]{1,0:T(8,128)(2,1)S(1)}, u32[]{:S(2)}) copy-start(bf16[148,256]{1,0:T(8,128)(2,1)S(1)} %collective-permute-done.1) | copy-start | bytes 227332
  22.0 6.3 %collective-permute-start.2 = (bf16[148,256]{1,0:T(8,128)(2,1)S(1)}, bf16[148,256]{1,0:T(8,128)(2,1)S(1)}, u32[]{:S(2)}, u32[]{:S(2)}) collective-permute-start(bf16[148,256]{1,0:T(8,128)(2,1)S(1)} %collective-permute-done.1), channel_id=1, source_target_pairs={{0,30},{1,31},{2,0},{3,1},{4,2},{5,3},{6,4},{7,5},{8,6},{9,7},{10,... | collective-permute-start | bytes 227336 | tf_op jit(solution)/shard_map/ppermute | solution.py:9
  28.3 75.4 %copy-start.2 = (bf16[148,256]{1,0:T(8,128)(2,1)}, bf16[148,256]{1,0:T(8,128)(2,1)S(1)}, u32[]{:S(2)}) copy-start(bf16[148,256]{1,0:T(8,128)(2,1)S(1)} %collective-permute-done.2) | copy-start | bytes 227332
  28.3 6.8 %collective-permute-start.3 = (bf16[148,256]{1,0:T(8,128)(2,1)S(1)}, bf16[148,256]{1,0:T(8,128)(2,1)S(1)}, u32[]{:S(2)}, u32[]{:S(2)}) collective-permute-start(bf16[148,256]{1,0:T(8,128)(2,1)S(1)} %collective-permute-done.2), channel_id=1, source_target_pairs={{0,30},{1,31},{2,0},{3,1},{4,2},{5,3},{6,4},{7,5},{8,6},{9,7},{10,... | collective-permute-start | bytes 227336 | tf_op jit(solution)/shard_map/ppermute | solution.py:9
  36.0 68.8 %collective-permute-start.4 = (bf16[4,148,256]{2,1,0:T(8,128)(2,1)}, bf16[4,148,256]{2,1,0:T(8,128)(2,1)}, u32[]{:S(2)}, u32[]{:S(2)}) collective-permute-start(bf16[4,148,256]{2,1,0:T(8,128)(2,1)} %pad_maximum_fusion.2), channel_id=1, source_target_pairs={{0,1},{1,0},{2,3},{3,2},{4,5},{5,4},{6,7},{7,6},{8,9},{9,8},{10,11... | collective-permute-start | bytes 909320 | tf_op jit(solution)/shard_map/ppermute | solution.py:67
  44.4 4.3 %collective-permute-start.7 = (f32[145]{0:T(256)S(1)}, f32[145]{0:T(256)S(1)}, u32[]{:S(2)}, u32[]{:S(2)}) collective-permute-start(f32[145]{0:T(256)S(1)} %pad_maximum_fusion.3), channel_id=1, source_target_pairs={{0,32},{32,0},{64,96},{96,64},{128,160},{160,128},{192,224},{224,1... | collective-permute-start | bytes 1748 | tf_op jit(solution)/shard_map/ppermute | solution.py:17
  48.7 5.8 %collective-permute-start.8 = (f32[145]{0:T(256)S(1)}, f32[145]{0:T(256)S(1)}, u32[]{:S(2)}, u32[]{:S(2)}) collective-permute-start(f32[145]{0:T(256)S(1)} %add.74), channel_id=1, source_target_pairs={{0,64},{32,96},{64,0},{96,32},{128,192},{160,224},{192,128},{224,1... | collective-permute-start | bytes 1748 | tf_op jit(solution)/shard_map/ppermute | solution.py:17
  54.5 4.3 %collective-permute-start.9 = (f32[145]{0:T(256)S(1)}, f32[145]{0:T(256)S(1)}, u32[]{:S(2)}, u32[]{:S(2)}) collective-permute-start(f32[145]{0:T(256)S(1)} %add.75), channel_id=1, source_target_pairs={{0,128},{32,160},{64,192},{96,224},{128,0},{160,32},{192,64},{224,... | collective-permute-start | bytes 1748 | tf_op jit(solution)/shard_map/ppermute | solution.py:17
  58.8 5.8 %collective-permute-start.10 = (f32[145]{0:T(256)S(1)}, f32[145]{0:T(256)S(1)}, u32[]{:S(2)}, u32[]{:S(2)}) collective-permute-start(f32[145]{0:T(256)S(1)} %add.76), channel_id=1, source_target_pairs={{0,256},{32,288},{64,320},{96,352},{128,384},{160,416},{192,448},{... | collective-permute-start | bytes 1748 | tf_op jit(solution)/shard_map/ppermute | solution.py:17
  64.6 7.3 %collective-permute-start.11 = (f32[145]{0:T(256)S(1)}, f32[145]{0:T(256)S(1)}, u32[]{:S(2)}, u32[]{:S(2)}) collective-permute-start(f32[145]{0:T(256)S(1)} %add.77), channel_id=1, source_target_pairs={{0,1},{1,0},{2,3},{3,2},{4,5},{5,4},{6,7},{7,6},{8,9},{9,8},{10,11... | collective-permute-start | bytes 1748 | tf_op jit(solution)/shard_map/ppermute | solution.py:17
  71.9 4.3 %collective-permute-start.12 = (f32[145]{0:T(256)S(1)}, f32[145]{0:T(256)S(1)}, u32[]{:S(2)}, u32[]{:S(2)}) collective-permute-start(f32[145]{0:T(256)S(1)} %add.78), channel_id=1, source_target_pairs={{0,2},{1,3},{2,0},{3,1},{4,6},{5,7},{6,4},{7,5},{8,10},{9,11},{10,... | collective-permute-start | bytes 1748 | tf_op jit(solution)/shard_map/ppermute | solution.py:17
  76.3 5.2 %collective-permute-start.13 = (f32[145]{0:T(256)S(1)}, f32[145]{0:T(256)S(1)}, u32[]{:S(2)}, u32[]{:S(2)}) collective-permute-start(f32[145]{0:T(256)S(1)} %add.79), channel_id=1, source_target_pairs={{0,4},{1,5},{2,6},{3,7},{4,0},{5,1},{6,2},{7,3},{8,12},{9,13},{10,... | collective-permute-start | bytes 1748 | tf_op jit(solution)/shard_map/ppermute | solution.py:17
  81.5 8.2 %collective-permute-start.14 = (f32[145]{0:T(256)S(1)}, f32[145]{0:T(256)S(1)}, u32[]{:S(2)}, u32[]{:S(2)}) collective-permute-start(f32[145]{0:T(256)S(1)} %add.80), channel_id=1, source_target_pairs={{0,8},{1,9},{2,10},{3,11},{4,12},{5,13},{6,14},{7,15},{8,0},{9,1},... | collective-permute-start | bytes 1748 | tf_op jit(solution)/shard_map/ppermute | solution.py:17
  89.7 13.4 %collective-permute-start.15 = (f32[145]{0:T(256)S(1)}, f32[145]{0:T(256)S(1)}, u32[]{:S(2)}, u32[]{:S(2)}) collective-permute-start(f32[145]{0:T(256)S(1)} %add.81), channel_id=1, source_target_pairs={{0,16},{1,17},{2,18},{3,19},{4,20},{5,21},{6,22},{7,23},{8,24},{9,... | collective-permute-start | bytes 1748 | tf_op jit(solution)/shard_map/ppermute | solution.py:17
  107.2 0.7 copy-start.4
  107.9 11.0 %copy-start.3 = (f32[2,128]{1,0:T(2,128)S(1)}, f32[2,128]{1,0:T(2,128)}, u32[]{:S(2)}) copy-start(f32[2,128]{1,0:T(2,128)} %param.6) | copy-start | bytes 3076
  108.2 10.0 %collective-permute-start.6 = (f32[148,2,2,2]{3,0,2,1:T(8,128)S(1)}, f32[148,2,2,2]{3,0,2,1:T(8,128)S(1)}, u32[]{:S(2)}, u32[]{:S(2)}) collective-permute-start(f32[148,2,2,2]{3,0,2,1:T(8,128)S(1)} %get-tuple-element.14), channel_id=1, source_target_pairs={{1,0},{2,1},{3,2},{4,3},{5,4},{6,5},{7,6},{8,7},{9,8},{10,9},{11,1... | collective-permute-start | bytes 14216 | tf_op jit(solution)/shard_map/ppermute | solution.py:32
  112.8 5.5 %collective-permute-start.5 = (f32[148,2,2,2]{3,0,2,1:T(8,128)S(1)}, f32[148,2,2,2]{3,0,2,1:T(8,128)S(1)}, u32[]{:S(2)}, u32[]{:S(2)}) collective-permute-start(f32[148,2,2,2]{3,0,2,1:T(8,128)S(1)} %get-tuple-element.13), channel_id=1, source_target_pairs={{0,1},{1,2},{2,3},{3,4},{4,5},{5,6},{6,7},{7,8},{8,9},{9,10},{10,1... | collective-permute-start | bytes 14216 | tf_op jit(solution)/shard_map/ppermute | solution.py:29

commit v5 on v4

--- a/solution.py
+++ b/solution.py
@@ -70,10 +70,17 @@
     counts = stacked[:, fields + 3, 0].astype(jnp.float32)
     live = counts > jnp.arange(slot_count, dtype=jnp.float32)
     stacked = jnp.where(live[:, None, None], stacked, jnp.zeros_like(stacked))
-    moments = lax.dot_general(
-        stacked, weights[0, 0], (((0, 2), (0, 1)), ((), ())), preferred_element_type=jnp.float32
+    flat = stacked.transpose(1, 0, 2).reshape(fields + 4, slot_count * cell_count)
+    moments = jnp.dot(
+        flat,
+        weights[0, 0].reshape(slot_count * cell_count, 3 * cell_count),
+        preferred_element_type=jnp.float32,
     )
-    moments = moments.reshape(fields + 4, 3, tile_rows, tile_cols)
+    moment = [
+        moments[:, m * cell_count : (m + 1) * cell_count].reshape(fields + 4, tile_rows, tile_cols)
+        for m in range(3)
+    ]
+    moments = jnp.stack(moment, axis=1)
     mean_adj = moments[:, 0]
     curv_adj = moments[:, 2]
     signs = jnp.array([-3.0, 3.0], jnp.float32)[None, :, None, None]
@@ -106,6 +113,4 @@
         P("lat", "lon", None, None, None),
     )
     out_specs = P(None, "lat", "lon")
-    return jax.shard_map(
-        on_device_body, mesh=mesh, in_specs=in_specs, out_specs=out_specs, check_vma=False
-    )
+    return jax.shard_map(on_device_body, mesh=mesh, in_specs=in_specs, out_specs=out_specs, check_vma=False)

time: 122 us -> 126 us (1.033); the launches traced: 120 us -> 126 us
  waiting for transfers between devices: 23.9 us -> 29.2 us
  other arithmetic: 10.3 us -> 12.2 us
  local copies, waits for them, and re-layouts: 8.33 us -> 6.97 us
    dot_general x1 -> x0, local copies, waits for them, and re-layouts: 5.72 us -> none  [on_device_body(): lax.dot_general(stacked, weights[0, 0], (((0, 2), (0, 1)), ((), ())), pre...]
    ppermute x9, waiting for transfers between devices: 15.4 us -> 20.8 us  [butterfly_sum(): partner = lax.ppermute(value, axis, [(i, i ^ step) for i in range(length)])]
    ppermute x1, starting transfers between devices: 4.56 us -> 0.38 us  [padded_2(): lax.ppermute(lax.slice_in_dim(block, 0, width, axis=dim), axis, backward)]
    ppermute x1, starting transfers between devices: 0.61 us -> 4.57 us  [padded_2(): lax.ppermute(lax.slice_in_dim(block, block.shape[dim] - width, None, axis...]
    another operation x0 -> x2, local copies, waits for them, and re-layouts: none -> 2.38 us  [the longest x1 1.65 us: on_device_body(): mean_adj = moments[:, 0]]
    another operation x2, other arithmetic: 2.03 us -> 0.1 us  [on_device_body(): pairs = jnp.stack([jnp.stack(ring[:half]), swapped], axis=1)]
    sub x1, other arithmetic: 0.35 us -> 2.15 us  [on_device_body(): stencil = mean_adj + 6.0 * curv_adj + 7.0 / 12.0 * near - 1.0 / 12.0 * far]
    concatenate x1, other arithmetic: 0.31 us -> 2.06 us  [padded_2(): block = jnp.concatenate([low, block, high], axis=dim)]
  transfers between devices with their start and end apart: 16 -> 16, of which waited for: 12 -> 14; matrix products, arithmetic and copies ran while one was open for 10% -> 5% of each run, Pallas kernels for 0% -> 0%
where the time goes in v5:
time: 126 us
  starting transfers between devices  75.4 us (60%)
  waiting for transfers between devices  29.2 us (23%)
  other arithmetic  12.2 us (10%)
  local copies, waits for them, and re-layouts  6.97 us (6%)
    ppermute x9, starting transfers between devices, butterfly_sum(): partner = lax.ppermute(value, axis, [(i, i ^ step) for i in range(length)])  37.4 us
    ppermute x4, starting transfers between devices, shifted(): lax.ppermute(value, axis, [(i, (i + by) % length) for i in range(length)])  26.7 us
    ppermute x9, waiting for transfers between devices, butterfly_sum(): partner = lax.ppermute(value, axis, [(i, i ^ step) for i in range(length)])  20.8 us
    ppermute x1, starting transfers between devices, on_device_body(): lax.ppermute(offer, 'lon', [(i, i ^ 1) for i in range(lax.axis_size('lon'...  6.39 us
    ppermute x1, starting transfers between devices, padded_2(): lax.ppermute(lax.slice_in_dim(block, block.shape[dim] - width, None, axis...  4.57 us
    ppermute x4, waiting for transfers between devices, shifted(): lax.ppermute(value, axis, [(i, (i + by) % length) for i in range(length)])  4.27 us
    ppermute x1, waiting for transfers between devices, padded_2(): lax.ppermute(lax.slice_in_dim(block, 0, width, axis=dim), axis, backward)  2.77 us
  transfers between devices with their start and end apart: 16, of which 14 were waited for; matrix products, arithmetic and copies ran while one was open for 5% of the time, Pallas kernels for 0%

profile of v5, /device:TPU:1, one launch (start us, length us, event | category | flops | bytes accessed | tf_op | source)
XLA Modules:
  0.0 125.6 jit_solution(10484969642698525566)
XLA Ops:
  0.0 0.0 copy-start
  0.8 0.8 fusion.4
  1.6 0.9 copy.14
  2.6 11.9 %collective-permute-start = (bf16[148,256]{1,0:T(8,128)(2,1)S(1)}, bf16[148,256]{1,0:T(8,128)(2,1)S(1)}, u32[]{:S(2)}, u32[]{:S(2)}) collective-permute-start(bf16[148,256]{1,0:T(8,128)(2,1)S(1)} %concatenate.9), channel_id=1, source_target_pairs={{0,30},{1,31},{2,0},{3,1},{4,2},{5,3},{6,4},{7,5},{8,6},{9,7},{10,... | collective-permute-start | bytes 227336 | tf_op jit(solution)/shard_map/ppermute | solution.py:9
  14.5 1.4 %collective-permute-done = bf16[148,256]{1,0:T(8,128)(2,1)S(1)} collective-permute-done((bf16[148,256]{1,0:T(8,128)(2,1)S(1)}, bf16[148,256]{1,0:T(8,128)(2,1)S(1)}, u32[]{:S(2)}, u32[]{:S(2)}) %collective-permute-start) | collective-permute-done | bytes 75808 | tf_op jit(solution)/shard_map/ppermute | solution.py:9
  16.0 4.9 %collective-permute-start.1 = (bf16[148,256]{1,0:T(8,128)(2,1)S(1)}, bf16[148,256]{1,0:T(8,128)(2,1)S(1)}, u32[]{:S(2)}, u32[]{:S(2)}) collective-permute-start(bf16[148,256]{1,0:T(8,128)(2,1)S(1)} %collective-permute-done), channel_id=1, source_target_pairs={{0,30},{1,31},{2,0},{3,1},{4,2},{5,3},{6,4},{7,5},{8,6},{9,7},{10,... | collective-permute-start | bytes 227336 | tf_op jit(solution)/shard_map/ppermute | solution.py:9
  20.9 1.4 %collective-permute-done.1 = bf16[148,256]{1,0:T(8,128)(2,1)S(1)} collective-permute-done((bf16[148,256]{1,0:T(8,128)(2,1)S(1)}, bf16[148,256]{1,0:T(8,128)(2,1)S(1)}, u32[]{:S(2)}, u32[]{:S(2)}) %collective-permute-start.1) | collective-permute-done | bytes 75808 | tf_op jit(solution)/shard_map/ppermute | solution.py:9
  22.3 4.9 %collective-permute-start.2 = (bf16[148,256]{1,0:T(8,128)(2,1)S(1)}, bf16[148,256]{1,0:T(8,128)(2,1)S(1)}, u32[]{:S(2)}, u32[]{:S(2)}) collective-permute-start(bf16[148,256]{1,0:T(8,128)(2,1)S(1)} %collective-permute-done.1), channel_id=1, source_target_pairs={{0,30},{1,31},{2,0},{3,1},{4,2},{5,3},{6,4},{7,5},{8,6},{9,7},{10,... | collective-permute-start | bytes 227336 | tf_op jit(solution)/shard_map/ppermute | solution.py:9
  27.2 1.4 %collective-permute-done.2 = bf16[148,256]{1,0:T(8,128)(2,1)S(1)} collective-permute-done((bf16[148,256]{1,0:T(8,128)(2,1)S(1)}, bf16[148,256]{1,0:T(8,128)(2,1)S(1)}, u32[]{:S(2)}, u32[]{:S(2)}) %collective-permute-start.2) | collective-permute-done | bytes 75808 | tf_op jit(solution)/shard_map/ppermute | solution.py:9
  28.6 4.9 %collective-permute-start.3 = (bf16[148,256]{1,0:T(8,128)(2,1)S(1)}, bf16[148,256]{1,0:T(8,128)(2,1)S(1)}, u32[]{:S(2)}, u32[]{:S(2)}) collective-permute-start(bf16[148,256]{1,0:T(8,128)(2,1)S(1)} %collective-permute-done.2), channel_id=1, source_target_pairs={{0,30},{1,31},{2,0},{3,1},{4,2},{5,3},{6,4},{7,5},{8,6},{9,7},{10,... | collective-permute-start | bytes 227336 | tf_op jit(solution)/shard_map/ppermute | solution.py:9
  33.6 1.9 %multiply_reduce_fusion = f32[144]{0:T(256)S(1)} fusion(bf16[144,2,128]{2,1,0:T(2,128)(2,1)} %param.5, f32[2,128]{1,0:T(2,128)} %param.6), kind=kLoop, calls=%fused_computation.19 | loop fusion | flops 110448 | bytes 75328 | tf_op jit(solution)/shard_map/reduce_sum | solution.py:50
  35.5 0.0 collective-permute-done.3
  35.6 6.4 %collective-permute-start.4 = (bf16[4,148,256]{2,1,0:T(8,128)(2,1)S(1)}, bf16[4,148,256]{2,1,0:T(8,128)(2,1)S(1)}, u32[]{:S(2)}, u32[]{:S(2)}) collective-permute-start(bf16[4,148,256]{2,1,0:T(8,128)(2,1)S(1)} %pad_maximum_fusion.2), channel_id=1, source_target_pairs={{0,1},{1,0},{2,3},{3,2},{4,5},{5,4},{6,7},{7,6},{8,9},{9,8},{10,11... | collective-permute-start | bytes 909320 | tf_op jit(solution)/shard_map/ppermute | solution.py:67
  42.0 1.3 %multiply_reduce_fusion.1 = f32[]{:T(128)} fusion(f32[2,128]{1,0:T(2,128)} %param.6), kind=kLoop, calls=%fused_computation.38 | loop fusion | flops 511 | bytes 1028 | tf_op jit(solution)/shard_map/reduce_sum | solution.py:51
  43.2 0.7 pad_maximum_fusion.3
  44.0 3.1 %collective-permute-start.7 = (f32[145]{0:T(256)S(1)}, f32[145]{0:T(256)S(1)}, u32[]{:S(2)}, u32[]{:S(2)}) collective-permute-start(f32[145]{0:T(256)S(1)} %pad_maximum_fusion.3), channel_id=1, source_target_pairs={{0,32},{32,0},{64,96},{96,64},{128,160},{160,128},{192,224},{224,1... | collective-permute-start | bytes 1748 | tf_op jit(solution)/shard_map/ppermute | solution.py:17
  47.1 1.2 collective-permute-done.7
  48.3 4.6 %collective-permute-start.8 = (f32[145]{0:T(256)S(1)}, f32[145]{0:T(256)S(1)}, u32[]{:S(2)}, u32[]{:S(2)}) collective-permute-start(f32[145]{0:T(256)S(1)} %add.74), channel_id=1, source_target_pairs={{0,64},{32,96},{64,0},{96,32},{128,192},{160,224},{192,128},{224,1... | collective-permute-start | bytes 1748 | tf_op jit(solution)/shard_map/ppermute | solution.py:17
  52.9 1.2 collective-permute-done.8
  54.1 3.2 %collective-permute-start.9 = (f32[145]{0:T(256)S(1)}, f32[145]{0:T(256)S(1)}, u32[]{:S(2)}, u32[]{:S(2)}) collective-permute-start(f32[145]{0:T(256)S(1)} %add.75), channel_id=1, source_target_pairs={{0,128},{32,160},{64,192},{96,224},{128,0},{160,32},{192,64},{224,... | collective-permute-start | bytes 1748 | tf_op jit(solution)/shard_map/ppermute | solution.py:17
  57.3 1.1 collective-permute-done.9
  58.4 4.8 %collective-permute-start.10 = (f32[145]{0:T(256)S(1)}, f32[145]{0:T(256)S(1)}, u32[]{:S(2)}, u32[]{:S(2)}) collective-permute-start(f32[145]{0:T(256)S(1)} %add.76), channel_id=1, source_target_pairs={{0,256},{32,288},{64,320},{96,352},{128,384},{160,416},{192,448},{... | collective-permute-start | bytes 1748 | tf_op jit(solution)/shard_map/ppermute | solution.py:17
  63.2 1.0 collective-permute-done.10
  64.2 6.5 %collective-permute-start.11 = (f32[145]{0:T(256)S(1)}, f32[145]{0:T(256)S(1)}, u32[]{:S(2)}, u32[]{:S(2)}) collective-permute-start(f32[145]{0:T(256)S(1)} %add.77), channel_id=1, source_target_pairs={{0,1},{1,0},{2,3},{3,2},{4,5},{5,4},{6,7},{7,6},{8,9},{9,8},{10,11... | collective-permute-start | bytes 1748 | tf_op jit(solution)/shard_map/ppermute | solution.py:17
  70.7 0.8 collective-permute-done.11
  71.5 1.9 %collective-permute-start.12 = (f32[145]{0:T(256)S(1)}, f32[145]{0:T(256)S(1)}, u32[]{:S(2)}, u32[]{:S(2)}) collective-permute-start(f32[145]{0:T(256)S(1)} %add.78), channel_id=1, source_target_pairs={{0,2},{1,3},{2,0},{3,1},{4,6},{5,7},{6,4},{7,5},{8,10},{9,11},{10,... | collective-permute-start | bytes 1748 | tf_op jit(solution)/shard_map/ppermute | solution.py:17
  73.5 2.4 %collective-permute-done.12 = f32[145]{0:T(256)S(1)} collective-permute-done((f32[145]{0:T(256)S(1)}, f32[145]{0:T(256)S(1)}, u32[]{:S(2)}, u32[]{:S(2)}) %collective-permute-start.12) | collective-permute-done | bytes 612 | tf_op jit(solution)/shard_map/ppermute | solution.py:17
  75.8 1.9 %collective-permute-start.13 = (f32[145]{0:T(256)S(1)}, f32[145]{0:T(256)S(1)}, u32[]{:S(2)}, u32[]{:S(2)}) collective-permute-start(f32[145]{0:T(256)S(1)} %add.79), channel_id=1, source_target_pairs={{0,4},{1,5},{2,6},{3,7},{4,0},{5,1},{6,2},{7,3},{8,12},{9,13},{10,... | collective-permute-start | bytes 1748 | tf_op jit(solution)/shard_map/ppermute | solution.py:17
  77.8 3.3 %collective-permute-done.13 = f32[145]{0:T(256)S(1)} collective-permute-done((f32[145]{0:T(256)S(1)}, f32[145]{0:T(256)S(1)}, u32[]{:S(2)}, u32[]{:S(2)}) %collective-permute-start.13) | collective-permute-done | bytes 612 | tf_op jit(solution)/shard_map/ppermute | solution.py:17
  81.1 3.7 %collective-permute-start.14 = (f32[145]{0:T(256)S(1)}, f32[145]{0:T(256)S(1)}, u32[]{:S(2)}, u32[]{:S(2)}) collective-permute-start(f32[145]{0:T(256)S(1)} %add.80), channel_id=1, source_target_pairs={{0,8},{1,9},{2,10},{3,11},{4,12},{5,13},{6,14},{7,15},{8,0},{9,1},... | collective-permute-start | bytes 1748 | tf_op jit(solution)/shard_map/ppermute | solution.py:17
  84.8 4.5 %collective-permute-done.14 = f32[145]{0:T(256)S(1)} collective-permute-done((f32[145]{0:T(256)S(1)}, f32[145]{0:T(256)S(1)}, u32[]{:S(2)}, u32[]{:S(2)}) %collective-permute-start.14) | collective-permute-done | bytes 612 | tf_op jit(solution)/shard_map/ppermute | solution.py:17
  89.3 7.6 %collective-permute-start.15 = (f32[145]{0:T(256)S(1)}, f32[145]{0:T(256)S(1)}, u32[]{:S(2)}, u32[]{:S(2)}) collective-permute-start(f32[145]{0:T(256)S(1)} %add.81), channel_id=1, source_target_pairs={{0,16},{1,17},{2,18},{3,19},{4,20},{5,21},{6,22},{7,23},{8,24},{9,... | collective-permute-start | bytes 1748 | tf_op jit(solution)/shard_map/ppermute | solution.py:17
  96.9 5.4 %collective-permute-done.15 = f32[145]{0:T(256)S(1)} collective-permute-done((f32[145]{0:T(256)S(1)}, f32[145]{0:T(256)S(1)}, u32[]{:S(2)}, u32[]{:S(2)}) %collective-permute-start.15) | collective-permute-done | bytes 612 | tf_op jit(solution)/shard_map/ppermute | solution.py:17
  102.3 0.6 slice.84
  102.9 0.0 collective-permute-done.4
  102.9 0.1 pad_maximum_fusion
  103.0 0.2 compare_reduce_fusion
  103.2 0.1 select_bitcast_fusion
  103.4 0.1 copy.10
  103.6 0.1 copy.12
  103.7 0.0 copy-done
  103.7 0.0 copy-start.2
  103.7 0.7 fusion.9
  104.4 0.7 fusion.7
  105.1 0.7 squeeze_stack_reshape.7
  105.8 0.7 add.68
  106.6 0.0 copy-done.2
  106.6 0.0 copy-start.1
  106.6 1.2 multiply_add_fusion
  107.7 1.1 fusion.8
  108.9 4.6 %collective-permute-start.5 = (f32[148,2,2,2]{3,2,0,1:T(2,128)}, f32[148,2,2,2]{3,2,0,1:T(2,128)}, u32[]{:S(2)}, u32[]{:S(2)}) collective-permute-start(f32[148,2,2,2]{3,2,0,1:T(2,128)} %get-tuple-element.14), channel_id=1, source_target_pairs={{0,1},{1,2},{2,3},{3,4},{4,5},{5,6},{6,7},{7,8},{8,9},{9,10},{10,1... | collective-permute-start | bytes 14216 | tf_op jit(solution)/shard_map/ppermute | solution.py:29
  113.4 0.4 collective-permute-start.6
  113.8 0.6 slice_divide_fusion
  114.5 1.6 %squeeze_stack_reshape.6 = f32[148,2,128]{2,1,0:T(2,128)} reshape(f32[148,256]{1,0:T(8,128)} %get-tuple-element.11) | data formatting | bytes 303104 | tf_op jit(solution)/shard_map/squeeze;stack;reshape | solution.py:84
  116.1 1.4 %collective-permute-done.5 = f32[148,2,2,2]{3,2,0,1:T(2,128)} collective-permute-done((f32[148,2,2,2]{3,2,0,1:T(2,128)}, f32[148,2,2,2]{3,2,0,1:T(2,128)}, u32[]{:S(2)}, u32[]{:S(2)}) %collective-permute-start.5) | collective-permute-done | bytes 4768 | tf_op jit(solution)/shard_map/ppermute | solution.py:29
  117.5 2.8 %collective-permute-done.6 = f32[148,2,2,2]{3,2,0,1:T(2,128)} collective-permute-done((f32[148,2,2,2]{3,2,0,1:T(2,128)}, f32[148,2,2,2]{3,2,0,1:T(2,128)}, u32[]{:S(2)}, u32[]{:S(2)}) %collective-permute-start.6) | collective-permute-done | bytes 4768 | tf_op jit(solution)/shard_map/ppermute | solution.py:32
  120.3 2.1 %pad_maximum_fusion.1 = f32[148,2,2,132]{3,2,0,1:T(2,128)S(1)} fusion(f32[148,2,2,2]{3,2,0,1:T(2,128)} %collective-permute-done.6, f32[148,2,2,128]{3,2,0,1:T(2,128)S(1)} %multiply_add_fusion, f32[148,2,2,2]{3,2,0,1:T(2,128)} %collective-permute-done.5), kind=kLoop, calls=%fused_computation.2 | loop fusion | flops 156288 | bytes 625152 | tf_op jit(solution)/shard_map/concatenate | solution.py:33
  122.3 0.2 slice_bitcast_fusion.1
  122.6 2.1 %fusion.1 = f32[148,2,128]{2,1,0:T(2,128)S(1)} fusion(f32[148,2,132]{2,1,0:T(2,128)S(1)} %get-tuple-element.10, f32[148,2,132]{2,1,0:T(2,128)S(1)} %get-tuple-element.9, f32[148,2,128]{2,1,0:T(2,128)} %squeeze_stack_reshape.6, f32[148,2,128]{2,1,0:T(2,128)} %squeeze_stack_reshape.7), kind=kLoop, calls=%fused_computation.10 | loop fusion | flops 454656 | bytes 1667072 | tf_op jit(solution)/shard_map/sub | solution.py:103
  124.7 0.0 copy-done.1
  124.7 0.9 slice_add_fusion.2
  (16 shorter events, 0.2 us)
Async XLA Ops:
  0.0 103.7 %copy-start = (bf16[1,1,8,256,768]{4,3,2,1,0:T(8,128)(2,1)S(1)}, bf16[1,1,8,256,768]{4,3,2,1,0:T(8,128)(2,1)}, u32[]{:S(2)}) copy-start(bf16[1,1,8,256,768]{4,3,2,1,0:T(8,128)(2,1)} %param.8) | copy-start | bytes 9437188
  2.6 13.4 %collective-permute-start = (bf16[148,256]{1,0:T(8,128)(2,1)S(1)}, bf16[148,256]{1,0:T(8,128)(2,1)S(1)}, u32[]{:S(2)}, u32[]{:S(2)}) collective-permute-start(bf16[148,256]{1,0:T(8,128)(2,1)S(1)} %concatenate.9), channel_id=1, source_target_pairs={{0,30},{1,31},{2,0},{3,1},{4,2},{5,3},{6,4},{7,5},{8,6},{9,7},{10,... | collective-permute-start | bytes 227336 | tf_op jit(solution)/shard_map/ppermute | solution.py:9
  16.0 6.3 %collective-permute-start.1 = (bf16[148,256]{1,0:T(8,128)(2,1)S(1)}, bf16[148,256]{1,0:T(8,128)(2,1)S(1)}, u32[]{:S(2)}, u32[]{:S(2)}) collective-permute-start(bf16[148,256]{1,0:T(8,128)(2,1)S(1)} %collective-permute-done), channel_id=1, source_target_pairs={{0,30},{1,31},{2,0},{3,1},{4,2},{5,3},{6,4},{7,5},{8,6},{9,7},{10,... | collective-permute-start | bytes 227336 | tf_op jit(solution)/shard_map/ppermute | solution.py:9
  22.3 6.3 %collective-permute-start.2 = (bf16[148,256]{1,0:T(8,128)(2,1)S(1)}, bf16[148,256]{1,0:T(8,128)(2,1)S(1)}, u32[]{:S(2)}, u32[]{:S(2)}) collective-permute-start(bf16[148,256]{1,0:T(8,128)(2,1)S(1)} %collective-permute-done.1), channel_id=1, source_target_pairs={{0,30},{1,31},{2,0},{3,1},{4,2},{5,3},{6,4},{7,5},{8,6},{9,7},{10,... | collective-permute-start | bytes 227336 | tf_op jit(solution)/shard_map/ppermute | solution.py:9
  28.6 6.8 %collective-permute-start.3 = (bf16[148,256]{1,0:T(8,128)(2,1)S(1)}, bf16[148,256]{1,0:T(8,128)(2,1)S(1)}, u32[]{:S(2)}, u32[]{:S(2)}) collective-permute-start(bf16[148,256]{1,0:T(8,128)(2,1)S(1)} %collective-permute-done.2), channel_id=1, source_target_pairs={{0,30},{1,31},{2,0},{3,1},{4,2},{5,3},{6,4},{7,5},{8,6},{9,7},{10,... | collective-permute-start | bytes 227336 | tf_op jit(solution)/shard_map/ppermute | solution.py:9
  35.6 67.4 %collective-permute-start.4 = (bf16[4,148,256]{2,1,0:T(8,128)(2,1)S(1)}, bf16[4,148,256]{2,1,0:T(8,128)(2,1)S(1)}, u32[]{:S(2)}, u32[]{:S(2)}) collective-permute-start(bf16[4,148,256]{2,1,0:T(8,128)(2,1)S(1)} %pad_maximum_fusion.2), channel_id=1, source_target_pairs={{0,1},{1,0},{2,3},{3,2},{4,5},{5,4},{6,7},{7,6},{8,9},{9,8},{10,11... | collective-permute-start | bytes 909320 | tf_op jit(solution)/shard_map/ppermute | solution.py:67
  44.0 4.3 %collective-permute-start.7 = (f32[145]{0:T(256)S(1)}, f32[145]{0:T(256)S(1)}, u32[]{:S(2)}, u32[]{:S(2)}) collective-permute-start(f32[145]{0:T(256)S(1)} %pad_maximum_fusion.3), channel_id=1, source_target_pairs={{0,32},{32,0},{64,96},{96,64},{128,160},{160,128},{192,224},{224,1... | collective-permute-start | bytes 1748 | tf_op jit(solution)/shard_map/ppermute | solution.py:17
  48.3 5.8 %collective-permute-start.8 = (f32[145]{0:T(256)S(1)}, f32[145]{0:T(256)S(1)}, u32[]{:S(2)}, u32[]{:S(2)}) collective-permute-start(f32[145]{0:T(256)S(1)} %add.74), channel_id=1, source_target_pairs={{0,64},{32,96},{64,0},{96,32},{128,192},{160,224},{192,128},{224,1... | collective-permute-start | bytes 1748 | tf_op jit(solution)/shard_map/ppermute | solution.py:17
  54.1 4.3 %collective-permute-start.9 = (f32[145]{0:T(256)S(1)}, f32[145]{0:T(256)S(1)}, u32[]{:S(2)}, u32[]{:S(2)}) collective-permute-start(f32[145]{0:T(256)S(1)} %add.75), channel_id=1, source_target_pairs={{0,128},{32,160},{64,192},{96,224},{128,0},{160,32},{192,64},{224,... | collective-permute-start | bytes 1748 | tf_op jit(solution)/shard_map/ppermute | solution.py:17
  58.4 5.8 %collective-permute-start.10 = (f32[145]{0:T(256)S(1)}, f32[145]{0:T(256)S(1)}, u32[]{:S(2)}, u32[]{:S(2)}) collective-permute-start(f32[145]{0:T(256)S(1)} %add.76), channel_id=1, source_target_pairs={{0,256},{32,288},{64,320},{96,352},{128,384},{160,416},{192,448},{... | collective-permute-start | bytes 1748 | tf_op jit(solution)/shard_map/ppermute | solution.py:17
  64.2 7.3 %collective-permute-start.11 = (f32[145]{0:T(256)S(1)}, f32[145]{0:T(256)S(1)}, u32[]{:S(2)}, u32[]{:S(2)}) collective-permute-start(f32[145]{0:T(256)S(1)} %add.77), channel_id=1, source_target_pairs={{0,1},{1,0},{2,3},{3,2},{4,5},{5,4},{6,7},{7,6},{8,9},{9,8},{10,11... | collective-permute-start | bytes 1748 | tf_op jit(solution)/shard_map/ppermute | solution.py:17
  71.5 4.3 %collective-permute-start.12 = (f32[145]{0:T(256)S(1)}, f32[145]{0:T(256)S(1)}, u32[]{:S(2)}, u32[]{:S(2)}) collective-permute-start(f32[145]{0:T(256)S(1)} %add.78), channel_id=1, source_target_pairs={{0,2},{1,3},{2,0},{3,1},{4,6},{5,7},{6,4},{7,5},{8,10},{9,11},{10,... | collective-permute-start | bytes 1748 | tf_op jit(solution)/shard_map/ppermute | solution.py:17
  75.8 5.2 %collective-permute-start.13 = (f32[145]{0:T(256)S(1)}, f32[145]{0:T(256)S(1)}, u32[]{:S(2)}, u32[]{:S(2)}) collective-permute-start(f32[145]{0:T(256)S(1)} %add.79), channel_id=1, source_target_pairs={{0,4},{1,5},{2,6},{3,7},{4,0},{5,1},{6,2},{7,3},{8,12},{9,13},{10,... | collective-permute-start | bytes 1748 | tf_op jit(solution)/shard_map/ppermute | solution.py:17
  81.1 8.2 %collective-permute-start.14 = (f32[145]{0:T(256)S(1)}, f32[145]{0:T(256)S(1)}, u32[]{:S(2)}, u32[]{:S(2)}) collective-permute-start(f32[145]{0:T(256)S(1)} %add.80), channel_id=1, source_target_pairs={{0,8},{1,9},{2,10},{3,11},{4,12},{5,13},{6,14},{7,15},{8,0},{9,1},... | collective-permute-start | bytes 1748 | tf_op jit(solution)/shard_map/ppermute | solution.py:17
  89.3 13.0 %collective-permute-start.15 = (f32[145]{0:T(256)S(1)}, f32[145]{0:T(256)S(1)}, u32[]{:S(2)}, u32[]{:S(2)}) collective-permute-start(f32[145]{0:T(256)S(1)} %add.81), channel_id=1, source_target_pairs={{0,16},{1,17},{2,18},{3,19},{4,20},{5,21},{6,22},{7,23},{8,24},{9,... | collective-permute-start | bytes 1748 | tf_op jit(solution)/shard_map/ppermute | solution.py:17
  103.7 2.8 %copy-start.2 = (f32[2]{0:T(128)S(1)}, f32[2]{0:T(128)}, u32[]{:S(2)}) copy-start(f32[2]{0:T(128)} %constant.30.clone) | copy-start | bytes 28
  106.6 18.2 %copy-start.1 = (f32[2,128]{1,0:T(2,128)S(1)}, f32[2,128]{1,0:T(2,128)}, u32[]{:S(2)}) copy-start(f32[2,128]{1,0:T(2,128)} %param.6) | copy-start | bytes 3076
  108.9 8.6 %collective-permute-start.5 = (f32[148,2,2,2]{3,2,0,1:T(2,128)}, f32[148,2,2,2]{3,2,0,1:T(2,128)}, u32[]{:S(2)}, u32[]{:S(2)}) collective-permute-start(f32[148,2,2,2]{3,2,0,1:T(2,128)} %get-tuple-element.14), channel_id=1, source_target_pairs={{0,1},{1,2},{2,3},{3,4},{4,5},{5,6},{6,7},{7,8},{8,9},{9,10},{10,1... | collective-permute-start | bytes 14216 | tf_op jit(solution)/shard_map/ppermute | solution.py:29
  113.4 6.8 %collective-permute-start.6 = (f32[148,2,2,2]{3,2,0,1:T(2,128)}, f32[148,2,2,2]{3,2,0,1:T(2,128)}, u32[]{:S(2)}, u32[]{:S(2)}) collective-permute-start(f32[148,2,2,2]{3,2,0,1:T(2,128)} %get-tuple-element.15), channel_id=1, source_target_pairs={{1,0},{2,1},{3,2},{4,3},{5,4},{6,5},{7,6},{8,7},{9,8},{10,9},{11,1... | collective-permute-start | bytes 14216 | tf_op jit(solution)/shard_map/ppermute | solution.py:32

commit v6 on v5

--- a/solution.py
+++ b/solution.py
@@ -76,15 +76,18 @@
         weights[0, 0].reshape(slot_count * cell_count, 3 * cell_count),
         preferred_element_type=jnp.float32,
     )
-    moment = [
-        moments[:, m * cell_count : (m + 1) * cell_count].reshape(fields + 4, tile_rows, tile_cols)
-        for m in range(3)
+
+    def block(moment_index, row):
+        start = moment_index * cell_count + row * tile_cols
+        return moments[:, start : start + tile_cols]
+
+    mean_adj = jnp.stack([block(0, row) for row in range(tile_rows)], axis=1)
+    curv_adj = jnp.stack([block(2, row) for row in range(tile_rows)], axis=1)
+    sides = [
+        jnp.stack([block(1, row) + sign * block(2, row) for row in range(tile_rows)], axis=1)
+        for sign in (-3.0, 3.0)
     ]
-    moments = jnp.stack(moment, axis=1)
-    mean_adj = moments[:, 0]
-    curv_adj = moments[:, 2]
-    signs = jnp.array([-3.0, 3.0], jnp.float32)[None, :, None, None]
-    edge_pair = moments[:, 1:2] + signs * moments[:, 2:3]
+    edge_pair = jnp.stack(sides, axis=1)
     padded = padded_2(edge_pair, (("lon", 3),), 2)
     left_pad = padded[:, 0]
     right_pad = padded[:, 1]
@@ -113,4 +116,6 @@
         P("lat", "lon", None, None, None),
     )
     out_specs = P(None, "lat", "lon")
-    return jax.shard_map(on_device_body, mesh=mesh, in_specs=in_specs, out_specs=out_specs, check_vma=False)
+    return jax.shard_map(
+        on_device_body, mesh=mesh, in_specs=in_specs, out_specs=out_specs, check_vma=False
+    )

time: 126 us -> 118 us (0.937)
  the two profiles are of different devices: /device:TPU:1 before, /device:TPU:4 now
where the time goes in v6:
time: 118 us
  starting transfers between devices  60.9 us (52%)
  waiting for transfers between devices  45.7 us (39%)
  other arithmetic  6.81 us (6%)
  local copies, waits for them, and re-layouts  2.75 us (2%)
    ppermute x9, waiting for transfers between devices, butterfly_sum(): partner = lax.ppermute(value, axis, [(i, i ^ step) for i in range(length)])  32.6 us
    ppermute x9, starting transfers between devices, butterfly_sum(): partner = lax.ppermute(value, axis, [(i, i ^ step) for i in range(length)])  30.6 us
    ppermute x4, starting transfers between devices, shifted(): lax.ppermute(value, axis, [(i, (i + by) % length) for i in range(length)])  27.8 us
    ppermute x4, waiting for transfers between devices, shifted(): lax.ppermute(value, axis, [(i, (i + by) % length) for i in range(length)])  6.07 us
    ppermute x1, waiting for transfers between devices, padded_2(): lax.ppermute(lax.slice_in_dim(block, block.shape[dim] - width, None, axis...  3.86 us
    ppermute x1, waiting for transfers between devices, padded_2(): lax.ppermute(lax.slice_in_dim(block, 0, width, axis=dim), axis, backward)  3.26 us
  transfers between devices with their start and end apart: 16, of which 15 were waited for; matrix products, arithmetic and copies ran while one was open for 4% of the time, Pallas kernels for 0%

profile of v6, /device:TPU:4, one launch (start us, length us, event | category | flops | bytes accessed | tf_op | source)
XLA Modules:
  0.0 117.8 jit_solution(2285055669780341700)
XLA Ops:
  0.0 0.0 copy-start
  0.0 1.0 copy.16
  1.1 0.7 fusion.4
  2.4 11.4 %collective-permute-start = (bf16[148,256]{1,0:T(8,128)(2,1)S(1)}, bf16[148,256]{1,0:T(8,128)(2,1)S(1)}, u32[]{:S(2)}, u32[]{:S(2)}) collective-permute-start(bf16[148,256]{1,0:T(8,128)(2,1)S(1)} %concatenate.9), channel_id=1, source_target_pairs={{0,30},{1,31},{2,0},{3,1},{4,2},{5,3},{6,4},{7,5},{8,6},{9,7},{10,... | collective-permute-start | bytes 227336 | tf_op jit(solution)/shard_map/ppermute | solution.py:9
  13.8 2.0 %collective-permute-done = bf16[148,256]{1,0:T(8,128)(2,1)S(1)} collective-permute-done((bf16[148,256]{1,0:T(8,128)(2,1)S(1)}, bf16[148,256]{1,0:T(8,128)(2,1)S(1)}, u32[]{:S(2)}, u32[]{:S(2)}) %collective-permute-start) | collective-permute-done | bytes 75808 | tf_op jit(solution)/shard_map/ppermute | solution.py:9
  15.8 5.5 %collective-permute-start.1 = (bf16[148,256]{1,0:T(8,128)(2,1)S(1)}, bf16[148,256]{1,0:T(8,128)(2,1)S(1)}, u32[]{:S(2)}, u32[]{:S(2)}) collective-permute-start(bf16[148,256]{1,0:T(8,128)(2,1)S(1)} %collective-permute-done), channel_id=1, source_target_pairs={{0,30},{1,31},{2,0},{3,1},{4,2},{5,3},{6,4},{7,5},{8,6},{9,7},{10,... | collective-permute-start | bytes 227336 | tf_op jit(solution)/shard_map/ppermute | solution.py:9
  21.3 2.0 %collective-permute-done.1 = bf16[148,256]{1,0:T(8,128)(2,1)S(1)} collective-permute-done((bf16[148,256]{1,0:T(8,128)(2,1)S(1)}, bf16[148,256]{1,0:T(8,128)(2,1)S(1)}, u32[]{:S(2)}, u32[]{:S(2)}) %collective-permute-start.1) | collective-permute-done | bytes 75808 | tf_op jit(solution)/shard_map/ppermute | solution.py:9
  23.3 5.5 %collective-permute-start.2 = (bf16[148,256]{1,0:T(8,128)(2,1)S(1)}, bf16[148,256]{1,0:T(8,128)(2,1)S(1)}, u32[]{:S(2)}, u32[]{:S(2)}) collective-permute-start(bf16[148,256]{1,0:T(8,128)(2,1)S(1)} %collective-permute-done.1), channel_id=1, source_target_pairs={{0,30},{1,31},{2,0},{3,1},{4,2},{5,3},{6,4},{7,5},{8,6},{9,7},{10,... | collective-permute-start | bytes 227336 | tf_op jit(solution)/shard_map/ppermute | solution.py:9
  28.8 2.0 %collective-permute-done.2 = bf16[148,256]{1,0:T(8,128)(2,1)S(1)} collective-permute-done((bf16[148,256]{1,0:T(8,128)(2,1)S(1)}, bf16[148,256]{1,0:T(8,128)(2,1)S(1)}, u32[]{:S(2)}, u32[]{:S(2)}) %collective-permute-start.2) | collective-permute-done | bytes 75808 | tf_op jit(solution)/shard_map/ppermute | solution.py:9
  30.8 5.5 %collective-permute-start.3 = (bf16[148,256]{1,0:T(8,128)(2,1)S(1)}, bf16[148,256]{1,0:T(8,128)(2,1)S(1)}, u32[]{:S(2)}, u32[]{:S(2)}) collective-permute-start(bf16[148,256]{1,0:T(8,128)(2,1)S(1)} %collective-permute-done.2), channel_id=1, source_target_pairs={{0,30},{1,31},{2,0},{3,1},{4,2},{5,3},{6,4},{7,5},{8,6},{9,7},{10,... | collective-permute-start | bytes 227336 | tf_op jit(solution)/shard_map/ppermute | solution.py:9
  36.3 1.9 %multiply_reduce_fusion = f32[144]{0:T(256)S(1)} fusion(bf16[144,2,128]{2,1,0:T(2,128)(2,1)} %param.4, f32[2,128]{1,0:T(2,128)} %param.5), kind=kLoop, calls=%fused_computation.24 | loop fusion | flops 110448 | bytes 75328 | tf_op jit(solution)/shard_map/reduce_sum | solution.py:50
  38.2 0.1 collective-permute-done.3
  38.4 1.9 %collective-permute-start.4 = (bf16[4,148,256]{2,1,0:T(8,128)(2,1)S(1)}, bf16[4,148,256]{2,1,0:T(8,128)(2,1)S(1)}, u32[]{:S(2)}, u32[]{:S(2)}) collective-permute-start(bf16[4,148,256]{2,1,0:T(8,128)(2,1)S(1)} %pad_maximum_fusion.3), channel_id=1, source_target_pairs={{0,1},{1,0},{2,3},{3,2},{4,5},{5,4},{6,7},{7,6},{8,9},{9,8},{10,11... | collective-permute-start | bytes 909320 | tf_op jit(solution)/shard_map/ppermute | solution.py:67
  40.3 1.3 %multiply_reduce_fusion.1 = f32[]{:T(128)} fusion(f32[2,128]{1,0:T(2,128)} %param.5), kind=kLoop, calls=%fused_computation.49 | loop fusion | flops 511 | bytes 1028 | tf_op jit(solution)/shard_map/reduce_sum | solution.py:51
  41.6 0.7 pad_maximum_fusion.4
  42.3 3.1 %collective-permute-start.7 = (f32[145]{0:T(256)S(1)}, f32[145]{0:T(256)S(1)}, u32[]{:S(2)}, u32[]{:S(2)}) collective-permute-start(f32[145]{0:T(256)S(1)} %pad_maximum_fusion.4), channel_id=1, source_target_pairs={{0,32},{32,0},{64,96},{96,64},{128,160},{160,128},{192,224},{224,1... | collective-permute-start | bytes 1748 | tf_op jit(solution)/shard_map/ppermute | solution.py:17
  45.4 2.4 %collective-permute-done.7 = f32[145]{0:T(256)S(1)} collective-permute-done((f32[145]{0:T(256)S(1)}, f32[145]{0:T(256)S(1)}, u32[]{:S(2)}, u32[]{:S(2)}) %collective-permute-start.7) | collective-permute-done | bytes 612 | tf_op jit(solution)/shard_map/ppermute | solution.py:17
  47.8 2.4 %collective-permute-start.8 = (f32[145]{0:T(256)S(1)}, f32[145]{0:T(256)S(1)}, u32[]{:S(2)}, u32[]{:S(2)}) collective-permute-start(f32[145]{0:T(256)S(1)} %add.77), channel_id=1, source_target_pairs={{0,64},{32,96},{64,0},{96,32},{128,192},{160,224},{192,128},{224,1... | collective-permute-start | bytes 1748 | tf_op jit(solution)/shard_map/ppermute | solution.py:17
  50.2 4.5 %collective-permute-done.8 = f32[145]{0:T(256)S(1)} collective-permute-done((f32[145]{0:T(256)S(1)}, f32[145]{0:T(256)S(1)}, u32[]{:S(2)}, u32[]{:S(2)}) %collective-permute-start.8) | collective-permute-done | bytes 612 | tf_op jit(solution)/shard_map/ppermute | solution.py:17
  54.8 3.5 %collective-permute-start.9 = (f32[145]{0:T(256)S(1)}, f32[145]{0:T(256)S(1)}, u32[]{:S(2)}, u32[]{:S(2)}) collective-permute-start(f32[145]{0:T(256)S(1)} %add.78), channel_id=1, source_target_pairs={{0,128},{32,160},{64,192},{96,224},{128,0},{160,32},{192,64},{224,... | collective-permute-start | bytes 1748 | tf_op jit(solution)/shard_map/ppermute | solution.py:17
  58.2 2.0 %collective-permute-done.9 = f32[145]{0:T(256)S(1)} collective-permute-done((f32[145]{0:T(256)S(1)}, f32[145]{0:T(256)S(1)}, u32[]{:S(2)}, u32[]{:S(2)}) %collective-permute-start.9) | collective-permute-done | bytes 612 | tf_op jit(solution)/shard_map/ppermute | solution.py:17
  60.2 5.1 %collective-permute-start.10 = (f32[145]{0:T(256)S(1)}, f32[145]{0:T(256)S(1)}, u32[]{:S(2)}, u32[]{:S(2)}) collective-permute-start(f32[145]{0:T(256)S(1)} %add.79), channel_id=1, source_target_pairs={{0,256},{32,288},{64,320},{96,352},{128,384},{160,416},{192,448},{... | collective-permute-start | bytes 1748 | tf_op jit(solution)/shard_map/ppermute | solution.py:17
  65.3 1.9 %collective-permute-done.10 = f32[145]{0:T(256)S(1)} collective-permute-done((f32[145]{0:T(256)S(1)}, f32[145]{0:T(256)S(1)}, u32[]{:S(2)}, u32[]{:S(2)}) %collective-permute-start.10) | collective-permute-done | bytes 612 | tf_op jit(solution)/shard_map/ppermute | solution.py:17
  67.2 1.9 %collective-permute-start.11 = (f32[145]{0:T(256)S(1)}, f32[145]{0:T(256)S(1)}, u32[]{:S(2)}, u32[]{:S(2)}) collective-permute-start(f32[145]{0:T(256)S(1)} %add.80), channel_id=1, source_target_pairs={{0,1},{1,0},{2,3},{3,2},{4,5},{5,4},{6,7},{7,6},{8,9},{9,8},{10,11... | collective-permute-start | bytes 1748 | tf_op jit(solution)/shard_map/ppermute | solution.py:17
  69.1 1.1 collective-permute-done.11
  70.2 1.9 %collective-permute-start.12 = (f32[145]{0:T(256)S(1)}, f32[145]{0:T(256)S(1)}, u32[]{:S(2)}, u32[]{:S(2)}) collective-permute-start(f32[145]{0:T(256)S(1)} %add.81), channel_id=1, source_target_pairs={{0,2},{1,3},{2,0},{3,1},{4,6},{5,7},{6,4},{7,5},{8,10},{9,11},{10,... | collective-permute-start | bytes 1748 | tf_op jit(solution)/shard_map/ppermute | solution.py:17
  72.2 3.5 %collective-permute-done.12 = f32[145]{0:T(256)S(1)} collective-permute-done((f32[145]{0:T(256)S(1)}, f32[145]{0:T(256)S(1)}, u32[]{:S(2)}, u32[]{:S(2)}) %collective-permute-start.12) | collective-permute-done | bytes 612 | tf_op jit(solution)/shard_map/ppermute | solution.py:17
  75.7 1.9 %collective-permute-start.13 = (f32[145]{0:T(256)S(1)}, f32[145]{0:T(256)S(1)}, u32[]{:S(2)}, u32[]{:S(2)}) collective-permute-start(f32[145]{0:T(256)S(1)} %add.82), channel_id=1, source_target_pairs={{0,4},{1,5},{2,6},{3,7},{4,0},{5,1},{6,2},{7,3},{8,12},{9,13},{10,... | collective-permute-start | bytes 1748 | tf_op jit(solution)/shard_map/ppermute | solution.py:17
  77.6 4.4 %collective-permute-done.13 = f32[145]{0:T(256)S(1)} collective-permute-done((f32[145]{0:T(256)S(1)}, f32[145]{0:T(256)S(1)}, u32[]{:S(2)}, u32[]{:S(2)}) %collective-permute-start.13) | collective-permute-done | bytes 612 | tf_op jit(solution)/shard_map/ppermute | solution.py:17
  82.1 3.4 %collective-permute-start.14 = (f32[145]{0:T(256)S(1)}, f32[145]{0:T(256)S(1)}, u32[]{:S(2)}, u32[]{:S(2)}) collective-permute-start(f32[145]{0:T(256)S(1)} %add.83), channel_id=1, source_target_pairs={{0,8},{1,9},{2,10},{3,11},{4,12},{5,13},{6,14},{7,15},{8,0},{9,1},... | collective-permute-start | bytes 1748 | tf_op jit(solution)/shard_map/ppermute | solution.py:17
  85.5 5.9 %collective-permute-done.14 = f32[145]{0:T(256)S(1)} collective-permute-done((f32[145]{0:T(256)S(1)}, f32[145]{0:T(256)S(1)}, u32[]{:S(2)}, u32[]{:S(2)}) %collective-permute-start.14) | collective-permute-done | bytes 612 | tf_op jit(solution)/shard_map/ppermute | solution.py:17
  91.4 7.4 %collective-permute-start.15 = (f32[145]{0:T(256)S(1)}, f32[145]{0:T(256)S(1)}, u32[]{:S(2)}, u32[]{:S(2)}) collective-permute-start(f32[145]{0:T(256)S(1)} %add.84), channel_id=1, source_target_pairs={{0,16},{1,17},{2,18},{3,19},{4,20},{5,21},{6,22},{7,23},{8,24},{9,... | collective-permute-start | bytes 1748 | tf_op jit(solution)/shard_map/ppermute | solution.py:17
  98.8 6.8 %collective-permute-done.15 = f32[145]{0:T(256)S(1)} collective-permute-done((f32[145]{0:T(256)S(1)}, f32[145]{0:T(256)S(1)}, u32[]{:S(2)}, u32[]{:S(2)}) %collective-permute-start.15) | collective-permute-done | bytes 612 | tf_op jit(solution)/shard_map/ppermute | solution.py:17
  105.6 0.6 slice.102
  106.2 0.0 collective-permute-done.4
  106.2 0.1 pad_maximum_fusion
  106.3 0.2 compare_reduce_fusion
  106.5 0.1 select_bitcast_fusion
  106.7 0.1 copy.11
  106.9 0.1 copy.14
  107.0 0.0 copy-done
  107.0 0.7 fusion.5
  107.7 0.0 copy-start.1
  107.8 0.2 slice_maximum_fusion
  107.9 0.0 collective-permute-start.6
  108.0 0.5 collective-permute-start.5
  108.5 0.6 slice_divide_fusion
  109.1 3.3 %collective-permute-done.6 = f32[148,2,2,2]{3,0,2,1:T(8,128)S(1)} collective-permute-done((f32[148,2,2,2]{3,0,2,1:T(8,128)S(1)}, f32[148,2,2,2]{3,0,2,1:T(8,128)S(1)}, u32[]{:S(2)}, u32[]{:S(2)}) %collective-permute-start.6) | collective-permute-done | bytes 4768 | tf_op jit(solution)/shard_map/ppermute | solution.py:32
  112.4 3.9 %collective-permute-done.5 = f32[148,2,2,2]{3,0,2,1:T(8,128)S(1)} collective-permute-done((f32[148,2,2,2]{3,0,2,1:T(8,128)S(1)}, f32[148,2,2,2]{3,0,2,1:T(8,128)S(1)}, u32[]{:S(2)}, u32[]{:S(2)}) %collective-permute-start.5) | collective-permute-done | bytes 4768 | tf_op jit(solution)/shard_map/ppermute | solution.py:29
  116.2 0.3 pad_maximum_fusion.1
  116.6 0.4 fusion.1
  117.0 0.0 copy-done.1
  117.0 0.1 slice_add_fusion.2
  117.1 0.7 copy.12
  (20 shorter events, 0.4 us)
Async XLA Ops:
  0.0 107.0 %copy-start = (bf16[1,1,8,256,768]{4,3,2,1,0:T(8,128)(2,1)S(1)}, bf16[1,1,8,256,768]{4,3,2,1,0:T(8,128)(2,1)}, u32[]{:S(2)}) copy-start(bf16[1,1,8,256,768]{4,3,2,1,0:T(8,128)(2,1)} %param.7) | copy-start | bytes 9437188
  2.4 13.4 %collective-permute-start = (bf16[148,256]{1,0:T(8,128)(2,1)S(1)}, bf16[148,256]{1,0:T(8,128)(2,1)S(1)}, u32[]{:S(2)}, u32[]{:S(2)}) collective-permute-start(bf16[148,256]{1,0:T(8,128)(2,1)S(1)} %concatenate.9), channel_id=1, source_target_pairs={{0,30},{1,31},{2,0},{3,1},{4,2},{5,3},{6,4},{7,5},{8,6},{9,7},{10,... | collective-permute-start | bytes 227336 | tf_op jit(solution)/shard_map/ppermute | solution.py:9
  15.8 7.5 %collective-permute-start.1 = (bf16[148,256]{1,0:T(8,128)(2,1)S(1)}, bf16[148,256]{1,0:T(8,128)(2,1)S(1)}, u32[]{:S(2)}, u32[]{:S(2)}) collective-permute-start(bf16[148,256]{1,0:T(8,128)(2,1)S(1)} %collective-permute-done), channel_id=1, source_target_pairs={{0,30},{1,31},{2,0},{3,1},{4,2},{5,3},{6,4},{7,5},{8,6},{9,7},{10,... | collective-permute-start | bytes 227336 | tf_op jit(solution)/shard_map/ppermute | solution.py:9
  23.3 7.5 %collective-permute-start.2 = (bf16[148,256]{1,0:T(8,128)(2,1)S(1)}, bf16[148,256]{1,0:T(8,128)(2,1)S(1)}, u32[]{:S(2)}, u32[]{:S(2)}) collective-permute-start(bf16[148,256]{1,0:T(8,128)(2,1)S(1)} %collective-permute-done.1), channel_id=1, source_target_pairs={{0,30},{1,31},{2,0},{3,1},{4,2},{5,3},{6,4},{7,5},{8,6},{9,7},{10,... | collective-permute-start | bytes 227336 | tf_op jit(solution)/shard_map/ppermute | solution.py:9
  30.8 7.5 %collective-permute-start.3 = (bf16[148,256]{1,0:T(8,128)(2,1)S(1)}, bf16[148,256]{1,0:T(8,128)(2,1)S(1)}, u32[]{:S(2)}, u32[]{:S(2)}) collective-permute-start(bf16[148,256]{1,0:T(8,128)(2,1)S(1)} %collective-permute-done.2), channel_id=1, source_target_pairs={{0,30},{1,31},{2,0},{3,1},{4,2},{5,3},{6,4},{7,5},{8,6},{9,7},{10,... | collective-permute-start | bytes 227336 | tf_op jit(solution)/shard_map/ppermute | solution.py:9
  38.4 67.8 %collective-permute-start.4 = (bf16[4,148,256]{2,1,0:T(8,128)(2,1)S(1)}, bf16[4,148,256]{2,1,0:T(8,128)(2,1)S(1)}, u32[]{:S(2)}, u32[]{:S(2)}) collective-permute-start(bf16[4,148,256]{2,1,0:T(8,128)(2,1)S(1)} %pad_maximum_fusion.3), channel_id=1, source_target_pairs={{0,1},{1,0},{2,3},{3,2},{4,5},{5,4},{6,7},{7,6},{8,9},{9,8},{10,11... | collective-permute-start | bytes 909320 | tf_op jit(solution)/shard_map/ppermute | solution.py:67
  42.3 5.5 %collective-permute-start.7 = (f32[145]{0:T(256)S(1)}, f32[145]{0:T(256)S(1)}, u32[]{:S(2)}, u32[]{:S(2)}) collective-permute-start(f32[145]{0:T(256)S(1)} %pad_maximum_fusion.4), channel_id=1, source_target_pairs={{0,32},{32,0},{64,96},{96,64},{128,160},{160,128},{192,224},{224,1... | collective-permute-start | bytes 1748 | tf_op jit(solution)/shard_map/ppermute | solution.py:17
  47.8 7.0 %collective-permute-start.8 = (f32[145]{0:T(256)S(1)}, f32[145]{0:T(256)S(1)}, u32[]{:S(2)}, u32[]{:S(2)}) collective-permute-start(f32[145]{0:T(256)S(1)} %add.77), channel_id=1, source_target_pairs={{0,64},{32,96},{64,0},{96,32},{128,192},{160,224},{192,128},{224,1... | collective-permute-start | bytes 1748 | tf_op jit(solution)/shard_map/ppermute | solution.py:17
  54.8 5.5 %collective-permute-start.9 = (f32[145]{0:T(256)S(1)}, f32[145]{0:T(256)S(1)}, u32[]{:S(2)}, u32[]{:S(2)}) collective-permute-start(f32[145]{0:T(256)S(1)} %add.78), channel_id=1, source_target_pairs={{0,128},{32,160},{64,192},{96,224},{128,0},{160,32},{192,64},{224,... | collective-permute-start | bytes 1748 | tf_op jit(solution)/shard_map/ppermute | solution.py:17
  60.2 7.0 %collective-permute-start.10 = (f32[145]{0:T(256)S(1)}, f32[145]{0:T(256)S(1)}, u32[]{:S(2)}, u32[]{:S(2)}) collective-permute-start(f32[145]{0:T(256)S(1)} %add.79), channel_id=1, source_target_pairs={{0,256},{32,288},{64,320},{96,352},{128,384},{160,416},{192,448},{... | collective-permute-start | bytes 1748 | tf_op jit(solution)/shard_map/ppermute | solution.py:17
  67.2 3.0 %collective-permute-start.11 = (f32[145]{0:T(256)S(1)}, f32[145]{0:T(256)S(1)}, u32[]{:S(2)}, u32[]{:S(2)}) collective-permute-start(f32[145]{0:T(256)S(1)} %add.80), channel_id=1, source_target_pairs={{0,1},{1,0},{2,3},{3,2},{4,5},{5,4},{6,7},{7,6},{8,9},{9,8},{10,11... | collective-permute-start | bytes 1748 | tf_op jit(solution)/shard_map/ppermute | solution.py:17
  70.2 5.5 %collective-permute-start.12 = (f32[145]{0:T(256)S(1)}, f32[145]{0:T(256)S(1)}, u32[]{:S(2)}, u32[]{:S(2)}) collective-permute-start(f32[145]{0:T(256)S(1)} %add.81), channel_id=1, source_target_pairs={{0,2},{1,3},{2,0},{3,1},{4,6},{5,7},{6,4},{7,5},{8,10},{9,11},{10,... | collective-permute-start | bytes 1748 | tf_op jit(solution)/shard_map/ppermute | solution.py:17
  75.7 6.4 %collective-permute-start.13 = (f32[145]{0:T(256)S(1)}, f32[145]{0:T(256)S(1)}, u32[]{:S(2)}, u32[]{:S(2)}) collective-permute-start(f32[145]{0:T(256)S(1)} %add.82), channel_id=1, source_target_pairs={{0,4},{1,5},{2,6},{3,7},{4,0},{5,1},{6,2},{7,3},{8,12},{9,13},{10,... | collective-permute-start | bytes 1748 | tf_op jit(solution)/shard_map/ppermute | solution.py:17
  82.1 9.4 %collective-permute-start.14 = (f32[145]{0:T(256)S(1)}, f32[145]{0:T(256)S(1)}, u32[]{:S(2)}, u32[]{:S(2)}) collective-permute-start(f32[145]{0:T(256)S(1)} %add.83), channel_id=1, source_target_pairs={{0,8},{1,9},{2,10},{3,11},{4,12},{5,13},{6,14},{7,15},{8,0},{9,1},... | collective-permute-start | bytes 1748 | tf_op jit(solution)/shard_map/ppermute | solution.py:17
  91.4 14.2 %collective-permute-start.15 = (f32[145]{0:T(256)S(1)}, f32[145]{0:T(256)S(1)}, u32[]{:S(2)}, u32[]{:S(2)}) collective-permute-start(f32[145]{0:T(256)S(1)} %add.84), channel_id=1, source_target_pairs={{0,16},{1,17},{2,18},{3,19},{4,20},{5,21},{6,22},{7,23},{8,24},{9,... | collective-permute-start | bytes 1748 | tf_op jit(solution)/shard_map/ppermute | solution.py:17
  107.7 9.2 %copy-start.1 = (f32[2,128]{1,0:T(2,128)S(1)}, f32[2,128]{1,0:T(2,128)}, u32[]{:S(2)}) copy-start(f32[2,128]{1,0:T(2,128)} %param.5) | copy-start | bytes 3076
  107.9 4.4 %collective-permute-start.6 = (f32[148,2,2,2]{3,0,2,1:T(8,128)S(1)}, f32[148,2,2,2]{3,0,2,1:T(8,128)S(1)}, u32[]{:S(2)}, u32[]{:S(2)}) collective-permute-start(f32[148,2,2,2]{3,0,2,1:T(8,128)S(1)} %get-tuple-element.20), channel_id=1, source_target_pairs={{1,0},{2,1},{3,2},{4,3},{5,4},{6,5},{7,6},{8,7},{9,8},{10,9},{11,1... | collective-permute-start | bytes 14216 | tf_op jit(solution)/shard_map/ppermute | solution.py:32
  108.0 8.3 %collective-permute-start.5 = (f32[148,2,2,2]{3,0,2,1:T(8,128)S(1)}, f32[148,2,2,2]{3,0,2,1:T(8,128)S(1)}, u32[]{:S(2)}, u32[]{:S(2)}) collective-permute-start(f32[148,2,2,2]{3,0,2,1:T(8,128)S(1)} %get-tuple-element.19), channel_id=1, source_target_pairs={{0,1},{1,2},{2,3},{3,4},{4,5},{5,6},{6,7},{7,8},{8,9},{9,10},{10,1... | collective-permute-start | bytes 14216 | tf_op jit(solution)/shard_map/ppermute | solution.py:29

commit v7 on v6

--- a/solution.py
+++ b/solution.py
@@ -9,14 +9,43 @@
     return lax.ppermute(value, axis, [(i, (i + by) % length) for i in range(length)])
 
 
+def xor_rounds(length):
+    rounds, step = [], 1
+    while step < length:
+        rounds.append([i ^ step for i in range(length)])
+        step *= 2
+    return rounds
+
+
+def lat_rounds(length):
+    if length != 16:
+        return xor_rounds(length)
+    def mirror(i, scale):
+        digit = (i // scale) % 4
+        return i + (3 - 2 * digit) * scale
+    return [
+        [i ^ 1 for i in range(length)],
+        [mirror(i, 1) for i in range(length)],
+        [i ^ 4 for i in range(length)],
+        [mirror(i, 4) for i in range(length)],
+    ]
+
+
+def lon_rounds(length):
+    if length != 32:
+        return xor_rounds(length)
+    def across(i):
+        chip, core = divmod(i, 2)
+        return 2 * ((chip + (12 if chip < 4 else 4 if chip < 8 else -4 if chip < 12 else -12)) % 16) + core
+    return xor_rounds(length)[:4] + [[across(i) for i in range(length)]]
+
+
 def butterfly_sum(value, axes):
     for axis in axes:
         length = lax.axis_size(axis)
-        step = 1
-        while step < length:
-            partner = lax.ppermute(value, axis, [(i, i ^ step) for i in range(length)])
+        for partner_of in (lat_rounds if axis == "lat" else lon_rounds)(length):
+            partner = lax.ppermute(value, axis, [(i, partner_of[i]) for i in range(length)])
             value = value + partner
-            step *= 2
     return value
 
 

time: 118 us -> 113 us (0.958)
  the two profiles are of different devices: /device:TPU:4 before, /device:TPU:30 now
where the time goes in v7:
time: 113 us; the launch traced here: 112 us
  starting transfers between devices  54.8 us (48%)
  waiting for transfers between devices  46.5 us (41%)
  other arithmetic  6.81 us (6%)
  local copies, waits for them, and re-layouts  2.75 us (2%)
    ppermute x9, waiting for transfers between devices, butterfly_sum(): lax.ppermute(value, axis, [(i, partner_of[i]) for i in range(length)])  33.3 us
    ppermute x4, starting transfers between devices, shifted(): lax.ppermute(value, axis, [(i, (i + by) % length) for i in range(length)])  27.8 us
    ppermute x9, starting transfers between devices, butterfly_sum(): lax.ppermute(value, axis, [(i, partner_of[i]) for i in range(length)])  24.5 us
    ppermute x4, waiting for transfers between devices, shifted(): lax.ppermute(value, axis, [(i, (i + by) % length) for i in range(length)])  6.07 us
    ppermute x1, waiting for transfers between devices, padded_2(): lax.ppermute(lax.slice_in_dim(block, block.shape[dim] - width, None, axis...  3.86 us
    ppermute x1, waiting for transfers between devices, padded_2(): lax.ppermute(lax.slice_in_dim(block, 0, width, axis=dim), axis, backward)  3.26 us
  transfers between devices with their start and end apart: 16, of which 15 were waited for; matrix products, arithmetic and copies ran while one was open for 5% of the time, Pallas kernels for 0%

profile of v7, /device:TPU:30, one launch (start us, length us, event | category | flops | bytes accessed | tf_op | source)
XLA Modules:
  0.0 112.4 jit_solution(1289129205123569322)
XLA Ops:
  0.0 0.0 copy-start
  0.0 1.0 copy.16
  1.1 0.7 fusion.4
  2.4 11.4 %collective-permute-start = (bf16[148,256]{1,0:T(8,128)(2,1)S(1)}, bf16[148,256]{1,0:T(8,128)(2,1)S(1)}, u32[]{:S(2)}, u32[]{:S(2)}) collective-permute-start(bf16[148,256]{1,0:T(8,128)(2,1)S(1)} %concatenate.9), channel_id=1, source_target_pairs={{0,30},{1,31},{2,0},{3,1},{4,2},{5,3},{6,4},{7,5},{8,6},{9,7},{10,... | collective-permute-start | bytes 227336 | tf_op jit(solution)/shard_map/ppermute | solution.py:9
  13.8 2.0 %collective-permute-done = bf16[148,256]{1,0:T(8,128)(2,1)S(1)} collective-permute-done((bf16[148,256]{1,0:T(8,128)(2,1)S(1)}, bf16[148,256]{1,0:T(8,128)(2,1)S(1)}, u32[]{:S(2)}, u32[]{:S(2)}) %collective-permute-start) | collective-permute-done | bytes 75808 | tf_op jit(solution)/shard_map/ppermute | solution.py:9
  15.8 5.5 %collective-permute-start.1 = (bf16[148,256]{1,0:T(8,128)(2,1)S(1)}, bf16[148,256]{1,0:T(8,128)(2,1)S(1)}, u32[]{:S(2)}, u32[]{:S(2)}) collective-permute-start(bf16[148,256]{1,0:T(8,128)(2,1)S(1)} %collective-permute-done), channel_id=1, source_target_pairs={{0,30},{1,31},{2,0},{3,1},{4,2},{5,3},{6,4},{7,5},{8,6},{9,7},{10,... | collective-permute-start | bytes 227336 | tf_op jit(solution)/shard_map/ppermute | solution.py:9
  21.3 2.0 %collective-permute-done.1 = bf16[148,256]{1,0:T(8,128)(2,1)S(1)} collective-permute-done((bf16[148,256]{1,0:T(8,128)(2,1)S(1)}, bf16[148,256]{1,0:T(8,128)(2,1)S(1)}, u32[]{:S(2)}, u32[]{:S(2)}) %collective-permute-start.1) | collective-permute-done | bytes 75808 | tf_op jit(solution)/shard_map/ppermute | solution.py:9
  23.3 5.5 %collective-permute-start.2 = (bf16[148,256]{1,0:T(8,128)(2,1)S(1)}, bf16[148,256]{1,0:T(8,128)(2,1)S(1)}, u32[]{:S(2)}, u32[]{:S(2)}) collective-permute-start(bf16[148,256]{1,0:T(8,128)(2,1)S(1)} %collective-permute-done.1), channel_id=1, source_target_pairs={{0,30},{1,31},{2,0},{3,1},{4,2},{5,3},{6,4},{7,5},{8,6},{9,7},{10,... | collective-permute-start | bytes 227336 | tf_op jit(solution)/shard_map/ppermute | solution.py:9
  28.8 2.0 %collective-permute-done.2 = bf16[148,256]{1,0:T(8,128)(2,1)S(1)} collective-permute-done((bf16[148,256]{1,0:T(8,128)(2,1)S(1)}, bf16[148,256]{1,0:T(8,128)(2,1)S(1)}, u32[]{:S(2)}, u32[]{:S(2)}) %collective-permute-start.2) | collective-permute-done | bytes 75808 | tf_op jit(solution)/shard_map/ppermute | solution.py:9
  30.8 5.5 %collective-permute-start.3 = (bf16[148,256]{1,0:T(8,128)(2,1)S(1)}, bf16[148,256]{1,0:T(8,128)(2,1)S(1)}, u32[]{:S(2)}, u32[]{:S(2)}) collective-permute-start(bf16[148,256]{1,0:T(8,128)(2,1)S(1)} %collective-permute-done.2), channel_id=1, source_target_pairs={{0,30},{1,31},{2,0},{3,1},{4,2},{5,3},{6,4},{7,5},{8,6},{9,7},{10,... | collective-permute-start | bytes 227336 | tf_op jit(solution)/shard_map/ppermute | solution.py:9
  36.3 1.9 %multiply_reduce_fusion = f32[144]{0:T(256)S(1)} fusion(bf16[144,2,128]{2,1,0:T(2,128)(2,1)} %param.4, f32[2,128]{1,0:T(2,128)} %param.5), kind=kLoop, calls=%fused_computation.24 | loop fusion | flops 110448 | bytes 75328 | tf_op jit(solution)/shard_map/reduce_sum | solution.py:79
  38.2 0.1 collective-permute-done.3
  38.4 1.9 %collective-permute-start.4 = (bf16[4,148,256]{2,1,0:T(8,128)(2,1)S(1)}, bf16[4,148,256]{2,1,0:T(8,128)(2,1)S(1)}, u32[]{:S(2)}, u32[]{:S(2)}) collective-permute-start(bf16[4,148,256]{2,1,0:T(8,128)(2,1)S(1)} %pad_maximum_fusion.3), channel_id=1, source_target_pairs={{0,1},{1,0},{2,3},{3,2},{4,5},{5,4},{6,7},{7,6},{8,9},{9,8},{10,11... | collective-permute-start | bytes 909320 | tf_op jit(solution)/shard_map/ppermute | solution.py:96
  40.3 1.3 %multiply_reduce_fusion.1 = f32[]{:T(128)} fusion(f32[2,128]{1,0:T(2,128)} %param.5), kind=kLoop, calls=%fused_computation.49 | loop fusion | flops 511 | bytes 1028 | tf_op jit(solution)/shard_map/reduce_sum | solution.py:80
  41.6 0.7 pad_maximum_fusion.4
  42.3 2.7 %collective-permute-start.7 = (f32[145]{0:T(256)S(1)}, f32[145]{0:T(256)S(1)}, u32[]{:S(2)}, u32[]{:S(2)}) collective-permute-start(f32[145]{0:T(256)S(1)} %pad_maximum_fusion.4), channel_id=1, source_target_pairs={{0,32},{32,0},{64,96},{96,64},{128,160},{160,128},{192,224},{224,1... | collective-permute-start | bytes 1748 | tf_op jit(solution)/shard_map/ppermute | solution.py:47
  45.1 2.7 %collective-permute-done.7 = f32[145]{0:T(256)S(1)} collective-permute-done((f32[145]{0:T(256)S(1)}, f32[145]{0:T(256)S(1)}, u32[]{:S(2)}, u32[]{:S(2)}) %collective-permute-start.7) | collective-permute-done | bytes 612 | tf_op jit(solution)/shard_map/ppermute | solution.py:47
  47.8 2.4 %collective-permute-start.8 = (f32[145]{0:T(256)S(1)}, f32[145]{0:T(256)S(1)}, u32[]{:S(2)}, u32[]{:S(2)}) collective-permute-start(f32[145]{0:T(256)S(1)} %add.77), channel_id=1, source_target_pairs={{0,96},{32,64},{64,32},{96,0},{128,224},{160,192},{192,160},{224,1... | collective-permute-start | bytes 1748 | tf_op jit(solution)/shard_map/ppermute | solution.py:47
  50.2 4.3 %collective-permute-done.8 = f32[145]{0:T(256)S(1)} collective-permute-done((f32[145]{0:T(256)S(1)}, f32[145]{0:T(256)S(1)}, u32[]{:S(2)}, u32[]{:S(2)}) %collective-permute-start.8) | collective-permute-done | bytes 612 | tf_op jit(solution)/shard_map/ppermute | solution.py:47
  54.5 2.6 %collective-permute-start.9 = (f32[145]{0:T(256)S(1)}, f32[145]{0:T(256)S(1)}, u32[]{:S(2)}, u32[]{:S(2)}) collective-permute-start(f32[145]{0:T(256)S(1)} %add.78), channel_id=1, source_target_pairs={{0,128},{32,160},{64,192},{96,224},{128,0},{160,32},{192,64},{224,... | collective-permute-start | bytes 1748 | tf_op jit(solution)/shard_map/ppermute | solution.py:47
  57.1 2.8 %collective-permute-done.9 = f32[145]{0:T(256)S(1)} collective-permute-done((f32[145]{0:T(256)S(1)}, f32[145]{0:T(256)S(1)}, u32[]{:S(2)}, u32[]{:S(2)}) %collective-permute-start.9) | collective-permute-done | bytes 612 | tf_op jit(solution)/shard_map/ppermute | solution.py:47
  59.9 2.1 %collective-permute-start.10 = (f32[145]{0:T(256)S(1)}, f32[145]{0:T(256)S(1)}, u32[]{:S(2)}, u32[]{:S(2)}) collective-permute-start(f32[145]{0:T(256)S(1)} %add.79), channel_id=1, source_target_pairs={{0,384},{32,416},{64,448},{96,480},{128,256},{160,288},{192,320},{... | collective-permute-start | bytes 1748 | tf_op jit(solution)/shard_map/ppermute | solution.py:47
  62.1 4.5 %collective-permute-done.10 = f32[145]{0:T(256)S(1)} collective-permute-done((f32[145]{0:T(256)S(1)}, f32[145]{0:T(256)S(1)}, u32[]{:S(2)}, u32[]{:S(2)}) %collective-permute-start.10) | collective-permute-done | bytes 612 | tf_op jit(solution)/shard_map/ppermute | solution.py:47
  66.6 1.9 %collective-permute-start.11 = (f32[145]{0:T(256)S(1)}, f32[145]{0:T(256)S(1)}, u32[]{:S(2)}, u32[]{:S(2)}) collective-permute-start(f32[145]{0:T(256)S(1)} %add.80), channel_id=1, source_target_pairs={{0,1},{1,0},{2,3},{3,2},{4,5},{5,4},{6,7},{7,6},{8,9},{9,8},{10,11... | collective-permute-start | bytes 1748 | tf_op jit(solution)/shard_map/ppermute | solution.py:47
  68.5 1.1 %collective-permute-done.11 = f32[145]{0:T(256)S(1)} collective-permute-done((f32[145]{0:T(256)S(1)}, f32[145]{0:T(256)S(1)}, u32[]{:S(2)}, u32[]{:S(2)}) %collective-permute-start.11) | collective-permute-done | bytes 612 | tf_op jit(solution)/shard_map/ppermute | solution.py:47
  69.6 1.9 %collective-permute-start.12 = (f32[145]{0:T(256)S(1)}, f32[145]{0:T(256)S(1)}, u32[]{:S(2)}, u32[]{:S(2)}) collective-permute-start(f32[145]{0:T(256)S(1)} %add.81), channel_id=1, source_target_pairs={{0,2},{1,3},{2,0},{3,1},{4,6},{5,7},{6,4},{7,5},{8,10},{9,11},{10,... | collective-permute-start | bytes 1748 | tf_op jit(solution)/shard_map/ppermute | solution.py:47
  71.6 3.5 %collective-permute-done.12 = f32[145]{0:T(256)S(1)} collective-permute-done((f32[145]{0:T(256)S(1)}, f32[145]{0:T(256)S(1)}, u32[]{:S(2)}, u32[]{:S(2)}) %collective-permute-start.12) | collective-permute-done | bytes 612 | tf_op jit(solution)/shard_map/ppermute | solution.py:47
  75.1 1.9 %collective-permute-start.13 = (f32[145]{0:T(256)S(1)}, f32[145]{0:T(256)S(1)}, u32[]{:S(2)}, u32[]{:S(2)}) collective-permute-start(f32[145]{0:T(256)S(1)} %add.82), channel_id=1, source_target_pairs={{0,4},{1,5},{2,6},{3,7},{4,0},{5,1},{6,2},{7,3},{8,12},{9,13},{10,... | collective-permute-start | bytes 1748 | tf_op jit(solution)/shard_map/ppermute | solution.py:47
  77.0 4.4 %collective-permute-done.13 = f32[145]{0:T(256)S(1)} collective-permute-done((f32[145]{0:T(256)S(1)}, f32[145]{0:T(256)S(1)}, u32[]{:S(2)}, u32[]{:S(2)}) %collective-permute-start.13) | collective-permute-done | bytes 612 | tf_op jit(solution)/shard_map/ppermute | solution.py:47
  81.5 3.4 %collective-permute-start.14 = (f32[145]{0:T(256)S(1)}, f32[145]{0:T(256)S(1)}, u32[]{:S(2)}, u32[]{:S(2)}) collective-permute-start(f32[145]{0:T(256)S(1)} %add.83), channel_id=1, source_target_pairs={{0,8},{1,9},{2,10},{3,11},{4,12},{5,13},{6,14},{7,15},{8,0},{9,1},... | collective-permute-start | bytes 1748 | tf_op jit(solution)/shard_map/ppermute | solution.py:47
  84.9 5.9 %collective-permute-done.14 = f32[145]{0:T(256)S(1)} collective-permute-done((f32[145]{0:T(256)S(1)}, f32[145]{0:T(256)S(1)}, u32[]{:S(2)}, u32[]{:S(2)}) %collective-permute-start.14) | collective-permute-done | bytes 612 | tf_op jit(solution)/shard_map/ppermute | solution.py:47
  90.8 5.4 %collective-permute-start.15 = (f32[145]{0:T(256)S(1)}, f32[145]{0:T(256)S(1)}, u32[]{:S(2)}, u32[]{:S(2)}) collective-permute-start(f32[145]{0:T(256)S(1)} %add.84), channel_id=1, source_target_pairs={{0,24},{1,25},{2,26},{3,27},{4,28},{5,29},{6,30},{7,31},{8,16},{9,... | collective-permute-start | bytes 1748 | tf_op jit(solution)/shard_map/ppermute | solution.py:47
  96.3 3.9 %collective-permute-done.15 = f32[145]{0:T(256)S(1)} collective-permute-done((f32[145]{0:T(256)S(1)}, f32[145]{0:T(256)S(1)}, u32[]{:S(2)}, u32[]{:S(2)}) %collective-permute-start.15) | collective-permute-done | bytes 612 | tf_op jit(solution)/shard_map/ppermute | solution.py:47
  100.2 0.6 slice.102
  100.8 0.0 collective-permute-done.4
  100.8 0.1 pad_maximum_fusion
  100.9 0.2 compare_reduce_fusion
  101.2 0.1 select_bitcast_fusion
  101.3 0.1 copy.11
  101.5 0.1 copy.14
  101.6 0.0 copy-done
  101.6 0.7 fusion.5
  102.3 0.0 copy-start.1
  102.4 0.2 slice_maximum_fusion
  102.5 0.0 collective-permute-start.6
  102.6 0.5 collective-permute-start.5
  103.1 0.6 slice_divide_fusion
  103.7 3.3 %collective-permute-done.6 = f32[148,2,2,2]{3,0,2,1:T(8,128)S(1)} collective-permute-done((f32[148,2,2,2]{3,0,2,1:T(8,128)S(1)}, f32[148,2,2,2]{3,0,2,1:T(8,128)S(1)}, u32[]{:S(2)}, u32[]{:S(2)}) %collective-permute-start.6) | collective-permute-done | bytes 4768 | tf_op jit(solution)/shard_map/ppermute | solution.py:61
  107.0 3.9 %collective-permute-done.5 = f32[148,2,2,2]{3,0,2,1:T(8,128)S(1)} collective-permute-done((f32[148,2,2,2]{3,0,2,1:T(8,128)S(1)}, f32[148,2,2,2]{3,0,2,1:T(8,128)S(1)}, u32[]{:S(2)}, u32[]{:S(2)}) %collective-permute-start.5) | collective-permute-done | bytes 4768 | tf_op jit(solution)/shard_map/ppermute | solution.py:58
  110.8 0.3 pad_maximum_fusion.1
  111.2 0.4 fusion.1
  111.6 0.0 copy-done.1
  111.6 0.1 slice_add_fusion.2
  111.7 0.7 copy.12
  (20 shorter events, 0.4 us)
Async XLA Ops:
  0.0 101.6 %copy-start = (bf16[1,1,8,256,768]{4,3,2,1,0:T(8,128)(2,1)S(1)}, bf16[1,1,8,256,768]{4,3,2,1,0:T(8,128)(2,1)}, u32[]{:S(2)}) copy-start(bf16[1,1,8,256,768]{4,3,2,1,0:T(8,128)(2,1)} %param.7) | copy-start | bytes 9437188
  2.4 13.4 %collective-permute-start = (bf16[148,256]{1,0:T(8,128)(2,1)S(1)}, bf16[148,256]{1,0:T(8,128)(2,1)S(1)}, u32[]{:S(2)}, u32[]{:S(2)}) collective-permute-start(bf16[148,256]{1,0:T(8,128)(2,1)S(1)} %concatenate.9), channel_id=1, source_target_pairs={{0,30},{1,31},{2,0},{3,1},{4,2},{5,3},{6,4},{7,5},{8,6},{9,7},{10,... | collective-permute-start | bytes 227336 | tf_op jit(solution)/shard_map/ppermute | solution.py:9
  15.8 7.5 %collective-permute-start.1 = (bf16[148,256]{1,0:T(8,128)(2,1)S(1)}, bf16[148,256]{1,0:T(8,128)(2,1)S(1)}, u32[]{:S(2)}, u32[]{:S(2)}) collective-permute-start(bf16[148,256]{1,0:T(8,128)(2,1)S(1)} %collective-permute-done), channel_id=1, source_target_pairs={{0,30},{1,31},{2,0},{3,1},{4,2},{5,3},{6,4},{7,5},{8,6},{9,7},{10,... | collective-permute-start | bytes 227336 | tf_op jit(solution)/shard_map/ppermute | solution.py:9
  23.3 7.5 %collective-permute-start.2 = (bf16[148,256]{1,0:T(8,128)(2,1)S(1)}, bf16[148,256]{1,0:T(8,128)(2,1)S(1)}, u32[]{:S(2)}, u32[]{:S(2)}) collective-permute-start(bf16[148,256]{1,0:T(8,128)(2,1)S(1)} %collective-permute-done.1), channel_id=1, source_target_pairs={{0,30},{1,31},{2,0},{3,1},{4,2},{5,3},{6,4},{7,5},{8,6},{9,7},{10,... | collective-permute-start | bytes 227336 | tf_op jit(solution)/shard_map/ppermute | solution.py:9
  30.8 7.5 %collective-permute-start.3 = (bf16[148,256]{1,0:T(8,128)(2,1)S(1)}, bf16[148,256]{1,0:T(8,128)(2,1)S(1)}, u32[]{:S(2)}, u32[]{:S(2)}) collective-permute-start(bf16[148,256]{1,0:T(8,128)(2,1)S(1)} %collective-permute-done.2), channel_id=1, source_target_pairs={{0,30},{1,31},{2,0},{3,1},{4,2},{5,3},{6,4},{7,5},{8,6},{9,7},{10,... | collective-permute-start | bytes 227336 | tf_op jit(solution)/shard_map/ppermute | solution.py:9
  38.4 62.4 %collective-permute-start.4 = (bf16[4,148,256]{2,1,0:T(8,128)(2,1)S(1)}, bf16[4,148,256]{2,1,0:T(8,128)(2,1)S(1)}, u32[]{:S(2)}, u32[]{:S(2)}) collective-permute-start(bf16[4,148,256]{2,1,0:T(8,128)(2,1)S(1)} %pad_maximum_fusion.3), channel_id=1, source_target_pairs={{0,1},{1,0},{2,3},{3,2},{4,5},{5,4},{6,7},{7,6},{8,9},{9,8},{10,11... | collective-permute-start | bytes 909320 | tf_op jit(solution)/shard_map/ppermute | solution.py:96
  42.3 5.5 %collective-permute-start.7 = (f32[145]{0:T(256)S(1)}, f32[145]{0:T(256)S(1)}, u32[]{:S(2)}, u32[]{:S(2)}) collective-permute-start(f32[145]{0:T(256)S(1)} %pad_maximum_fusion.4), channel_id=1, source_target_pairs={{0,32},{32,0},{64,96},{96,64},{128,160},{160,128},{192,224},{224,1... | collective-permute-start | bytes 1748 | tf_op jit(solution)/shard_map/ppermute | solution.py:47
  47.8 6.7 %collective-permute-start.8 = (f32[145]{0:T(256)S(1)}, f32[145]{0:T(256)S(1)}, u32[]{:S(2)}, u32[]{:S(2)}) collective-permute-start(f32[145]{0:T(256)S(1)} %add.77), channel_id=1, source_target_pairs={{0,96},{32,64},{64,32},{96,0},{128,224},{160,192},{192,160},{224,1... | collective-permute-start | bytes 1748 | tf_op jit(solution)/shard_map/ppermute | solution.py:47
  54.5 5.5 %collective-permute-start.9 = (f32[145]{0:T(256)S(1)}, f32[145]{0:T(256)S(1)}, u32[]{:S(2)}, u32[]{:S(2)}) collective-permute-start(f32[145]{0:T(256)S(1)} %add.78), channel_id=1, source_target_pairs={{0,128},{32,160},{64,192},{96,224},{128,0},{160,32},{192,64},{224,... | collective-permute-start | bytes 1748 | tf_op jit(solution)/shard_map/ppermute | solution.py:47
  59.9 6.7 %collective-permute-start.10 = (f32[145]{0:T(256)S(1)}, f32[145]{0:T(256)S(1)}, u32[]{:S(2)}, u32[]{:S(2)}) collective-permute-start(f32[145]{0:T(256)S(1)} %add.79), channel_id=1, source_target_pairs={{0,384},{32,416},{64,448},{96,480},{128,256},{160,288},{192,320},{... | collective-permute-start | bytes 1748 | tf_op jit(solution)/shard_map/ppermute | solution.py:47
  66.6 3.0 %collective-permute-start.11 = (f32[145]{0:T(256)S(1)}, f32[145]{0:T(256)S(1)}, u32[]{:S(2)}, u32[]{:S(2)}) collective-permute-start(f32[145]{0:T(256)S(1)} %add.80), channel_id=1, source_target_pairs={{0,1},{1,0},{2,3},{3,2},{4,5},{5,4},{6,7},{7,6},{8,9},{9,8},{10,11... | collective-permute-start | bytes 1748 | tf_op jit(solution)/shard_map/ppermute | solution.py:47
  69.6 5.5 %collective-permute-start.12 = (f32[145]{0:T(256)S(1)}, f32[145]{0:T(256)S(1)}, u32[]{:S(2)}, u32[]{:S(2)}) collective-permute-start(f32[145]{0:T(256)S(1)} %add.81), channel_id=1, source_target_pairs={{0,2},{1,3},{2,0},{3,1},{4,6},{5,7},{6,4},{7,5},{8,10},{9,11},{10,... | collective-permute-start | bytes 1748 | tf_op jit(solution)/shard_map/ppermute | solution.py:47
  75.1 6.4 %collective-permute-start.13 = (f32[145]{0:T(256)S(1)}, f32[145]{0:T(256)S(1)}, u32[]{:S(2)}, u32[]{:S(2)}) collective-permute-start(f32[145]{0:T(256)S(1)} %add.82), channel_id=1, source_target_pairs={{0,4},{1,5},{2,6},{3,7},{4,0},{5,1},{6,2},{7,3},{8,12},{9,13},{10,... | collective-permute-start | bytes 1748 | tf_op jit(solution)/shard_map/ppermute | solution.py:47
  81.5 9.4 %collective-permute-start.14 = (f32[145]{0:T(256)S(1)}, f32[145]{0:T(256)S(1)}, u32[]{:S(2)}, u32[]{:S(2)}) collective-permute-start(f32[145]{0:T(256)S(1)} %add.83), channel_id=1, source_target_pairs={{0,8},{1,9},{2,10},{3,11},{4,12},{5,13},{6,14},{7,15},{8,0},{9,1},... | collective-permute-start | bytes 1748 | tf_op jit(solution)/shard_map/ppermute | solution.py:47
  90.8 9.4 %collective-permute-start.15 = (f32[145]{0:T(256)S(1)}, f32[145]{0:T(256)S(1)}, u32[]{:S(2)}, u32[]{:S(2)}) collective-permute-start(f32[145]{0:T(256)S(1)} %add.84), channel_id=1, source_target_pairs={{0,24},{1,25},{2,26},{3,27},{4,28},{5,29},{6,30},{7,31},{8,16},{9,... | collective-permute-start | bytes 1748 | tf_op jit(solution)/shard_map/ppermute | solution.py:47
  102.3 9.2 %copy-start.1 = (f32[2,128]{1,0:T(2,128)S(1)}, f32[2,128]{1,0:T(2,128)}, u32[]{:S(2)}) copy-start(f32[2,128]{1,0:T(2,128)} %param.5) | copy-start | bytes 3076
  102.5 4.4 %collective-permute-start.6 = (f32[148,2,2,2]{3,0,2,1:T(8,128)S(1)}, f32[148,2,2,2]{3,0,2,1:T(8,128)S(1)}, u32[]{:S(2)}, u32[]{:S(2)}) collective-permute-start(f32[148,2,2,2]{3,0,2,1:T(8,128)S(1)} %get-tuple-element.20), channel_id=1, source_target_pairs={{1,0},{2,1},{3,2},{4,3},{5,4},{6,5},{7,6},{8,7},{9,8},{10,9},{11,1... | collective-permute-start | bytes 14216 | tf_op jit(solution)/shard_map/ppermute | solution.py:61
  102.6 8.3 %collective-permute-start.5 = (f32[148,2,2,2]{3,0,2,1:T(8,128)S(1)}, f32[148,2,2,2]{3,0,2,1:T(8,128)S(1)}, u32[]{:S(2)}, u32[]{:S(2)}) collective-permute-start(f32[148,2,2,2]{3,0,2,1:T(8,128)S(1)} %get-tuple-element.19), channel_id=1, source_target_pairs={{0,1},{1,2},{2,3},{3,4},{4,5},{5,6},{6,7},{7,8},{8,9},{9,10},{10,1... | collective-permute-start | bytes 14216 | tf_op jit(solution)/shard_map/ppermute | solution.py:58

commit v8 on v7

--- a/solution.py
+++ b/solution.py
@@ -75,17 +75,19 @@
     fields, tile_rows, tile_cols = cotangent.shape
     cell_count = tile_rows * tile_cols
     slot_count = weights.shape[2]
-    cot_full = cotangent.astype(jnp.float32)
-    weighted = jnp.sum(cot_full * cell_area[None], axis=(1, 2))
-    squares = jnp.sum(cell_area * cell_area)
+    area_parts = split_bf16(cell_area.reshape(1, cell_count))
+    count_row = jnp.full((1, cell_count), reach_count[0, 0], jnp.float32).astype(jnp.bfloat16)
+    payload = jnp.concatenate([cotangent.reshape(fields, cell_count)] + area_parts + [count_row], axis=0)
+    payload = lax.optimization_barrier(payload)
+    products = jnp.dot(
+        payload[: fields + 3], jnp.concatenate(area_parts, axis=0).T, preferred_element_type=jnp.float32
+    ).sum(axis=1)
+    weighted = products[:fields]
+    squares = products[fields] + products[fields + 1] + products[fields + 2]
     stats, area_late = lax.optimization_barrier((jnp.concatenate([weighted, squares[None]]), cell_area))
     stats = butterfly_sum(stats, ("lat", "lon"))
     factor = stats[:fields] / stats[fields]
 
-    area_parts = split_bf16(cell_area.reshape(1, cell_count))
-    count_row = jnp.full((1, cell_count), reach_count[0, 0], jnp.float32).astype(jnp.bfloat16)
-    payload = jnp.concatenate([cotangent.reshape(fields, cell_count)] + area_parts + [count_row], axis=0)
-    payload = lax.optimization_barrier(payload)
     ring = [payload]
     for _ in range(slot_count // 2):
         ring.append(shifted(ring[-1], "lon", -2))
@@ -145,6 +147,4 @@
         P("lat", "lon", None, None, None),
     )
     out_specs = P(None, "lat", "lon")
-    return jax.shard_map(
-        on_device_body, mesh=mesh, in_specs=in_specs, out_specs=out_specs, check_vma=False
-    )
+    return jax.shard_map(on_device_body, mesh=mesh, in_specs=in_specs, out_specs=out_specs, check_vma=False)

time: 113 us -> 113 us (level)
  the two profiles are of different devices: /device:TPU:30 before, /device:TPU:1 now
where the time goes in v8:
time: 113 us
  starting transfers between devices  73 us (65%)
  waiting for transfers between devices  29.5 us (26%)
  local copies, waits for them, and re-layouts  3.27 us (3%)
  other arithmetic  3.11 us (3%)
  between operations  3.02 us (3%)
    ppermute x9, starting transfers between devices, butterfly_sum(): lax.ppermute(value, axis, [(i, partner_of[i]) for i in range(length)])  34.4 us
    ppermute x4, starting transfers between devices, shifted(): lax.ppermute(value, axis, [(i, (i + by) % length) for i in range(length)])  26.7 us
    ppermute x9, waiting for transfers between devices, butterfly_sum(): lax.ppermute(value, axis, [(i, partner_of[i]) for i in range(length)])  18.4 us
    ppermute x1, starting transfers between devices, on_device_body(): lax.ppermute(offer, 'lon', [(i, i ^ 1) for i in range(lax.axis_size('lon'...  6.89 us
    ppermute x4, waiting for transfers between devices, shifted(): lax.ppermute(value, axis, [(i, (i + by) % length) for i in range(length)])  5.54 us
    ppermute x1, starting transfers between devices, padded_2(): lax.ppermute(lax.slice_in_dim(block, block.shape[dim] - width, None, axis...  4.58 us
    ppermute x1, waiting for transfers between devices, padded_2(): lax.ppermute(lax.slice_in_dim(block, block.shape[dim] - width, None, axis...  2.78 us
    ppermute x1, waiting for transfers between devices, padded_2(): lax.ppermute(lax.slice_in_dim(block, 0, width, axis=dim), axis, backward)  2.77 us
  transfers between devices with their start and end apart: 16, of which 15 were waited for; matrix products, arithmetic and copies ran while one was open for 2% of the time, Pallas kernels for 0%

profile of v8, /device:TPU:1, one launch (start us, length us, event | category | flops | bytes accessed | tf_op | source)
XLA Modules:
  0.0 112.7 jit_solution(2815910409815992145)
XLA Ops:
  0.0 0.0 copy-start
  0.8 0.8 fusion.10
  1.6 0.9 copy.16
  2.6 11.9 %collective-permute-start = (bf16[148,256]{1,0:T(8,128)(2,1)S(1)}, bf16[148,256]{1,0:T(8,128)(2,1)S(1)}, u32[]{:S(2)}, u32[]{:S(2)}) collective-permute-start(bf16[148,256]{1,0:T(8,128)(2,1)S(1)} %concatenate.12), channel_id=1, source_target_pairs={{0,30},{1,31},{2,0},{3,1},{4,2},{5,3},{6,4},{7,5},{8,6},{9,7},{10,... | collective-permute-start | bytes 227336 | tf_op jit(solution)/shard_map/ppermute | solution.py:9
  14.5 1.4 %collective-permute-done = bf16[148,256]{1,0:T(8,128)(2,1)S(1)} collective-permute-done((bf16[148,256]{1,0:T(8,128)(2,1)S(1)}, bf16[148,256]{1,0:T(8,128)(2,1)S(1)}, u32[]{:S(2)}, u32[]{:S(2)}) %collective-permute-start) | collective-permute-done | bytes 75808 | tf_op jit(solution)/shard_map/ppermute | solution.py:9
  16.0 4.9 %collective-permute-start.1 = (bf16[148,256]{1,0:T(8,128)(2,1)S(1)}, bf16[148,256]{1,0:T(8,128)(2,1)S(1)}, u32[]{:S(2)}, u32[]{:S(2)}) collective-permute-start(bf16[148,256]{1,0:T(8,128)(2,1)S(1)} %collective-permute-done), channel_id=1, source_target_pairs={{0,30},{1,31},{2,0},{3,1},{4,2},{5,3},{6,4},{7,5},{8,6},{9,7},{10,... | collective-permute-start | bytes 227336 | tf_op jit(solution)/shard_map/ppermute | solution.py:9
  20.9 1.4 %collective-permute-done.1 = bf16[148,256]{1,0:T(8,128)(2,1)S(1)} collective-permute-done((bf16[148,256]{1,0:T(8,128)(2,1)S(1)}, bf16[148,256]{1,0:T(8,128)(2,1)S(1)}, u32[]{:S(2)}, u32[]{:S(2)}) %collective-permute-start.1) | collective-permute-done | bytes 75808 | tf_op jit(solution)/shard_map/ppermute | solution.py:9
  22.3 4.9 %collective-permute-start.2 = (bf16[148,256]{1,0:T(8,128)(2,1)S(1)}, bf16[148,256]{1,0:T(8,128)(2,1)S(1)}, u32[]{:S(2)}, u32[]{:S(2)}) collective-permute-start(bf16[148,256]{1,0:T(8,128)(2,1)S(1)} %collective-permute-done.1), channel_id=1, source_target_pairs={{0,30},{1,31},{2,0},{3,1},{4,2},{5,3},{6,4},{7,5},{8,6},{9,7},{10,... | collective-permute-start | bytes 227336 | tf_op jit(solution)/shard_map/ppermute | solution.py:9
  27.2 1.4 %collective-permute-done.2 = bf16[148,256]{1,0:T(8,128)(2,1)S(1)} collective-permute-done((bf16[148,256]{1,0:T(8,128)(2,1)S(1)}, bf16[148,256]{1,0:T(8,128)(2,1)S(1)}, u32[]{:S(2)}, u32[]{:S(2)}) %collective-permute-start.2) | collective-permute-done | bytes 75808 | tf_op jit(solution)/shard_map/ppermute | solution.py:9
  28.6 4.9 %collective-permute-start.3 = (bf16[148,256]{1,0:T(8,128)(2,1)S(1)}, bf16[148,256]{1,0:T(8,128)(2,1)S(1)}, u32[]{:S(2)}, u32[]{:S(2)}) collective-permute-start(bf16[148,256]{1,0:T(8,128)(2,1)S(1)} %collective-permute-done.2), channel_id=1, source_target_pairs={{0,30},{1,31},{2,0},{3,1},{4,2},{5,3},{6,4},{7,5},{8,6},{9,7},{10,... | collective-permute-start | bytes 227336 | tf_op jit(solution)/shard_map/ppermute | solution.py:9
  33.6 0.1 convolution_reduce_fusion
  33.7 1.3 %collective-permute-done.3 = bf16[148,256]{1,0:T(8,128)(2,1)S(1)} collective-permute-done((bf16[148,256]{1,0:T(8,128)(2,1)S(1)}, bf16[148,256]{1,0:T(8,128)(2,1)S(1)}, u32[]{:S(2)}, u32[]{:S(2)}) %collective-permute-start.3) | collective-permute-done | bytes 75808 | tf_op jit(solution)/shard_map/ppermute | solution.py:9
  35.1 6.9 %collective-permute-start.4 = (bf16[4,148,256]{2,1,0:T(8,128)(2,1)S(1)}, bf16[4,148,256]{2,1,0:T(8,128)(2,1)S(1)}, u32[]{:S(2)}, u32[]{:S(2)}) collective-permute-start(bf16[4,148,256]{2,1,0:T(8,128)(2,1)S(1)} %pad_maximum_fusion.3), channel_id=1, source_target_pairs={{0,1},{1,0},{2,3},{3,2},{4,5},{5,4},{6,7},{7,6},{8,9},{9,8},{10,11... | collective-permute-start | bytes 909320 | tf_op jit(solution)/shard_map/ppermute | solution.py:98
  42.0 0.7 fusion.12
  44.5 0.1 pad_maximum_fusion.4
  44.6 3.1 %collective-permute-start.7 = (f32[145]{0:T(256)S(1)}, f32[145]{0:T(256)S(1)}, u32[]{:S(2)}, u32[]{:S(2)}) collective-permute-start(f32[145]{0:T(256)S(1)} %pad_maximum_fusion.4), channel_id=1, source_target_pairs={{0,32},{32,0},{64,96},{96,64},{128,160},{160,128},{192,224},{224,1... | collective-permute-start | bytes 1748 | tf_op jit(solution)/shard_map/ppermute | solution.py:47
  47.7 1.2 %collective-permute-done.7 = f32[145]{0:T(256)S(1)} collective-permute-done((f32[145]{0:T(256)S(1)}, f32[145]{0:T(256)S(1)}, u32[]{:S(2)}, u32[]{:S(2)}) %collective-permute-start.7) | collective-permute-done | bytes 612 | tf_op jit(solution)/shard_map/ppermute | solution.py:47
  48.9 4.4 %collective-permute-start.8 = (f32[145]{0:T(256)S(1)}, f32[145]{0:T(256)S(1)}, u32[]{:S(2)}, u32[]{:S(2)}) collective-permute-start(f32[145]{0:T(256)S(1)} %add.87), channel_id=1, source_target_pairs={{0,96},{32,64},{64,32},{96,0},{128,224},{160,192},{192,160},{224,1... | collective-permute-start | bytes 1748 | tf_op jit(solution)/shard_map/ppermute | solution.py:47
  53.3 1.1 %collective-permute-done.8 = f32[145]{0:T(256)S(1)} collective-permute-done((f32[145]{0:T(256)S(1)}, f32[145]{0:T(256)S(1)}, u32[]{:S(2)}, u32[]{:S(2)}) %collective-permute-start.8) | collective-permute-done | bytes 612 | tf_op jit(solution)/shard_map/ppermute | solution.py:47
  54.4 3.2 %collective-permute-start.9 = (f32[145]{0:T(256)S(1)}, f32[145]{0:T(256)S(1)}, u32[]{:S(2)}, u32[]{:S(2)}) collective-permute-start(f32[145]{0:T(256)S(1)} %add.88), channel_id=1, source_target_pairs={{0,128},{32,160},{64,192},{96,224},{128,0},{160,32},{192,64},{224,... | collective-permute-start | bytes 1748 | tf_op jit(solution)/shard_map/ppermute | solution.py:47
  57.6 1.1 collective-permute-done.9
  58.7 4.6 %collective-permute-start.10 = (f32[145]{0:T(256)S(1)}, f32[145]{0:T(256)S(1)}, u32[]{:S(2)}, u32[]{:S(2)}) collective-permute-start(f32[145]{0:T(256)S(1)} %add.89), channel_id=1, source_target_pairs={{0,384},{32,416},{64,448},{96,480},{128,256},{160,288},{192,320},{... | collective-permute-start | bytes 1748 | tf_op jit(solution)/shard_map/ppermute | solution.py:47
  63.4 0.9 collective-permute-done.10
  64.3 6.4 %collective-permute-start.11 = (f32[145]{0:T(256)S(1)}, f32[145]{0:T(256)S(1)}, u32[]{:S(2)}, u32[]{:S(2)}) collective-permute-start(f32[145]{0:T(256)S(1)} %add.90), channel_id=1, source_target_pairs={{0,1},{1,0},{2,3},{3,2},{4,5},{5,4},{6,7},{7,6},{8,9},{9,8},{10,11... | collective-permute-start | bytes 1748 | tf_op jit(solution)/shard_map/ppermute | solution.py:47
  70.8 0.8 collective-permute-done.11
  71.6 1.9 %collective-permute-start.12 = (f32[145]{0:T(256)S(1)}, f32[145]{0:T(256)S(1)}, u32[]{:S(2)}, u32[]{:S(2)}) collective-permute-start(f32[145]{0:T(256)S(1)} %add.91), channel_id=1, source_target_pairs={{0,2},{1,3},{2,0},{3,1},{4,6},{5,7},{6,4},{7,5},{8,10},{9,11},{10,... | collective-permute-start | bytes 1748 | tf_op jit(solution)/shard_map/ppermute | solution.py:47
  73.5 2.4 %collective-permute-done.12 = f32[145]{0:T(256)S(1)} collective-permute-done((f32[145]{0:T(256)S(1)}, f32[145]{0:T(256)S(1)}, u32[]{:S(2)}, u32[]{:S(2)}) %collective-permute-start.12) | collective-permute-done | bytes 612 | tf_op jit(solution)/shard_map/ppermute | solution.py:47
  75.9 1.9 %collective-permute-start.13 = (f32[145]{0:T(256)S(1)}, f32[145]{0:T(256)S(1)}, u32[]{:S(2)}, u32[]{:S(2)}) collective-permute-start(f32[145]{0:T(256)S(1)} %add.92), channel_id=1, source_target_pairs={{0,4},{1,5},{2,6},{3,7},{4,0},{5,1},{6,2},{7,3},{8,12},{9,13},{10,... | collective-permute-start | bytes 1748 | tf_op jit(solution)/shard_map/ppermute | solution.py:47
  77.8 3.3 %collective-permute-done.13 = f32[145]{0:T(256)S(1)} collective-permute-done((f32[145]{0:T(256)S(1)}, f32[145]{0:T(256)S(1)}, u32[]{:S(2)}, u32[]{:S(2)}) %collective-permute-start.13) | collective-permute-done | bytes 612 | tf_op jit(solution)/shard_map/ppermute | solution.py:47
  81.1 3.7 %collective-permute-start.14 = (f32[145]{0:T(256)S(1)}, f32[145]{0:T(256)S(1)}, u32[]{:S(2)}, u32[]{:S(2)}) collective-permute-start(f32[145]{0:T(256)S(1)} %add.93), channel_id=1, source_target_pairs={{0,8},{1,9},{2,10},{3,11},{4,12},{5,13},{6,14},{7,15},{8,0},{9,1},... | collective-permute-start | bytes 1748 | tf_op jit(solution)/shard_map/ppermute | solution.py:47
  84.8 4.5 %collective-permute-done.14 = f32[145]{0:T(256)S(1)} collective-permute-done((f32[145]{0:T(256)S(1)}, f32[145]{0:T(256)S(1)}, u32[]{:S(2)}, u32[]{:S(2)}) %collective-permute-start.14) | collective-permute-done | bytes 612 | tf_op jit(solution)/shard_map/ppermute | solution.py:47
  89.3 5.2 %collective-permute-start.15 = (f32[145]{0:T(256)S(1)}, f32[145]{0:T(256)S(1)}, u32[]{:S(2)}, u32[]{:S(2)}) collective-permute-start(f32[145]{0:T(256)S(1)} %add.94), channel_id=1, source_target_pairs={{0,24},{1,25},{2,26},{3,27},{4,28},{5,29},{6,30},{7,31},{8,16},{9,... | collective-permute-start | bytes 1748 | tf_op jit(solution)/shard_map/ppermute | solution.py:47
  94.5 3.0 %collective-permute-done.15 = f32[145]{0:T(256)S(1)} collective-permute-done((f32[145]{0:T(256)S(1)}, f32[145]{0:T(256)S(1)}, u32[]{:S(2)}, u32[]{:S(2)}) %collective-permute-start.15) | collective-permute-done | bytes 612 | tf_op jit(solution)/shard_map/ppermute | solution.py:47
  97.5 0.6 slice.122
  98.2 0.0 collective-permute-done.4
  98.2 0.1 pad_maximum_fusion
  98.2 0.2 compare_reduce_fusion
  98.5 0.1 select_bitcast_fusion
  98.6 0.1 copy.11
  98.8 0.1 copy.14
  98.9 0.0 copy-done
  98.9 0.7 fusion.13
  99.7 0.0 copy-start.1
  99.7 0.2 slice_maximum_fusion
  99.9 4.6 %collective-permute-start.5 = (f32[148,2,2,2]{3,0,2,1:T(8,128)S(1)}, f32[148,2,2,2]{3,0,2,1:T(8,128)S(1)}, u32[]{:S(2)}, u32[]{:S(2)}) collective-permute-start(f32[148,2,2,2]{3,0,2,1:T(8,128)S(1)} %get-tuple-element.19), channel_id=1, source_target_pairs={{0,1},{1,2},{2,3},{3,4},{4,5},{5,6},{6,7},{7,8},{8,9},{9,10},{10,1... | collective-permute-start | bytes 14216 | tf_op jit(solution)/shard_map/ppermute | solution.py:58
  104.5 0.4 collective-permute-start.6
  104.9 0.6 slice_divide_fusion
  105.5 2.8 %collective-permute-done.5 = f32[148,2,2,2]{3,0,2,1:T(8,128)S(1)} collective-permute-done((f32[148,2,2,2]{3,0,2,1:T(8,128)S(1)}, f32[148,2,2,2]{3,0,2,1:T(8,128)S(1)}, u32[]{:S(2)}, u32[]{:S(2)}) %collective-permute-start.5) | collective-permute-done | bytes 4768 | tf_op jit(solution)/shard_map/ppermute | solution.py:58
  108.3 2.8 %collective-permute-done.6 = f32[148,2,2,2]{3,0,2,1:T(8,128)S(1)} collective-permute-done((f32[148,2,2,2]{3,0,2,1:T(8,128)S(1)}, f32[148,2,2,2]{3,0,2,1:T(8,128)S(1)}, u32[]{:S(2)}, u32[]{:S(2)}) %collective-permute-start.6) | collective-permute-done | bytes 4768 | tf_op jit(solution)/shard_map/ppermute | solution.py:61
  111.1 0.3 pad_maximum_fusion.1
  111.4 0.4 fusion.1
  111.8 0.0 copy-done.1
  111.8 0.1 slice_add_fusion.2
  111.9 0.7 copy.12
  (20 shorter events, 0.4 us)
Async XLA Ops:
  0.0 98.9 %copy-start = (bf16[1,1,8,256,768]{4,3,2,1,0:T(8,128)(2,1)S(1)}, bf16[1,1,8,256,768]{4,3,2,1,0:T(8,128)(2,1)}, u32[]{:S(2)}) copy-start(bf16[1,1,8,256,768]{4,3,2,1,0:T(8,128)(2,1)} %param.7) | copy-start | bytes 9437188
  2.6 13.4 %collective-permute-start = (bf16[148,256]{1,0:T(8,128)(2,1)S(1)}, bf16[148,256]{1,0:T(8,128)(2,1)S(1)}, u32[]{:S(2)}, u32[]{:S(2)}) collective-permute-start(bf16[148,256]{1,0:T(8,128)(2,1)S(1)} %concatenate.12), channel_id=1, source_target_pairs={{0,30},{1,31},{2,0},{3,1},{4,2},{5,3},{6,4},{7,5},{8,6},{9,7},{10,... | collective-permute-start | bytes 227336 | tf_op jit(solution)/shard_map/ppermute | solution.py:9
  16.0 6.3 %collective-permute-start.1 = (bf16[148,256]{1,0:T(8,128)(2,1)S(1)}, bf16[148,256]{1,0:T(8,128)(2,1)S(1)}, u32[]{:S(2)}, u32[]{:S(2)}) collective-permute-start(bf16[148,256]{1,0:T(8,128)(2,1)S(1)} %collective-permute-done), channel_id=1, source_target_pairs={{0,30},{1,31},{2,0},{3,1},{4,2},{5,3},{6,4},{7,5},{8,6},{9,7},{10,... | collective-permute-start | bytes 227336 | tf_op jit(solution)/shard_map/ppermute | solution.py:9
  22.3 6.3 %collective-permute-start.2 = (bf16[148,256]{1,0:T(8,128)(2,1)S(1)}, bf16[148,256]{1,0:T(8,128)(2,1)S(1)}, u32[]{:S(2)}, u32[]{:S(2)}) collective-permute-start(bf16[148,256]{1,0:T(8,128)(2,1)S(1)} %collective-permute-done.1), channel_id=1, source_target_pairs={{0,30},{1,31},{2,0},{3,1},{4,2},{5,3},{6,4},{7,5},{8,6},{9,7},{10,... | collective-permute-start | bytes 227336 | tf_op jit(solution)/shard_map/ppermute | solution.py:9
  28.6 6.3 %collective-permute-start.3 = (bf16[148,256]{1,0:T(8,128)(2,1)S(1)}, bf16[148,256]{1,0:T(8,128)(2,1)S(1)}, u32[]{:S(2)}, u32[]{:S(2)}) collective-permute-start(bf16[148,256]{1,0:T(8,128)(2,1)S(1)} %collective-permute-done.2), channel_id=1, source_target_pairs={{0,30},{1,31},{2,0},{3,1},{4,2},{5,3},{6,4},{7,5},{8,6},{9,7},{10,... | collective-permute-start | bytes 227336 | tf_op jit(solution)/shard_map/ppermute | solution.py:9
  35.1 63.1 %collective-permute-start.4 = (bf16[4,148,256]{2,1,0:T(8,128)(2,1)S(1)}, bf16[4,148,256]{2,1,0:T(8,128)(2,1)S(1)}, u32[]{:S(2)}, u32[]{:S(2)}) collective-permute-start(bf16[4,148,256]{2,1,0:T(8,128)(2,1)S(1)} %pad_maximum_fusion.3), channel_id=1, source_target_pairs={{0,1},{1,0},{2,3},{3,2},{4,5},{5,4},{6,7},{7,6},{8,9},{9,8},{10,11... | collective-permute-start | bytes 909320 | tf_op jit(solution)/shard_map/ppermute | solution.py:98
  44.6 4.3 %collective-permute-start.7 = (f32[145]{0:T(256)S(1)}, f32[145]{0:T(256)S(1)}, u32[]{:S(2)}, u32[]{:S(2)}) collective-permute-start(f32[145]{0:T(256)S(1)} %pad_maximum_fusion.4), channel_id=1, source_target_pairs={{0,32},{32,0},{64,96},{96,64},{128,160},{160,128},{192,224},{224,1... | collective-permute-start | bytes 1748 | tf_op jit(solution)/shard_map/ppermute | solution.py:47
  48.9 5.5 %collective-permute-start.8 = (f32[145]{0:T(256)S(1)}, f32[145]{0:T(256)S(1)}, u32[]{:S(2)}, u32[]{:S(2)}) collective-permute-start(f32[145]{0:T(256)S(1)} %add.87), channel_id=1, source_target_pairs={{0,96},{32,64},{64,32},{96,0},{128,224},{160,192},{192,160},{224,1... | collective-permute-start | bytes 1748 | tf_op jit(solution)/shard_map/ppermute | solution.py:47
  54.4 4.3 %collective-permute-start.9 = (f32[145]{0:T(256)S(1)}, f32[145]{0:T(256)S(1)}, u32[]{:S(2)}, u32[]{:S(2)}) collective-permute-start(f32[145]{0:T(256)S(1)} %add.88), channel_id=1, source_target_pairs={{0,128},{32,160},{64,192},{96,224},{128,0},{160,32},{192,64},{224,... | collective-permute-start | bytes 1748 | tf_op jit(solution)/shard_map/ppermute | solution.py:47
  58.7 5.6 %collective-permute-start.10 = (f32[145]{0:T(256)S(1)}, f32[145]{0:T(256)S(1)}, u32[]{:S(2)}, u32[]{:S(2)}) collective-permute-start(f32[145]{0:T(256)S(1)} %add.89), channel_id=1, source_target_pairs={{0,384},{32,416},{64,448},{96,480},{128,256},{160,288},{192,320},{... | collective-permute-start | bytes 1748 | tf_op jit(solution)/shard_map/ppermute | solution.py:47
  64.3 7.2 %collective-permute-start.11 = (f32[145]{0:T(256)S(1)}, f32[145]{0:T(256)S(1)}, u32[]{:S(2)}, u32[]{:S(2)}) collective-permute-start(f32[145]{0:T(256)S(1)} %add.90), channel_id=1, source_target_pairs={{0,1},{1,0},{2,3},{3,2},{4,5},{5,4},{6,7},{7,6},{8,9},{9,8},{10,11... | collective-permute-start | bytes 1748 | tf_op jit(solution)/shard_map/ppermute | solution.py:47
  71.6 4.3 %collective-permute-start.12 = (f32[145]{0:T(256)S(1)}, f32[145]{0:T(256)S(1)}, u32[]{:S(2)}, u32[]{:S(2)}) collective-permute-start(f32[145]{0:T(256)S(1)} %add.91), channel_id=1, source_target_pairs={{0,2},{1,3},{2,0},{3,1},{4,6},{5,7},{6,4},{7,5},{8,10},{9,11},{10,... | collective-permute-start | bytes 1748 | tf_op jit(solution)/shard_map/ppermute | solution.py:47
  75.9 5.2 %collective-permute-start.13 = (f32[145]{0:T(256)S(1)}, f32[145]{0:T(256)S(1)}, u32[]{:S(2)}, u32[]{:S(2)}) collective-permute-start(f32[145]{0:T(256)S(1)} %add.92), channel_id=1, source_target_pairs={{0,4},{1,5},{2,6},{3,7},{4,0},{5,1},{6,2},{7,3},{8,12},{9,13},{10,... | collective-permute-start | bytes 1748 | tf_op jit(solution)/shard_map/ppermute | solution.py:47
  81.1 8.2 %collective-permute-start.14 = (f32[145]{0:T(256)S(1)}, f32[145]{0:T(256)S(1)}, u32[]{:S(2)}, u32[]{:S(2)}) collective-permute-start(f32[145]{0:T(256)S(1)} %add.93), channel_id=1, source_target_pairs={{0,8},{1,9},{2,10},{3,11},{4,12},{5,13},{6,14},{7,15},{8,0},{9,1},... | collective-permute-start | bytes 1748 | tf_op jit(solution)/shard_map/ppermute | solution.py:47
  89.3 8.2 %collective-permute-start.15 = (f32[145]{0:T(256)S(1)}, f32[145]{0:T(256)S(1)}, u32[]{:S(2)}, u32[]{:S(2)}) collective-permute-start(f32[145]{0:T(256)S(1)} %add.94), channel_id=1, source_target_pairs={{0,24},{1,25},{2,26},{3,27},{4,28},{5,29},{6,30},{7,31},{8,16},{9,... | collective-permute-start | bytes 1748 | tf_op jit(solution)/shard_map/ppermute | solution.py:47
  99.7 12.1 %copy-start.1 = (f32[2,128]{1,0:T(2,128)S(1)}, f32[2,128]{1,0:T(2,128)}, u32[]{:S(2)}) copy-start(f32[2,128]{1,0:T(2,128)} %param.5) | copy-start | bytes 3076
  99.9 8.4 %collective-permute-start.5 = (f32[148,2,2,2]{3,0,2,1:T(8,128)S(1)}, f32[148,2,2,2]{3,0,2,1:T(8,128)S(1)}, u32[]{:S(2)}, u32[]{:S(2)}) collective-permute-start(f32[148,2,2,2]{3,0,2,1:T(8,128)S(1)} %get-tuple-element.19), channel_id=1, source_target_pairs={{0,1},{1,2},{2,3},{3,4},{4,5},{5,6},{6,7},{7,8},{8,9},{9,10},{10,1... | collective-permute-start | bytes 14216 | tf_op jit(solution)/shard_map/ppermute | solution.py:58
  104.5 6.6 %collective-permute-start.6 = (f32[148,2,2,2]{3,0,2,1:T(8,128)S(1)}, f32[148,2,2,2]{3,0,2,1:T(8,128)S(1)}, u32[]{:S(2)}, u32[]{:S(2)}) collective-permute-start(f32[148,2,2,2]{3,0,2,1:T(8,128)S(1)} %get-tuple-element.20), channel_id=1, source_target_pairs={{1,0},{2,1},{3,2},{4,3},{5,4},{6,5},{7,6},{8,7},{9,8},{10,9},{11,1... | collective-permute-start | bytes 14216 | tf_op jit(solution)/shard_map/ppermute | solution.py:61

commit v9 on v8

--- a/solution.py
+++ b/solution.py
@@ -82,9 +82,13 @@
     products = jnp.dot(
         payload[: fields + 3], jnp.concatenate(area_parts, axis=0).T, preferred_element_type=jnp.float32
     ).sum(axis=1)
-    weighted = products[:fields]
-    squares = products[fields] + products[fields + 1] + products[fields + 2]
-    stats, area_late = lax.optimization_barrier((jnp.concatenate([weighted, squares[None]]), cell_area))
+    count = fields + 1
+    stats = (
+        products[:count]
+        + jnp.pad(products[count : count + 1], (fields, 0))
+        + jnp.pad(products[count + 1 : count + 2], (fields, 0))
+    )
+    stats, area_late = lax.optimization_barrier((stats, cell_area))
     stats = butterfly_sum(stats, ("lat", "lon"))
     factor = stats[:fields] / stats[fields]
 
@@ -147,4 +151,6 @@
         P("lat", "lon", None, None, None),
     )
     out_specs = P(None, "lat", "lon")
-    return jax.shard_map(on_device_body, mesh=mesh, in_specs=in_specs, out_specs=out_specs, check_vma=False)
+    return jax.shard_map(
+        on_device_body, mesh=mesh, in_specs=in_specs, out_specs=out_specs, check_vma=False
+    )

time: 113 us -> 112 us (level)
  between operations: 3.02 us -> 1.11 us
  other arithmetic: 3.11 us -> 4.45 us
    add x0 -> x1, other arithmetic: none -> 1.41 us  [on_device_body(): products[:count] + jnp.pad(products[count:count + 1], (fields, 0))]
  transfers between devices with their start and end apart: 16 -> 16, of which waited for: 15 -> 15; matrix products, arithmetic and copies ran while one was open for 2% -> 3% of each run, Pallas kernels for 0% -> 0%
where the time goes in v9:
time: 112 us; the launch traced here: 111 us
  starting transfers between devices  73 us (65%)
  waiting for transfers between devices  28.8 us (26%)
  other arithmetic  4.45 us (4%)
  local copies, waits for them, and re-layouts  3.27 us (3%)
    ppermute x9, starting transfers between devices, butterfly_sum(): lax.ppermute(value, axis, [(i, partner_of[i]) for i in range(length)])  34.5 us
    ppermute x4, starting transfers between devices, shifted(): lax.ppermute(value, axis, [(i, (i + by) % length) for i in range(length)])  26.7 us
    ppermute x9, waiting for transfers between devices, butterfly_sum(): lax.ppermute(value, axis, [(i, partner_of[i]) for i in range(length)])  18.4 us
    ppermute x1, starting transfers between devices, on_device_body(): lax.ppermute(offer, 'lon', [(i, i ^ 1) for i in range(lax.axis_size('lon'...  6.89 us
    ppermute x4, waiting for transfers between devices, shifted(): lax.ppermute(value, axis, [(i, (i + by) % length) for i in range(length)])  4.87 us
    ppermute x1, starting transfers between devices, padded_2(): lax.ppermute(lax.slice_in_dim(block, block.shape[dim] - width, None, axis...  4.58 us
    ppermute x1, waiting for transfers between devices, padded_2(): lax.ppermute(lax.slice_in_dim(block, block.shape[dim] - width, None, axis...  2.79 us
    ppermute x1, waiting for transfers between devices, padded_2(): lax.ppermute(lax.slice_in_dim(block, 0, width, axis=dim), axis, backward)  2.77 us
  transfers between devices with their start and end apart: 16, of which 15 were waited for; matrix products, arithmetic and copies ran while one was open for 3% of the time, Pallas kernels for 0%

profile of v9, /device:TPU:1, one launch (start us, length us, event | category | flops | bytes accessed | tf_op | source)
XLA Modules:
  0.0 111.4 jit_solution(17300015695710159950)
XLA Ops:
  0.0 0.0 copy-start
  0.8 0.8 fusion.10
  1.6 0.9 copy.16
  2.6 11.9 %collective-permute-start = (bf16[148,256]{1,0:T(8,128)(2,1)S(1)}, bf16[148,256]{1,0:T(8,128)(2,1)S(1)}, u32[]{:S(2)}, u32[]{:S(2)}) collective-permute-start(bf16[148,256]{1,0:T(8,128)(2,1)S(1)} %concatenate.9), channel_id=1, source_target_pairs={{0,30},{1,31},{2,0},{3,1},{4,2},{5,3},{6,4},{7,5},{8,6},{9,7},{10,... | collective-permute-start | bytes 227336 | tf_op jit(solution)/shard_map/ppermute | solution.py:9
  14.5 1.4 %collective-permute-done = bf16[148,256]{1,0:T(8,128)(2,1)S(1)} collective-permute-done((bf16[148,256]{1,0:T(8,128)(2,1)S(1)}, bf16[148,256]{1,0:T(8,128)(2,1)S(1)}, u32[]{:S(2)}, u32[]{:S(2)}) %collective-permute-start) | collective-permute-done | bytes 75808 | tf_op jit(solution)/shard_map/ppermute | solution.py:9
  16.0 4.9 %collective-permute-start.1 = (bf16[148,256]{1,0:T(8,128)(2,1)S(1)}, bf16[148,256]{1,0:T(8,128)(2,1)S(1)}, u32[]{:S(2)}, u32[]{:S(2)}) collective-permute-start(bf16[148,256]{1,0:T(8,128)(2,1)S(1)} %collective-permute-done), channel_id=1, source_target_pairs={{0,30},{1,31},{2,0},{3,1},{4,2},{5,3},{6,4},{7,5},{8,6},{9,7},{10,... | collective-permute-start | bytes 227336 | tf_op jit(solution)/shard_map/ppermute | solution.py:9
  20.9 1.4 %collective-permute-done.1 = bf16[148,256]{1,0:T(8,128)(2,1)S(1)} collective-permute-done((bf16[148,256]{1,0:T(8,128)(2,1)S(1)}, bf16[148,256]{1,0:T(8,128)(2,1)S(1)}, u32[]{:S(2)}, u32[]{:S(2)}) %collective-permute-start.1) | collective-permute-done | bytes 75808 | tf_op jit(solution)/shard_map/ppermute | solution.py:9
  22.3 4.9 %collective-permute-start.2 = (bf16[148,256]{1,0:T(8,128)(2,1)S(1)}, bf16[148,256]{1,0:T(8,128)(2,1)S(1)}, u32[]{:S(2)}, u32[]{:S(2)}) collective-permute-start(bf16[148,256]{1,0:T(8,128)(2,1)S(1)} %collective-permute-done.1), channel_id=1, source_target_pairs={{0,30},{1,31},{2,0},{3,1},{4,2},{5,3},{6,4},{7,5},{8,6},{9,7},{10,... | collective-permute-start | bytes 227336 | tf_op jit(solution)/shard_map/ppermute | solution.py:9
  27.2 0.1 convolution_reduce_fusion
  27.4 1.3 %collective-permute-done.2 = bf16[148,256]{1,0:T(8,128)(2,1)S(1)} collective-permute-done((bf16[148,256]{1,0:T(8,128)(2,1)S(1)}, bf16[148,256]{1,0:T(8,128)(2,1)S(1)}, u32[]{:S(2)}, u32[]{:S(2)}) %collective-permute-start.2) | collective-permute-done | bytes 75808 | tf_op jit(solution)/shard_map/ppermute | solution.py:9
  28.6 4.9 %collective-permute-start.3 = (bf16[148,256]{1,0:T(8,128)(2,1)S(1)}, bf16[148,256]{1,0:T(8,128)(2,1)S(1)}, u32[]{:S(2)}, u32[]{:S(2)}) collective-permute-start(bf16[148,256]{1,0:T(8,128)(2,1)S(1)} %collective-permute-done.2), channel_id=1, source_target_pairs={{0,30},{1,31},{2,0},{3,1},{4,2},{5,3},{6,4},{7,5},{8,6},{9,7},{10,... | collective-permute-start | bytes 227336 | tf_op jit(solution)/shard_map/ppermute | solution.py:9
  33.6 0.7 fusion.12
  34.2 0.8 collective-permute-done.3
  35.1 6.9 %collective-permute-start.4 = (bf16[4,148,256]{2,1,0:T(8,128)(2,1)S(1)}, bf16[4,148,256]{2,1,0:T(8,128)(2,1)S(1)}, u32[]{:S(2)}, u32[]{:S(2)}) collective-permute-start(bf16[4,148,256]{2,1,0:T(8,128)(2,1)S(1)} %pad_maximum_fusion.3), channel_id=1, source_target_pairs={{0,1},{1,0},{2,3},{3,2},{4,5},{5,4},{6,7},{7,6},{8,9},{9,8},{10,11... | collective-permute-start | bytes 909320 | tf_op jit(solution)/shard_map/ppermute | solution.py:102
  42.0 1.4 %pad_add_fusion = f32[145]{0:T(256)S(1)} fusion(f32[1]{0:T(128)} %get-tuple-element.26, f32[1]{0:T(128)} %get-tuple-element.25, f32[147]{0:T(256)S(1)} %convolution_reduce_fusion), kind=kLoop, calls=%fused_computation.54 | loop fusion | flops 290 | bytes 1168 | tf_op jit(solution)/shard_map/add | solution.py:87
  43.4 3.1 %collective-permute-start.7 = (f32[145]{0:T(256)S(1)}, f32[145]{0:T(256)S(1)}, u32[]{:S(2)}, u32[]{:S(2)}) collective-permute-start(f32[145]{0:T(256)S(1)} %pad_add_fusion), channel_id=1, source_target_pairs={{0,32},{32,0},{64,96},{96,64},{128,160},{160,128},{192,224},{224,1... | collective-permute-start | bytes 1748 | tf_op jit(solution)/shard_map/ppermute | solution.py:47
  46.5 1.2 %collective-permute-done.7 = f32[145]{0:T(256)S(1)} collective-permute-done((f32[145]{0:T(256)S(1)}, f32[145]{0:T(256)S(1)}, u32[]{:S(2)}, u32[]{:S(2)}) %collective-permute-start.7) | collective-permute-done | bytes 612 | tf_op jit(solution)/shard_map/ppermute | solution.py:47
  47.7 4.4 %collective-permute-start.8 = (f32[145]{0:T(256)S(1)}, f32[145]{0:T(256)S(1)}, u32[]{:S(2)}, u32[]{:S(2)}) collective-permute-start(f32[145]{0:T(256)S(1)} %add.89), channel_id=1, source_target_pairs={{0,96},{32,64},{64,32},{96,0},{128,224},{160,192},{192,160},{224,1... | collective-permute-start | bytes 1748 | tf_op jit(solution)/shard_map/ppermute | solution.py:47
  52.1 1.1 %collective-permute-done.8 = f32[145]{0:T(256)S(1)} collective-permute-done((f32[145]{0:T(256)S(1)}, f32[145]{0:T(256)S(1)}, u32[]{:S(2)}, u32[]{:S(2)}) %collective-permute-start.8) | collective-permute-done | bytes 612 | tf_op jit(solution)/shard_map/ppermute | solution.py:47
  53.2 3.2 %collective-permute-start.9 = (f32[145]{0:T(256)S(1)}, f32[145]{0:T(256)S(1)}, u32[]{:S(2)}, u32[]{:S(2)}) collective-permute-start(f32[145]{0:T(256)S(1)} %add.90), channel_id=1, source_target_pairs={{0,128},{32,160},{64,192},{96,224},{128,0},{160,32},{192,64},{224,... | collective-permute-start | bytes 1748 | tf_op jit(solution)/shard_map/ppermute | solution.py:47
  56.4 1.1 collective-permute-done.9
  57.5 4.6 %collective-permute-start.10 = (f32[145]{0:T(256)S(1)}, f32[145]{0:T(256)S(1)}, u32[]{:S(2)}, u32[]{:S(2)}) collective-permute-start(f32[145]{0:T(256)S(1)} %add.91), channel_id=1, source_target_pairs={{0,384},{32,416},{64,448},{96,480},{128,256},{160,288},{192,320},{... | collective-permute-start | bytes 1748 | tf_op jit(solution)/shard_map/ppermute | solution.py:47
  62.2 0.9 collective-permute-done.10
  63.1 6.4 %collective-permute-start.11 = (f32[145]{0:T(256)S(1)}, f32[145]{0:T(256)S(1)}, u32[]{:S(2)}, u32[]{:S(2)}) collective-permute-start(f32[145]{0:T(256)S(1)} %add.92), channel_id=1, source_target_pairs={{0,1},{1,0},{2,3},{3,2},{4,5},{5,4},{6,7},{7,6},{8,9},{9,8},{10,11... | collective-permute-start | bytes 1748 | tf_op jit(solution)/shard_map/ppermute | solution.py:47
  69.6 0.8 collective-permute-done.11
  70.4 1.9 %collective-permute-start.12 = (f32[145]{0:T(256)S(1)}, f32[145]{0:T(256)S(1)}, u32[]{:S(2)}, u32[]{:S(2)}) collective-permute-start(f32[145]{0:T(256)S(1)} %add.93), channel_id=1, source_target_pairs={{0,2},{1,3},{2,0},{3,1},{4,6},{5,7},{6,4},{7,5},{8,10},{9,11},{10,... | collective-permute-start | bytes 1748 | tf_op jit(solution)/shard_map/ppermute | solution.py:47
  72.3 2.4 %collective-permute-done.12 = f32[145]{0:T(256)S(1)} collective-permute-done((f32[145]{0:T(256)S(1)}, f32[145]{0:T(256)S(1)}, u32[]{:S(2)}, u32[]{:S(2)}) %collective-permute-start.12) | collective-permute-done | bytes 612 | tf_op jit(solution)/shard_map/ppermute | solution.py:47
  74.7 1.9 %collective-permute-start.13 = (f32[145]{0:T(256)S(1)}, f32[145]{0:T(256)S(1)}, u32[]{:S(2)}, u32[]{:S(2)}) collective-permute-start(f32[145]{0:T(256)S(1)} %add.94), channel_id=1, source_target_pairs={{0,4},{1,5},{2,6},{3,7},{4,0},{5,1},{6,2},{7,3},{8,12},{9,13},{10,... | collective-permute-start | bytes 1748 | tf_op jit(solution)/shard_map/ppermute | solution.py:47
  76.6 3.3 %collective-permute-done.13 = f32[145]{0:T(256)S(1)} collective-permute-done((f32[145]{0:T(256)S(1)}, f32[145]{0:T(256)S(1)}, u32[]{:S(2)}, u32[]{:S(2)}) %collective-permute-start.13) | collective-permute-done | bytes 612 | tf_op jit(solution)/shard_map/ppermute | solution.py:47
  79.9 3.7 %collective-permute-start.14 = (f32[145]{0:T(256)S(1)}, f32[145]{0:T(256)S(1)}, u32[]{:S(2)}, u32[]{:S(2)}) collective-permute-start(f32[145]{0:T(256)S(1)} %add.95), channel_id=1, source_target_pairs={{0,8},{1,9},{2,10},{3,11},{4,12},{5,13},{6,14},{7,15},{8,0},{9,1},... | collective-permute-start | bytes 1748 | tf_op jit(solution)/shard_map/ppermute | solution.py:47
  83.6 4.5 %collective-permute-done.14 = f32[145]{0:T(256)S(1)} collective-permute-done((f32[145]{0:T(256)S(1)}, f32[145]{0:T(256)S(1)}, u32[]{:S(2)}, u32[]{:S(2)}) %collective-permute-start.14) | collective-permute-done | bytes 612 | tf_op jit(solution)/shard_map/ppermute | solution.py:47
  88.1 5.2 %collective-permute-start.15 = (f32[145]{0:T(256)S(1)}, f32[145]{0:T(256)S(1)}, u32[]{:S(2)}, u32[]{:S(2)}) collective-permute-start(f32[145]{0:T(256)S(1)} %add.96), channel_id=1, source_target_pairs={{0,24},{1,25},{2,26},{3,27},{4,28},{5,29},{6,30},{7,31},{8,16},{9,... | collective-permute-start | bytes 1748 | tf_op jit(solution)/shard_map/ppermute | solution.py:47
  93.3 3.0 %collective-permute-done.15 = f32[145]{0:T(256)S(1)} collective-permute-done((f32[145]{0:T(256)S(1)}, f32[145]{0:T(256)S(1)}, u32[]{:S(2)}, u32[]{:S(2)}) %collective-permute-start.15) | collective-permute-done | bytes 612 | tf_op jit(solution)/shard_map/ppermute | solution.py:47
  96.3 0.6 slice.118
  96.9 0.0 collective-permute-done.4
  97.0 0.1 pad_maximum_fusion
  97.0 0.2 compare_reduce_fusion
  97.3 0.1 select_bitcast_fusion
  97.4 0.1 copy.11
  97.6 0.1 copy.14
  97.7 0.0 copy-done
  97.7 0.7 fusion.13
  98.4 0.0 copy-start.1
  98.5 0.2 slice_maximum_fusion
  98.6 4.6 %collective-permute-start.5 = (f32[148,2,2,2]{3,0,2,1:T(8,128)S(1)}, f32[148,2,2,2]{3,0,2,1:T(8,128)S(1)}, u32[]{:S(2)}, u32[]{:S(2)}) collective-permute-start(f32[148,2,2,2]{3,0,2,1:T(8,128)S(1)} %get-tuple-element.19), channel_id=1, source_target_pairs={{0,1},{1,2},{2,3},{3,4},{4,5},{5,6},{6,7},{7,8},{8,9},{9,10},{10,1... | collective-permute-start | bytes 14216 | tf_op jit(solution)/shard_map/ppermute | solution.py:58
  103.2 0.4 collective-permute-start.6
  103.6 0.6 slice_divide_fusion
  104.3 2.8 %collective-permute-done.5 = f32[148,2,2,2]{3,0,2,1:T(8,128)S(1)} collective-permute-done((f32[148,2,2,2]{3,0,2,1:T(8,128)S(1)}, f32[148,2,2,2]{3,0,2,1:T(8,128)S(1)}, u32[]{:S(2)}, u32[]{:S(2)}) %collective-permute-start.5) | collective-permute-done | bytes 4768 | tf_op jit(solution)/shard_map/ppermute | solution.py:58
  107.1 2.8 %collective-permute-done.6 = f32[148,2,2,2]{3,0,2,1:T(8,128)S(1)} collective-permute-done((f32[148,2,2,2]{3,0,2,1:T(8,128)S(1)}, f32[148,2,2,2]{3,0,2,1:T(8,128)S(1)}, u32[]{:S(2)}, u32[]{:S(2)}) %collective-permute-start.6) | collective-permute-done | bytes 4768 | tf_op jit(solution)/shard_map/ppermute | solution.py:61
  109.9 0.3 pad_maximum_fusion.1
  110.2 0.4 fusion.1
  110.6 0.0 copy-done.1
  110.6 0.1 slice_add_fusion.2
  110.7 0.7 copy.12
  (20 shorter events, 0.4 us)
Async XLA Ops:
  0.0 97.7 %copy-start = (bf16[1,1,8,256,768]{4,3,2,1,0:T(8,128)(2,1)S(1)}, bf16[1,1,8,256,768]{4,3,2,1,0:T(8,128)(2,1)}, u32[]{:S(2)}) copy-start(bf16[1,1,8,256,768]{4,3,2,1,0:T(8,128)(2,1)} %param.7) | copy-start | bytes 9437188
  2.6 13.4 %collective-permute-start = (bf16[148,256]{1,0:T(8,128)(2,1)S(1)}, bf16[148,256]{1,0:T(8,128)(2,1)S(1)}, u32[]{:S(2)}, u32[]{:S(2)}) collective-permute-start(bf16[148,256]{1,0:T(8,128)(2,1)S(1)} %concatenate.9), channel_id=1, source_target_pairs={{0,30},{1,31},{2,0},{3,1},{4,2},{5,3},{6,4},{7,5},{8,6},{9,7},{10,... | collective-permute-start | bytes 227336 | tf_op jit(solution)/shard_map/ppermute | solution.py:9
  16.0 6.3 %collective-permute-start.1 = (bf16[148,256]{1,0:T(8,128)(2,1)S(1)}, bf16[148,256]{1,0:T(8,128)(2,1)S(1)}, u32[]{:S(2)}, u32[]{:S(2)}) collective-permute-start(bf16[148,256]{1,0:T(8,128)(2,1)S(1)} %collective-permute-done), channel_id=1, source_target_pairs={{0,30},{1,31},{2,0},{3,1},{4,2},{5,3},{6,4},{7,5},{8,6},{9,7},{10,... | collective-permute-start | bytes 227336 | tf_op jit(solution)/shard_map/ppermute | solution.py:9
  22.3 6.3 %collective-permute-start.2 = (bf16[148,256]{1,0:T(8,128)(2,1)S(1)}, bf16[148,256]{1,0:T(8,128)(2,1)S(1)}, u32[]{:S(2)}, u32[]{:S(2)}) collective-permute-start(bf16[148,256]{1,0:T(8,128)(2,1)S(1)} %collective-permute-done.1), channel_id=1, source_target_pairs={{0,30},{1,31},{2,0},{3,1},{4,2},{5,3},{6,4},{7,5},{8,6},{9,7},{10,... | collective-permute-start | bytes 227336 | tf_op jit(solution)/shard_map/ppermute | solution.py:9
  28.6 6.3 %collective-permute-start.3 = (bf16[148,256]{1,0:T(8,128)(2,1)S(1)}, bf16[148,256]{1,0:T(8,128)(2,1)S(1)}, u32[]{:S(2)}, u32[]{:S(2)}) collective-permute-start(bf16[148,256]{1,0:T(8,128)(2,1)S(1)} %collective-permute-done.2), channel_id=1, source_target_pairs={{0,30},{1,31},{2,0},{3,1},{4,2},{5,3},{6,4},{7,5},{8,6},{9,7},{10,... | collective-permute-start | bytes 227336 | tf_op jit(solution)/shard_map/ppermute | solution.py:9
  35.1 61.9 %collective-permute-start.4 = (bf16[4,148,256]{2,1,0:T(8,128)(2,1)S(1)}, bf16[4,148,256]{2,1,0:T(8,128)(2,1)S(1)}, u32[]{:S(2)}, u32[]{:S(2)}) collective-permute-start(bf16[4,148,256]{2,1,0:T(8,128)(2,1)S(1)} %pad_maximum_fusion.3), channel_id=1, source_target_pairs={{0,1},{1,0},{2,3},{3,2},{4,5},{5,4},{6,7},{7,6},{8,9},{9,8},{10,11... | collective-permute-start | bytes 909320 | tf_op jit(solution)/shard_map/ppermute | solution.py:102
  43.4 4.3 %collective-permute-start.7 = (f32[145]{0:T(256)S(1)}, f32[145]{0:T(256)S(1)}, u32[]{:S(2)}, u32[]{:S(2)}) collective-permute-start(f32[145]{0:T(256)S(1)} %pad_add_fusion), channel_id=1, source_target_pairs={{0,32},{32,0},{64,96},{96,64},{128,160},{160,128},{192,224},{224,1... | collective-permute-start | bytes 1748 | tf_op jit(solution)/shard_map/ppermute | solution.py:47
  47.7 5.5 %collective-permute-start.8 = (f32[145]{0:T(256)S(1)}, f32[145]{0:T(256)S(1)}, u32[]{:S(2)}, u32[]{:S(2)}) collective-permute-start(f32[145]{0:T(256)S(1)} %add.89), channel_id=1, source_target_pairs={{0,96},{32,64},{64,32},{96,0},{128,224},{160,192},{192,160},{224,1... | collective-permute-start | bytes 1748 | tf_op jit(solution)/shard_map/ppermute | solution.py:47
  53.2 4.3 %collective-permute-start.9 = (f32[145]{0:T(256)S(1)}, f32[145]{0:T(256)S(1)}, u32[]{:S(2)}, u32[]{:S(2)}) collective-permute-start(f32[145]{0:T(256)S(1)} %add.90), channel_id=1, source_target_pairs={{0,128},{32,160},{64,192},{96,224},{128,0},{160,32},{192,64},{224,... | collective-permute-start | bytes 1748 | tf_op jit(solution)/shard_map/ppermute | solution.py:47
  57.5 5.6 %collective-permute-start.10 = (f32[145]{0:T(256)S(1)}, f32[145]{0:T(256)S(1)}, u32[]{:S(2)}, u32[]{:S(2)}) collective-permute-start(f32[145]{0:T(256)S(1)} %add.91), channel_id=1, source_target_pairs={{0,384},{32,416},{64,448},{96,480},{128,256},{160,288},{192,320},{... | collective-permute-start | bytes 1748 | tf_op jit(solution)/shard_map/ppermute | solution.py:47
  63.1 7.2 %collective-permute-start.11 = (f32[145]{0:T(256)S(1)}, f32[145]{0:T(256)S(1)}, u32[]{:S(2)}, u32[]{:S(2)}) collective-permute-start(f32[145]{0:T(256)S(1)} %add.92), channel_id=1, source_target_pairs={{0,1},{1,0},{2,3},{3,2},{4,5},{5,4},{6,7},{7,6},{8,9},{9,8},{10,11... | collective-permute-start | bytes 1748 | tf_op jit(solution)/shard_map/ppermute | solution.py:47
  70.4 4.3 %collective-permute-start.12 = (f32[145]{0:T(256)S(1)}, f32[145]{0:T(256)S(1)}, u32[]{:S(2)}, u32[]{:S(2)}) collective-permute-start(f32[145]{0:T(256)S(1)} %add.93), channel_id=1, source_target_pairs={{0,2},{1,3},{2,0},{3,1},{4,6},{5,7},{6,4},{7,5},{8,10},{9,11},{10,... | collective-permute-start | bytes 1748 | tf_op jit(solution)/shard_map/ppermute | solution.py:47
  74.7 5.2 %collective-permute-start.13 = (f32[145]{0:T(256)S(1)}, f32[145]{0:T(256)S(1)}, u32[]{:S(2)}, u32[]{:S(2)}) collective-permute-start(f32[145]{0:T(256)S(1)} %add.94), channel_id=1, source_target_pairs={{0,4},{1,5},{2,6},{3,7},{4,0},{5,1},{6,2},{7,3},{8,12},{9,13},{10,... | collective-permute-start | bytes 1748 | tf_op jit(solution)/shard_map/ppermute | solution.py:47
  79.9 8.2 %collective-permute-start.14 = (f32[145]{0:T(256)S(1)}, f32[145]{0:T(256)S(1)}, u32[]{:S(2)}, u32[]{:S(2)}) collective-permute-start(f32[145]{0:T(256)S(1)} %add.95), channel_id=1, source_target_pairs={{0,8},{1,9},{2,10},{3,11},{4,12},{5,13},{6,14},{7,15},{8,0},{9,1},... | collective-permute-start | bytes 1748 | tf_op jit(solution)/shard_map/ppermute | solution.py:47
  88.1 8.2 %collective-permute-start.15 = (f32[145]{0:T(256)S(1)}, f32[145]{0:T(256)S(1)}, u32[]{:S(2)}, u32[]{:S(2)}) collective-permute-start(f32[145]{0:T(256)S(1)} %add.96), channel_id=1, source_target_pairs={{0,24},{1,25},{2,26},{3,27},{4,28},{5,29},{6,30},{7,31},{8,16},{9,... | collective-permute-start | bytes 1748 | tf_op jit(solution)/shard_map/ppermute | solution.py:47
  98.4 12.1 %copy-start.1 = (f32[2,128]{1,0:T(2,128)S(1)}, f32[2,128]{1,0:T(2,128)}, u32[]{:S(2)}) copy-start(f32[2,128]{1,0:T(2,128)} %param.5) | copy-start | bytes 3076
  98.6 8.4 %collective-permute-start.5 = (f32[148,2,2,2]{3,0,2,1:T(8,128)S(1)}, f32[148,2,2,2]{3,0,2,1:T(8,128)S(1)}, u32[]{:S(2)}, u32[]{:S(2)}) collective-permute-start(f32[148,2,2,2]{3,0,2,1:T(8,128)S(1)} %get-tuple-element.19), channel_id=1, source_target_pairs={{0,1},{1,2},{2,3},{3,4},{4,5},{5,6},{6,7},{7,8},{8,9},{9,10},{10,1... | collective-permute-start | bytes 14216 | tf_op jit(solution)/shard_map/ppermute | solution.py:58
  103.2 6.6 %collective-permute-start.6 = (f32[148,2,2,2]{3,0,2,1:T(8,128)S(1)}, f32[148,2,2,2]{3,0,2,1:T(8,128)S(1)}, u32[]{:S(2)}, u32[]{:S(2)}) collective-permute-start(f32[148,2,2,2]{3,0,2,1:T(8,128)S(1)} %get-tuple-element.20), channel_id=1, source_target_pairs={{1,0},{2,1},{3,2},{4,3},{5,4},{6,5},{7,6},{8,7},{9,8},{10,9},{11,1... | collective-permute-start | bytes 14216 | tf_op jit(solution)/shard_map/ppermute | solution.py:61

commit v10 on v9

--- a/solution.py
+++ b/solution.py
@@ -82,15 +82,10 @@
     products = jnp.dot(
         payload[: fields + 3], jnp.concatenate(area_parts, axis=0).T, preferred_element_type=jnp.float32
     ).sum(axis=1)
-    count = fields + 1
-    stats = (
-        products[:count]
-        + jnp.pad(products[count : count + 1], (fields, 0))
-        + jnp.pad(products[count + 1 : count + 2], (fields, 0))
-    )
-    stats, area_late = lax.optimization_barrier((stats, cell_area))
+    stats, area_late = lax.optimization_barrier((products, cell_area))
     stats = butterfly_sum(stats, ("lat", "lon"))
-    factor = stats[:fields] / stats[fields]
+    norm_sq = jnp.broadcast_to(stats[None, fields : fields + 3], (fields, 3)).sum(axis=1)
+    factor = stats[:fields] / norm_sq
 
     ring = [payload]
     for _ in range(slot_count // 2):

time: 112 us -> 111 us (level)
  local copies, waits for them, and re-layouts: 3.27 us -> 2.02 us
    add x1 -> x0, other arithmetic: 1.41 us -> none  [on_device_body(): products[:count] + jnp.pad(products[count:count + 1], (fields, 0))]
    slice x2 -> x0, local copies, waits for them, and re-layouts: 1.25 us -> none  [the longest x1 0.66 us: on_device_body(): products[count:count + 1]]
  transfers between devices with their start and end apart: 16 -> 16, of which waited for: 15 -> 15; matrix products, arithmetic and copies ran while one was open for 3% -> 1% of each run, Pallas kernels for 0% -> 0%
where the time goes in v10:
time: 111 us; the launch traced here: 110 us
  starting transfers between devices  73 us (66%)
  waiting for transfers between devices  29.6 us (27%)
  other arithmetic  3.71 us (3%)
  local copies, waits for them, and re-layouts  2.02 us (2%)
  between operations  1.11 us (1%)
    ppermute x9, starting transfers between devices, butterfly_sum(): lax.ppermute(value, axis, [(i, partner_of[i]) for i in range(length)])  34.5 us
    ppermute x4, starting transfers between devices, shifted(): lax.ppermute(value, axis, [(i, (i + by) % length) for i in range(length)])  26.7 us
    ppermute x9, waiting for transfers between devices, butterfly_sum(): lax.ppermute(value, axis, [(i, partner_of[i]) for i in range(length)])  18.4 us
    ppermute x1, starting transfers between devices, on_device_body(): lax.ppermute(offer, 'lon', [(i, i ^ 1) for i in range(lax.axis_size('lon'...  6.89 us
    ppermute x4, waiting for transfers between devices, shifted(): lax.ppermute(value, axis, [(i, (i + by) % length) for i in range(length)])  5.69 us
    ppermute x1, starting transfers between devices, padded_2(): lax.ppermute(lax.slice_in_dim(block, block.shape[dim] - width, None, axis...  4.59 us
    ppermute x1, waiting for transfers between devices, padded_2(): lax.ppermute(lax.slice_in_dim(block, block.shape[dim] - width, None, axis...  2.79 us
    ppermute x1, waiting for transfers between devices, padded_2(): lax.ppermute(lax.slice_in_dim(block, 0, width, axis=dim), axis, backward)  2.77 us
  transfers between devices with their start and end apart: 16, of which 15 were waited for; matrix products, arithmetic and copies ran while one was open for 1% of the time, Pallas kernels for 0%

profile of v10, /device:TPU:1, one launch (start us, length us, event | category | flops | bytes accessed | tf_op | source)
XLA Modules:
  0.0 110.3 jit_solution(11078862292702217207)
XLA Ops:
  0.0 0.0 copy-start
  0.8 0.8 fusion.10
  1.6 0.9 copy.16
  2.6 11.9 %collective-permute-start = (bf16[148,256]{1,0:T(8,128)(2,1)S(1)}, bf16[148,256]{1,0:T(8,128)(2,1)S(1)}, u32[]{:S(2)}, u32[]{:S(2)}) collective-permute-start(bf16[148,256]{1,0:T(8,128)(2,1)S(1)} %concatenate.9), channel_id=1, source_target_pairs={{0,30},{1,31},{2,0},{3,1},{4,2},{5,3},{6,4},{7,5},{8,6},{9,7},{10,... | collective-permute-start | bytes 227336 | tf_op jit(solution)/shard_map/ppermute | solution.py:9
  14.5 1.4 %collective-permute-done = bf16[148,256]{1,0:T(8,128)(2,1)S(1)} collective-permute-done((bf16[148,256]{1,0:T(8,128)(2,1)S(1)}, bf16[148,256]{1,0:T(8,128)(2,1)S(1)}, u32[]{:S(2)}, u32[]{:S(2)}) %collective-permute-start) | collective-permute-done | bytes 75808 | tf_op jit(solution)/shard_map/ppermute | solution.py:9
  16.0 4.9 %collective-permute-start.1 = (bf16[148,256]{1,0:T(8,128)(2,1)S(1)}, bf16[148,256]{1,0:T(8,128)(2,1)S(1)}, u32[]{:S(2)}, u32[]{:S(2)}) collective-permute-start(bf16[148,256]{1,0:T(8,128)(2,1)S(1)} %collective-permute-done), channel_id=1, source_target_pairs={{0,30},{1,31},{2,0},{3,1},{4,2},{5,3},{6,4},{7,5},{8,6},{9,7},{10,... | collective-permute-start | bytes 227336 | tf_op jit(solution)/shard_map/ppermute | solution.py:9
  20.9 1.4 %collective-permute-done.1 = bf16[148,256]{1,0:T(8,128)(2,1)S(1)} collective-permute-done((bf16[148,256]{1,0:T(8,128)(2,1)S(1)}, bf16[148,256]{1,0:T(8,128)(2,1)S(1)}, u32[]{:S(2)}, u32[]{:S(2)}) %collective-permute-start.1) | collective-permute-done | bytes 75808 | tf_op jit(solution)/shard_map/ppermute | solution.py:9
  22.3 4.9 %collective-permute-start.2 = (bf16[148,256]{1,0:T(8,128)(2,1)S(1)}, bf16[148,256]{1,0:T(8,128)(2,1)S(1)}, u32[]{:S(2)}, u32[]{:S(2)}) collective-permute-start(bf16[148,256]{1,0:T(8,128)(2,1)S(1)} %collective-permute-done.1), channel_id=1, source_target_pairs={{0,30},{1,31},{2,0},{3,1},{4,2},{5,3},{6,4},{7,5},{8,6},{9,7},{10,... | collective-permute-start | bytes 227336 | tf_op jit(solution)/shard_map/ppermute | solution.py:9
  27.2 1.4 %collective-permute-done.2 = bf16[148,256]{1,0:T(8,128)(2,1)S(1)} collective-permute-done((bf16[148,256]{1,0:T(8,128)(2,1)S(1)}, bf16[148,256]{1,0:T(8,128)(2,1)S(1)}, u32[]{:S(2)}, u32[]{:S(2)}) %collective-permute-start.2) | collective-permute-done | bytes 75808 | tf_op jit(solution)/shard_map/ppermute | solution.py:9
  28.6 4.9 %collective-permute-start.3 = (bf16[148,256]{1,0:T(8,128)(2,1)S(1)}, bf16[148,256]{1,0:T(8,128)(2,1)S(1)}, u32[]{:S(2)}, u32[]{:S(2)}) collective-permute-start(bf16[148,256]{1,0:T(8,128)(2,1)S(1)} %collective-permute-done.2), channel_id=1, source_target_pairs={{0,30},{1,31},{2,0},{3,1},{4,2},{5,3},{6,4},{7,5},{8,6},{9,7},{10,... | collective-permute-start | bytes 227336 | tf_op jit(solution)/shard_map/ppermute | solution.py:9
  33.6 1.4 %collective-permute-done.3 = bf16[148,256]{1,0:T(8,128)(2,1)S(1)} collective-permute-done((bf16[148,256]{1,0:T(8,128)(2,1)S(1)}, bf16[148,256]{1,0:T(8,128)(2,1)S(1)}, u32[]{:S(2)}, u32[]{:S(2)}) %collective-permute-start.3) | collective-permute-done | bytes 75808 | tf_op jit(solution)/shard_map/ppermute | solution.py:9
  35.1 6.9 %collective-permute-start.4 = (bf16[4,148,256]{2,1,0:T(8,128)(2,1)S(1)}, bf16[4,148,256]{2,1,0:T(8,128)(2,1)S(1)}, u32[]{:S(2)}, u32[]{:S(2)}) collective-permute-start(bf16[4,148,256]{2,1,0:T(8,128)(2,1)S(1)} %pad_maximum_fusion.3), channel_id=1, source_target_pairs={{0,1},{1,0},{2,3},{3,2},{4,5},{5,4},{6,7},{7,6},{8,9},{9,8},{10,11... | collective-permute-start | bytes 909320 | tf_op jit(solution)/shard_map/ppermute | solution.py:97
  42.0 0.1 convolution_reduce_fusion
  42.1 3.1 %collective-permute-start.7 = (f32[147]{0:T(256)S(1)}, f32[147]{0:T(256)S(1)}, u32[]{:S(2)}, u32[]{:S(2)}) collective-permute-start(f32[147]{0:T(256)S(1)} %convolution_reduce_fusion), channel_id=1, source_target_pairs={{0,32},{32,0},{64,96},{96,64},{128,160},{160,128},{192,224},{224,1... | collective-permute-start | bytes 1772 | tf_op jit(solution)/shard_map/ppermute | solution.py:47
  45.2 1.2 %collective-permute-done.7 = f32[147]{0:T(256)S(1)} collective-permute-done((f32[147]{0:T(256)S(1)}, f32[147]{0:T(256)S(1)}, u32[]{:S(2)}, u32[]{:S(2)}) %collective-permute-start.7) | collective-permute-done | bytes 620 | tf_op jit(solution)/shard_map/ppermute | solution.py:47
  46.4 4.4 %collective-permute-start.8 = (f32[147]{0:T(256)S(1)}, f32[147]{0:T(256)S(1)}, u32[]{:S(2)}, u32[]{:S(2)}) collective-permute-start(f32[147]{0:T(256)S(1)} %add.77), channel_id=1, source_target_pairs={{0,96},{32,64},{64,32},{96,0},{128,224},{160,192},{192,160},{224,1... | collective-permute-start | bytes 1772 | tf_op jit(solution)/shard_map/ppermute | solution.py:47
  50.8 1.1 %collective-permute-done.8 = f32[147]{0:T(256)S(1)} collective-permute-done((f32[147]{0:T(256)S(1)}, f32[147]{0:T(256)S(1)}, u32[]{:S(2)}, u32[]{:S(2)}) %collective-permute-start.8) | collective-permute-done | bytes 620 | tf_op jit(solution)/shard_map/ppermute | solution.py:47
  52.0 3.2 %collective-permute-start.9 = (f32[147]{0:T(256)S(1)}, f32[147]{0:T(256)S(1)}, u32[]{:S(2)}, u32[]{:S(2)}) collective-permute-start(f32[147]{0:T(256)S(1)} %add.78), channel_id=1, source_target_pairs={{0,128},{32,160},{64,192},{96,224},{128,0},{160,32},{192,64},{224,... | collective-permute-start | bytes 1772 | tf_op jit(solution)/shard_map/ppermute | solution.py:47
  55.2 1.1 %collective-permute-done.9 = f32[147]{0:T(256)S(1)} collective-permute-done((f32[147]{0:T(256)S(1)}, f32[147]{0:T(256)S(1)}, u32[]{:S(2)}, u32[]{:S(2)}) %collective-permute-start.9) | collective-permute-done | bytes 620 | tf_op jit(solution)/shard_map/ppermute | solution.py:47
  56.3 4.6 %collective-permute-start.10 = (f32[147]{0:T(256)S(1)}, f32[147]{0:T(256)S(1)}, u32[]{:S(2)}, u32[]{:S(2)}) collective-permute-start(f32[147]{0:T(256)S(1)} %add.79), channel_id=1, source_target_pairs={{0,384},{32,416},{64,448},{96,480},{128,256},{160,288},{192,320},{... | collective-permute-start | bytes 1772 | tf_op jit(solution)/shard_map/ppermute | solution.py:47
  60.9 0.9 collective-permute-done.10
  61.9 6.4 %collective-permute-start.11 = (f32[147]{0:T(256)S(1)}, f32[147]{0:T(256)S(1)}, u32[]{:S(2)}, u32[]{:S(2)}) collective-permute-start(f32[147]{0:T(256)S(1)} %add.80), channel_id=1, source_target_pairs={{0,1},{1,0},{2,3},{3,2},{4,5},{5,4},{6,7},{7,6},{8,9},{9,8},{10,11... | collective-permute-start | bytes 1772 | tf_op jit(solution)/shard_map/ppermute | solution.py:47
  68.3 0.8 collective-permute-done.11
  69.1 1.9 %collective-permute-start.12 = (f32[147]{0:T(256)S(1)}, f32[147]{0:T(256)S(1)}, u32[]{:S(2)}, u32[]{:S(2)}) collective-permute-start(f32[147]{0:T(256)S(1)} %add.81), channel_id=1, source_target_pairs={{0,2},{1,3},{2,0},{3,1},{4,6},{5,7},{6,4},{7,5},{8,10},{9,11},{10,... | collective-permute-start | bytes 1772 | tf_op jit(solution)/shard_map/ppermute | solution.py:47
  71.0 2.4 %collective-permute-done.12 = f32[147]{0:T(256)S(1)} collective-permute-done((f32[147]{0:T(256)S(1)}, f32[147]{0:T(256)S(1)}, u32[]{:S(2)}, u32[]{:S(2)}) %collective-permute-start.12) | collective-permute-done | bytes 620 | tf_op jit(solution)/shard_map/ppermute | solution.py:47
  73.4 1.9 %collective-permute-start.13 = (f32[147]{0:T(256)S(1)}, f32[147]{0:T(256)S(1)}, u32[]{:S(2)}, u32[]{:S(2)}) collective-permute-start(f32[147]{0:T(256)S(1)} %add.82), channel_id=1, source_target_pairs={{0,4},{1,5},{2,6},{3,7},{4,0},{5,1},{6,2},{7,3},{8,12},{9,13},{10,... | collective-permute-start | bytes 1772 | tf_op jit(solution)/shard_map/ppermute | solution.py:47
  75.3 3.3 %collective-permute-done.13 = f32[147]{0:T(256)S(1)} collective-permute-done((f32[147]{0:T(256)S(1)}, f32[147]{0:T(256)S(1)}, u32[]{:S(2)}, u32[]{:S(2)}) %collective-permute-start.13) | collective-permute-done | bytes 620 | tf_op jit(solution)/shard_map/ppermute | solution.py:47
  78.6 3.7 %collective-permute-start.14 = (f32[147]{0:T(256)S(1)}, f32[147]{0:T(256)S(1)}, u32[]{:S(2)}, u32[]{:S(2)}) collective-permute-start(f32[147]{0:T(256)S(1)} %add.83), channel_id=1, source_target_pairs={{0,8},{1,9},{2,10},{3,11},{4,12},{5,13},{6,14},{7,15},{8,0},{9,1},... | collective-permute-start | bytes 1772 | tf_op jit(solution)/shard_map/ppermute | solution.py:47
  82.4 4.5 %collective-permute-done.14 = f32[147]{0:T(256)S(1)} collective-permute-done((f32[147]{0:T(256)S(1)}, f32[147]{0:T(256)S(1)}, u32[]{:S(2)}, u32[]{:S(2)}) %collective-permute-start.14) | collective-permute-done | bytes 620 | tf_op jit(solution)/shard_map/ppermute | solution.py:47
  86.9 5.2 %collective-permute-start.15 = (f32[147]{0:T(256)S(1)}, f32[147]{0:T(256)S(1)}, u32[]{:S(2)}, u32[]{:S(2)}) collective-permute-start(f32[147]{0:T(256)S(1)} %add.84), channel_id=1, source_target_pairs={{0,24},{1,25},{2,26},{3,27},{4,28},{5,29},{6,30},{7,31},{8,16},{9,... | collective-permute-start | bytes 1772 | tf_op jit(solution)/shard_map/ppermute | solution.py:47
  92.0 3.0 %collective-permute-done.15 = f32[147]{0:T(256)S(1)} collective-permute-done((f32[147]{0:T(256)S(1)}, f32[147]{0:T(256)S(1)}, u32[]{:S(2)}, u32[]{:S(2)}) %collective-permute-start.15) | collective-permute-done | bytes 620 | tf_op jit(solution)/shard_map/ppermute | solution.py:47
  95.1 0.7 slice_reduce_fusion
  95.8 0.0 collective-permute-done.4
  95.8 0.1 pad_maximum_fusion
  95.9 0.2 compare_reduce_fusion
  96.1 0.1 select_bitcast_fusion
  96.2 0.1 copy.11
  96.4 0.1 copy.14
  96.6 0.0 copy-done
  96.6 0.7 fusion.12
  97.3 0.0 copy-start.1
  97.3 0.2 slice_maximum_fusion
  97.5 4.6 %collective-permute-start.5 = (f32[148,2,2,2]{3,0,2,1:T(8,128)S(1)}, f32[148,2,2,2]{3,0,2,1:T(8,128)S(1)}, u32[]{:S(2)}, u32[]{:S(2)}) collective-permute-start(f32[148,2,2,2]{3,0,2,1:T(8,128)S(1)} %get-tuple-element.19), channel_id=1, source_target_pairs={{0,1},{1,2},{2,3},{3,4},{4,5},{5,6},{6,7},{7,8},{8,9},{9,10},{10,1... | collective-permute-start | bytes 14216 | tf_op jit(solution)/shard_map/ppermute | solution.py:58
  102.1 0.4 collective-permute-start.6
  102.5 0.6 slice_divide_fusion
  103.1 2.8 %collective-permute-done.5 = f32[148,2,2,2]{3,0,2,1:T(8,128)S(1)} collective-permute-done((f32[148,2,2,2]{3,0,2,1:T(8,128)S(1)}, f32[148,2,2,2]{3,0,2,1:T(8,128)S(1)}, u32[]{:S(2)}, u32[]{:S(2)}) %collective-permute-start.5) | collective-permute-done | bytes 4768 | tf_op jit(solution)/shard_map/ppermute | solution.py:58
  105.9 2.8 %collective-permute-done.6 = f32[148,2,2,2]{3,0,2,1:T(8,128)S(1)} collective-permute-done((f32[148,2,2,2]{3,0,2,1:T(8,128)S(1)}, f32[148,2,2,2]{3,0,2,1:T(8,128)S(1)}, u32[]{:S(2)}, u32[]{:S(2)}) %collective-permute-start.6) | collective-permute-done | bytes 4768 | tf_op jit(solution)/shard_map/ppermute | solution.py:61
  108.7 0.3 pad_maximum_fusion.1
  109.1 0.4 fusion.1
  109.4 0.0 copy-done.1
  109.4 0.1 slice_add_fusion.2
  109.5 0.7 copy.12
  (20 shorter events, 0.3 us)
Async XLA Ops:
  0.0 96.6 %copy-start = (bf16[1,1,8,256,768]{4,3,2,1,0:T(8,128)(2,1)S(1)}, bf16[1,1,8,256,768]{4,3,2,1,0:T(8,128)(2,1)}, u32[]{:S(2)}) copy-start(bf16[1,1,8,256,768]{4,3,2,1,0:T(8,128)(2,1)} %param.7) | copy-start | bytes 9437188
  2.6 13.4 %collective-permute-start = (bf16[148,256]{1,0:T(8,128)(2,1)S(1)}, bf16[148,256]{1,0:T(8,128)(2,1)S(1)}, u32[]{:S(2)}, u32[]{:S(2)}) collective-permute-start(bf16[148,256]{1,0:T(8,128)(2,1)S(1)} %concatenate.9), channel_id=1, source_target_pairs={{0,30},{1,31},{2,0},{3,1},{4,2},{5,3},{6,4},{7,5},{8,6},{9,7},{10,... | collective-permute-start | bytes 227336 | tf_op jit(solution)/shard_map/ppermute | solution.py:9
  16.0 6.3 %collective-permute-start.1 = (bf16[148,256]{1,0:T(8,128)(2,1)S(1)}, bf16[148,256]{1,0:T(8,128)(2,1)S(1)}, u32[]{:S(2)}, u32[]{:S(2)}) collective-permute-start(bf16[148,256]{1,0:T(8,128)(2,1)S(1)} %collective-permute-done), channel_id=1, source_target_pairs={{0,30},{1,31},{2,0},{3,1},{4,2},{5,3},{6,4},{7,5},{8,6},{9,7},{10,... | collective-permute-start | bytes 227336 | tf_op jit(solution)/shard_map/ppermute | solution.py:9
  22.3 6.3 %collective-permute-start.2 = (bf16[148,256]{1,0:T(8,128)(2,1)S(1)}, bf16[148,256]{1,0:T(8,128)(2,1)S(1)}, u32[]{:S(2)}, u32[]{:S(2)}) collective-permute-start(bf16[148,256]{1,0:T(8,128)(2,1)S(1)} %collective-permute-done.1), channel_id=1, source_target_pairs={{0,30},{1,31},{2,0},{3,1},{4,2},{5,3},{6,4},{7,5},{8,6},{9,7},{10,... | collective-permute-start | bytes 227336 | tf_op jit(solution)/shard_map/ppermute | solution.py:9
  28.6 6.3 %collective-permute-start.3 = (bf16[148,256]{1,0:T(8,128)(2,1)S(1)}, bf16[148,256]{1,0:T(8,128)(2,1)S(1)}, u32[]{:S(2)}, u32[]{:S(2)}) collective-permute-start(bf16[148,256]{1,0:T(8,128)(2,1)S(1)} %collective-permute-done.2), channel_id=1, source_target_pairs={{0,30},{1,31},{2,0},{3,1},{4,2},{5,3},{6,4},{7,5},{8,6},{9,7},{10,... | collective-permute-start | bytes 227336 | tf_op jit(solution)/shard_map/ppermute | solution.py:9
  35.1 60.7 %collective-permute-start.4 = (bf16[4,148,256]{2,1,0:T(8,128)(2,1)S(1)}, bf16[4,148,256]{2,1,0:T(8,128)(2,1)S(1)}, u32[]{:S(2)}, u32[]{:S(2)}) collective-permute-start(bf16[4,148,256]{2,1,0:T(8,128)(2,1)S(1)} %pad_maximum_fusion.3), channel_id=1, source_target_pairs={{0,1},{1,0},{2,3},{3,2},{4,5},{5,4},{6,7},{7,6},{8,9},{9,8},{10,11... | collective-permute-start | bytes 909320 | tf_op jit(solution)/shard_map/ppermute | solution.py:97
  42.1 4.3 %collective-permute-start.7 = (f32[147]{0:T(256)S(1)}, f32[147]{0:T(256)S(1)}, u32[]{:S(2)}, u32[]{:S(2)}) collective-permute-start(f32[147]{0:T(256)S(1)} %convolution_reduce_fusion), channel_id=1, source_target_pairs={{0,32},{32,0},{64,96},{96,64},{128,160},{160,128},{192,224},{224,1... | collective-permute-start | bytes 1772 | tf_op jit(solution)/shard_map/ppermute | solution.py:47
  46.4 5.5 %collective-permute-start.8 = (f32[147]{0:T(256)S(1)}, f32[147]{0:T(256)S(1)}, u32[]{:S(2)}, u32[]{:S(2)}) collective-permute-start(f32[147]{0:T(256)S(1)} %add.77), channel_id=1, source_target_pairs={{0,96},{32,64},{64,32},{96,0},{128,224},{160,192},{192,160},{224,1... | collective-permute-start | bytes 1772 | tf_op jit(solution)/shard_map/ppermute | solution.py:47
  52.0 4.3 %collective-permute-start.9 = (f32[147]{0:T(256)S(1)}, f32[147]{0:T(256)S(1)}, u32[]{:S(2)}, u32[]{:S(2)}) collective-permute-start(f32[147]{0:T(256)S(1)} %add.78), channel_id=1, source_target_pairs={{0,128},{32,160},{64,192},{96,224},{128,0},{160,32},{192,64},{224,... | collective-permute-start | bytes 1772 | tf_op jit(solution)/shard_map/ppermute | solution.py:47
  56.3 5.6 %collective-permute-start.10 = (f32[147]{0:T(256)S(1)}, f32[147]{0:T(256)S(1)}, u32[]{:S(2)}, u32[]{:S(2)}) collective-permute-start(f32[147]{0:T(256)S(1)} %add.79), channel_id=1, source_target_pairs={{0,384},{32,416},{64,448},{96,480},{128,256},{160,288},{192,320},{... | collective-permute-start | bytes 1772 | tf_op jit(solution)/shard_map/ppermute | solution.py:47
  61.9 7.2 %collective-permute-start.11 = (f32[147]{0:T(256)S(1)}, f32[147]{0:T(256)S(1)}, u32[]{:S(2)}, u32[]{:S(2)}) collective-permute-start(f32[147]{0:T(256)S(1)} %add.80), channel_id=1, source_target_pairs={{0,1},{1,0},{2,3},{3,2},{4,5},{5,4},{6,7},{7,6},{8,9},{9,8},{10,11... | collective-permute-start | bytes 1772 | tf_op jit(solution)/shard_map/ppermute | solution.py:47
  69.1 4.3 %collective-permute-start.12 = (f32[147]{0:T(256)S(1)}, f32[147]{0:T(256)S(1)}, u32[]{:S(2)}, u32[]{:S(2)}) collective-permute-start(f32[147]{0:T(256)S(1)} %add.81), channel_id=1, source_target_pairs={{0,2},{1,3},{2,0},{3,1},{4,6},{5,7},{6,4},{7,5},{8,10},{9,11},{10,... | collective-permute-start | bytes 1772 | tf_op jit(solution)/shard_map/ppermute | solution.py:47
  73.4 5.2 %collective-permute-start.13 = (f32[147]{0:T(256)S(1)}, f32[147]{0:T(256)S(1)}, u32[]{:S(2)}, u32[]{:S(2)}) collective-permute-start(f32[147]{0:T(256)S(1)} %add.82), channel_id=1, source_target_pairs={{0,4},{1,5},{2,6},{3,7},{4,0},{5,1},{6,2},{7,3},{8,12},{9,13},{10,... | collective-permute-start | bytes 1772 | tf_op jit(solution)/shard_map/ppermute | solution.py:47
  78.6 8.2 %collective-permute-start.14 = (f32[147]{0:T(256)S(1)}, f32[147]{0:T(256)S(1)}, u32[]{:S(2)}, u32[]{:S(2)}) collective-permute-start(f32[147]{0:T(256)S(1)} %add.83), channel_id=1, source_target_pairs={{0,8},{1,9},{2,10},{3,11},{4,12},{5,13},{6,14},{7,15},{8,0},{9,1},... | collective-permute-start | bytes 1772 | tf_op jit(solution)/shard_map/ppermute | solution.py:47
  86.9 8.2 %collective-permute-start.15 = (f32[147]{0:T(256)S(1)}, f32[147]{0:T(256)S(1)}, u32[]{:S(2)}, u32[]{:S(2)}) collective-permute-start(f32[147]{0:T(256)S(1)} %add.84), channel_id=1, source_target_pairs={{0,24},{1,25},{2,26},{3,27},{4,28},{5,29},{6,30},{7,31},{8,16},{9,... | collective-permute-start | bytes 1772 | tf_op jit(solution)/shard_map/ppermute | solution.py:47
  97.3 12.1 %copy-start.1 = (f32[2,128]{1,0:T(2,128)S(1)}, f32[2,128]{1,0:T(2,128)}, u32[]{:S(2)}) copy-start(f32[2,128]{1,0:T(2,128)} %param.5) | copy-start | bytes 3076
  97.5 8.4 %collective-permute-start.5 = (f32[148,2,2,2]{3,0,2,1:T(8,128)S(1)}, f32[148,2,2,2]{3,0,2,1:T(8,128)S(1)}, u32[]{:S(2)}, u32[]{:S(2)}) collective-permute-start(f32[148,2,2,2]{3,0,2,1:T(8,128)S(1)} %get-tuple-element.19), channel_id=1, source_target_pairs={{0,1},{1,2},{2,3},{3,4},{4,5},{5,6},{6,7},{7,8},{8,9},{9,10},{10,1... | collective-permute-start | bytes 14216 | tf_op jit(solution)/shard_map/ppermute | solution.py:58
  102.1 6.6 %collective-permute-start.6 = (f32[148,2,2,2]{3,0,2,1:T(8,128)S(1)}, f32[148,2,2,2]{3,0,2,1:T(8,128)S(1)}, u32[]{:S(2)}, u32[]{:S(2)}) collective-permute-start(f32[148,2,2,2]{3,0,2,1:T(8,128)S(1)} %get-tuple-element.20), channel_id=1, source_target_pairs={{1,0},{2,1},{3,2},{4,3},{5,4},{6,5},{7,6},{8,7},{9,8},{10,9},{11,1... | collective-permute-start | bytes 14216 | tf_op jit(solution)/shard_map/ppermute | solution.py:61
